TPU v7x, 128 devices: a whole 4x4x4 slice. The times are simulated.
128 devices in a mesh: half: 2 (over core), row: 8 (over z_hi, x), col: 8 (over y, z_lo).
Axes of the slice: x: 4, y: 4, z: 4 (z_hi: 2, z_lo: 2; z = z_hi * 2 + z_lo), core: 2. Of those that a mesh axis runs over, the one named last changes fastest.
Arguments:
- child_diag: float32 [2, 512, 512], P('half'), as said below
- child_panel: float32 [2, 16, 8, 128, 512], P('half', None, 'row'), may hold values from -18 to 18
- child_window: float32 [2, 16, 8, 128, 8, 8, 128], P('half', None, 'row', None, None, 'col'), may hold values from -6 to 6
- parent_diag: float32 [512, 512], replicated
- parent_lead_panel: float32 [24, 8, 2, 8, 8, 512], P(None, 'row', 'half', 'col'), may hold values from -24 to 24
- index_maps: int32 [2, 128], replicated, may hold values from 0 to 191, as said below
Outputs:
- parent_front: float32 [24, 8, 128, 4, 2, 8, 128], P(None, 'row', None, None, 'half', 'col')
- parent_factor: float32 [24, 8, 2, 8, 8, 512], P(None, 'row', 'half', 'col')
- parent_pivot: float32 [512, 512], replicated
Inputs may be any that keep to these rules, and one draw needn't show every extreme that they name: child_diag and parent_diag are symmetric and positive definite. For each child k and each group a, the entries index_maps[k, a * 16 + u] with 0 <= u < 16 equal q * 16 + ((u + s) mod 16) for a group target q and a turn s fixed within the group; groups a < 4 have q = a, later groups have distinct q that rise with a; over the 8 groups of a child the turns s, taken modulo 8, are all different; for each child some group a < 4 has a turn divisible by 8, and another group a < 4 has a turn that leaves 1 modulo 8.
All inputs are finite; a program needn't handle non-finite values.
Results may differ from a plain program's by a relative error of at most 0.0001.
Values sent between devices are 32-bit elements; how exact they have to be, the bound alone decides.
No kernel may reach another device: no remote copies, remote signals or barrier semaphores. Data moves between devices by JAX's collectives and lax.ppermute only.
A program may use at most 192 MiB of HBM per device.

v0:
```python
import jax
import jax.numpy as jnp
from jax import lax
from jax.sharding import PartitionSpec as P

BLOCK_EXTENT = 128
PB = 4
SB = 128
RB = 192
WB = 64


def from_root(shard, axis, root):
    mine = lax.axis_index(axis) == root
    return lax.psum(jnp.where(mine, shard, jnp.zeros_like(shard)), axis)


def pick_ranked(owners, values, wanted, slot_count, missing):
    matches = owners[..., None, :] == wanted[:, None]
    ranking = jnp.cumsum(matches.astype(jnp.int32), axis=-1) - 1
    slot_ids = jnp.arange(slot_count, dtype=jnp.int32)
    chosen = matches[..., None, :] & (ranking[..., None, :] == slot_ids[:, None])
    present = jnp.any(chosen, axis=-1)
    picked = jnp.sum(jnp.where(chosen, values[..., None, None, :], 0), axis=-1)
    return jnp.where(present, picked, missing)


def _dot_t(x, y):
    return lax.dot_general(x, y, (((1,), (1,)), ((), ())), precision=lax.Precision.HIGHEST)


def _dot(x, y):
    return jnp.dot(x, y, precision=lax.Precision.HIGHEST)


def factor_and_inverse(spd, leaf):
    order = spd.shape[0]
    blocks = order // leaf
    work = spd
    columns = []
    inverses = []
    eye = jnp.eye(leaf, dtype=spd.dtype)
    for k in range(blocks):
        low = jnp.linalg.cholesky(work[:leaf, :leaf])
        inv = lax.linalg.triangular_solve(low, eye, left_side=True, lower=True)
        inverses.append(inv)
        if k < blocks - 1:
            below = _dot_t(work[leaf:, :leaf], inv)
            work = work[leaf:, leaf:] - _dot_t(below, below)
            columns.append(jnp.concatenate([low, below], axis=0))
        else:
            columns.append(low)
    lower = jnp.concatenate(
        [jnp.pad(c, ((order - c.shape[0], 0), (0, 0))) for c in columns], axis=1
    )
    size = leaf
    while len(inverses) > 1:
        merged = []
        for t in range(0, len(inverses), 2):
            start = t * size
            first, second = inverses[t], inverses[t + 1]
            coupling = lower[start + size : start + 2 * size, start : start + size]
            corner = -_dot(second, _dot(coupling, first))
            top = jnp.concatenate([first, jnp.zeros_like(first)], axis=1)
            bottom = jnp.concatenate([corner, second], axis=1)
            merged.append(jnp.concatenate([top, bottom], axis=0))
        inverses = merged
        size *= 2
    return lower, inverses[0]


def per_device(child_diag, child_panel, child_window, parent_diag, parent_lead_panel, index_maps):
    highest = lax.Precision.HIGHEST
    row_size = lax.axis_size("row")
    col_size = lax.axis_size("col")
    half_id = lax.axis_index("half")
    row_id = lax.axis_index("row")
    col_id = lax.axis_index("col")
    panel_width = PB * BLOCK_EXTENT
    group_size = 2 * row_size
    row_local = SB // row_size
    col_local = WB // row_size
    parent_row_blocks = RB // row_size
    parent_cols = WB // group_size
    per_row = 2 * (SB // group_size) // row_size
    per_col = (WB // group_size + row_size - 1) // row_size
    transpose_perm = [(i * col_size + j, j * row_size + i) for i in range(row_size) for j in range(col_size)]
    child_lead = child_panel[0, :col_local, 0]
    child_col_rows = lax.ppermute(child_lead, ("row", "col"), transpose_perm)
    sub_rows = parent_lead_panel.shape[4]
    own_rows = parent_lead_panel.reshape(-1, panel_width)
    gathered = lax.all_gather(
        parent_lead_panel.reshape(parent_row_blocks, sub_rows, panel_width),
        ("half", "col"),
        axis=1,
        tiled=True,
    )
    paired = gathered[: 2 * parent_cols].reshape(parent_cols, 2, BLOCK_EXTENT, panel_width)
    offered = lax.dynamic_index_in_dim(paired, half_id, axis=1, keepdims=False)
    parent_col_rows = lax.ppermute(offered, ("row", "col"), transpose_perm)
    child_low, child_inv = factor_and_inverse(child_diag[0], BLOCK_EXTENT)
    child_rows = child_panel.reshape(-1, panel_width)
    dims = (((1,), (1,)), ((), ()))
    child_factor = lax.dot_general(child_rows, child_inv, dims, precision=highest)
    child_columns = lax.dot_general(
        child_col_rows.reshape(-1, panel_width), child_inv, dims, precision=highest
    )
    schur_part = child_window.reshape(row_local * BLOCK_EXTENT, col_local * BLOCK_EXTENT) - lax.dot_general(
        child_factor, child_columns, dims, precision=highest
    )
    schur_blocks = schur_part.reshape(row_local, BLOCK_EXTENT, col_local, BLOCK_EXTENT)
    child_map = lax.dynamic_index_in_dim(index_maps, half_id, axis=0, keepdims=False)
    my_rows = lax.dynamic_index_in_dim(
        child_map.reshape(row_local, row_size), row_id, axis=1, keepdims=False
    )
    my_cols = lax.dynamic_index_in_dim(
        child_map[:WB].reshape(col_local, row_size), col_id, axis=1, keepdims=False
    )
    local_rows = jnp.arange(row_local, dtype=jnp.int32)
    local_cols = jnp.arange(col_local, dtype=jnp.int32)
    send_rows = pick_ranked(
        my_rows % row_size, local_rows, jnp.arange(row_size, dtype=jnp.int32), per_row, row_local
    )
    send_cols = pick_ranked(
        my_cols % group_size,
        local_cols,
        jnp.arange(group_size, dtype=jnp.int32),
        per_col,
        col_local,
    )
    all_rows = index_maps.reshape(2, row_local, row_size).transpose(0, 2, 1)
    row_target = pick_ranked(
        all_rows % row_size, all_rows // row_size, row_id[None], per_row, parent_row_blocks
    )[:, :, 0, :]
    all_cols = index_maps[:, :WB].reshape(2, col_local, row_size).transpose(0, 2, 1)
    col_target = pick_ranked(
        all_cols % group_size,
        all_cols // group_size,
        (half_id * row_size + col_id)[None],
        per_col,
        parent_cols,
    )[:, :, 0, :]
    send_row_index = jnp.minimum(send_rows, row_local - 1)[None, :, None, :, None]
    send_col_index = jnp.minimum(send_cols, col_local - 1).reshape(2, row_size, per_col)[:, None, :, None, :]
    outgoing = schur_blocks[send_row_index, :, send_col_index, :]
    outgoing, gathered, parent_col_rows, parent_diag = lax.optimization_barrier(
        (outgoing, gathered, parent_col_rows, parent_diag)
    )
    pivot_lower_factor, parent_inv = factor_and_inverse(parent_diag, BLOCK_EXTENT)
    solved = lax.dot_general(own_rows, parent_inv, dims, precision=highest)
    parent_factor = solved.reshape(parent_lead_panel.shape)
    row_factor = lax.dot_general(gathered.reshape(-1, panel_width), parent_inv, dims, precision=highest)
    column_factor = lax.dot_general(
        parent_col_rows.reshape(-1, panel_width), parent_inv, dims, precision=highest
    )
    update = lax.dot_general(row_factor, column_factor, dims, precision=highest)
    arrived = lax.all_to_all(
        outgoing.reshape(-1, per_row * per_col, BLOCK_EXTENT, BLOCK_EXTENT),
        ("half", "row", "col"),
        split_axis=0,
        concat_axis=0,
        tiled=True,
    )
    slot_shape = (2, row_size, row_size, per_row, per_col)
    slot_rows = jnp.broadcast_to(row_target[:, :, None, :, None], slot_shape).reshape(2, -1)
    slot_cols = jnp.broadcast_to(col_target[:, None, :, None, :], slot_shape).reshape(2, -1)
    slots = slot_rows.shape[1]
    match = (slot_rows[:, None, None, :] == jnp.arange(parent_row_blocks, dtype=jnp.int32)[None, :, None, None]) & (
        slot_cols[:, None, None, :] == jnp.arange(parent_cols, dtype=jnp.int32)[None, None, :, None]
    )
    slot_of = jnp.sum(jnp.where(match, jnp.arange(slots, dtype=jnp.int32), 0), axis=-1)
    present = jnp.any(match, axis=-1)
    flat_arrived = arrived.reshape(2, slots, BLOCK_EXTENT, BLOCK_EXTENT)
    first = jnp.take(flat_arrived[0], slot_of[0].reshape(-1), axis=0, mode="clip")
    second = jnp.take(flat_arrived[1], slot_of[1].reshape(-1), axis=0, mode="clip")
    block_shape = (parent_row_blocks, parent_cols, BLOCK_EXTENT, BLOCK_EXTENT)
    assembled = jnp.where(present[0, :, :, None, None], first.reshape(block_shape), 0.0) + jnp.where(
        present[1, :, :, None, None], second.reshape(block_shape), 0.0
    )
    updated = assembled.transpose(0, 2, 1, 3) - update.reshape(
        parent_row_blocks, BLOCK_EXTENT, parent_cols, BLOCK_EXTENT
    )
    return (
        updated.reshape(parent_row_blocks, 1, BLOCK_EXTENT, parent_cols, 1, 1, BLOCK_EXTENT),
        parent_factor,
        pivot_lower_factor,
    )


def solution(mesh):
    in_specs = (
        P("half", None, None),
        P("half", None, "row", None, None),
        P("half", None, "row", None, None, "col", None),
        P(),
        P(None, "row", "half", "col", None, None),
        P(),
    )
    out_specs = (
        P(None, "row", None, None, "half", "col", None),
        P(None, "row", "half", "col", None, None),
        P(),
    )
    return jax.shard_map(
        per_device, mesh=mesh, in_specs=in_specs, out_specs=out_specs, check_vma=False
    )
```

profile of v0, /device:TPU:10, one launch (start us, length us, event | category | flops | bytes accessed | tf_op | source)
XLA Modules:
  0.0 537.1 jit_solution(8305995273545225109)
XLA Ops:
  20.3 11.7 %cholesky.134 = f32[128,128]{1,0:T(8,128)S(1)} custom-call(f32[128,128]{1,0:T(8,128)S(1)} %fusion.69), custom_call_target="Cholesky" | custom-call | tf_op jit(solution)/shard_map/jit(cholesky)/cholesky | solution.py:44
  33.4 9.8 %custom-call.14 = f32[1,128,128]{1,2,0:T(8,128)S(1)} custom-call(f32[1,128,128]{2,1,0:T(8,128)S(1)} %get-tuple-element.45), custom_call_target="InvertDiagBlocksLowerTriangular" | custom-call | tf_op jit(solution)/shard_map/triangular_solve/custom-call.0 | solution.py:45
  44.6 11.7 %cholesky.145 = f32[128,128]{1,0:T(8,128)S(1)} custom-call(f32[128,128]{1,0:T(8,128)S(1)} %fusion.67), custom_call_target="Cholesky" | custom-call | tf_op jit(solution)/shard_map/jit(cholesky)/cholesky | solution.py:44
  57.6 10.0 %custom-call.15 = f32[1,128,128]{1,2,0:T(8,128)S(1)} custom-call(f32[1,128,128]{2,1,0:T(8,128)S(1)} %get-tuple-element.43), custom_call_target="InvertDiagBlocksLowerTriangular" | custom-call | tf_op jit(solution)/shard_map/triangular_solve/custom-call.0 | solution.py:45
  68.9 11.7 %cholesky.156 = f32[128,128]{1,0:T(8,128)S(1)} custom-call(f32[128,128]{1,0:T(8,128)S(1)} %fusion.65), custom_call_target="Cholesky" | custom-call | tf_op jit(solution)/shard_map/jit(cholesky)/cholesky | solution.py:44
  81.9 9.8 %custom-call.16 = f32[1,128,128]{1,2,0:T(8,128)S(1)} custom-call(f32[1,128,128]{2,1,0:T(8,128)S(1)} %fusion.44), custom_call_target="InvertDiagBlocksLowerTriangular" | custom-call | tf_op jit(solution)/shard_map/triangular_solve/custom-call.0 | solution.py:45
  92.7 21.3 %cholesky.167 = f32[128,128]{1,0:T(8,128)S(1)} custom-call(f32[128,128]{1,0:T(8,128)S(1)} %fusion.63), custom_call_target="Cholesky" | custom-call | tf_op jit(solution)/shard_map/jit(cholesky)/cholesky | solution.py:44
  115.3 9.8 %custom-call.17 = f32[1,128,128]{1,2,0:T(8,128)S(1)} custom-call(f32[1,128,128]{2,1,0:T(8,128)S(1)} %fusion.45), custom_call_target="InvertDiagBlocksLowerTriangular" | custom-call | tf_op jit(solution)/shard_map/triangular_solve/custom-call.0 | solution.py:45
  128.8 10.1 %fusion.3 = f32[512,2048]{1,0:T(8,128)} fusion(f32[2048,512]{1,0:T(8,128)} %bitcast.243, f32[256,256]{1,0:T(8,128)S(1)} %select_maximum_fusion.9, f32[128,128]{1,0:T(8,128)S(1)} %copy.131, f32[128,128]{1,0:T(8,128)S(1)} %convolution_negate_fusion.4, f32[128,256]{1,0:T(8,128)S(1)} %concatenate.86, f32[256,256]{1,0:T(8,128)S(1)} %convolution_negate_fusion.1), kind=kOutput, calls=%fused_computation.28 | convolution fusion | flops 6444023808 | bytes 9175040 | tf_op jit(solution)/shard_map/dot_general | solution.py:104
  155.2 19.4 %fusion = f32[256,8,8,128]{3,1,2,0:T(8,128)S(1)} fusion(f32[256,8,8,128]{3,2,1,0:T(8,128)} %bitcast.242, f32[512,2048]{1,0:T(8,128)S(1)} %copy-done, f32[512,1024]{1,0:T(8,128)S(1)} %fusion.2), kind=kOutput, calls=%fused_computation.4 | convolution fusion | flops 12886999040 | bytes 23068672 | tf_op jit(solution)/shard_map/dot_general | solution.py:108
  181.4 16.2 %gather_fusion = f32[256,128,128]{2,1,0:T(8,128)} fusion(f32[16,128,8,128]{3,1,2,0:T(8,128)} %copy.137, s32[256]{0:T(256)S(1)} %reshape.454), kind=kCustom, calls=%fused_computation | custom fusion | bytes 33556480 | tf_op jit(solution)/shard_map/gather | solution.py:145
  198.6 14.6 %all-to-all-start = ((f32[128,2,128,128]{3,2,1,0:T(8,128)}), f32[128,2,128,128]{3,2,1,0:T(8,128)}, u32[]{:S(2)}, u32[]{:S(2)}) async-start(f32[128,2,128,128]{3,2,1,0:T(8,128)} %bitcast.233), calls=%async_computation | async-start | bytes 33554432 | tf_op jit(solution)/shard_map/all_to_all | solution.py:157
  216.3 11.7 %cholesky.178 = f32[128,128]{1,0:T(8,128)S(1)} custom-call(f32[128,128]{1,0:T(8,128)S(1)} %fusion.61), custom_call_target="Cholesky" | custom-call | tf_op jit(solution)/shard_map/jit(cholesky)/cholesky | solution.py:44
  229.4 9.8 %custom-call.18 = f32[1,128,128]{1,2,0:T(8,128)S(1)} custom-call(f32[1,128,128]{2,1,0:T(8,128)S(1)} %get-tuple-element.37), custom_call_target="InvertDiagBlocksLowerTriangular" | custom-call | tf_op jit(solution)/shard_map/triangular_solve/custom-call.0 | solution.py:45
  243.2 12.1 %cholesky.189 = f32[128,128]{1,0:T(8,128)S(1)} custom-call(f32[128,128]{1,0:T(8,128)S(1)} %fusion.59), custom_call_target="Cholesky" | custom-call | tf_op jit(solution)/shard_map/jit(cholesky)/cholesky | solution.py:44
  256.6 9.8 %custom-call.19 = f32[1,128,128]{1,2,0:T(8,128)S(1)} custom-call(f32[1,128,128]{2,1,0:T(8,128)S(1)} %get-tuple-element.35), custom_call_target="InvertDiagBlocksLowerTriangular" | custom-call | tf_op jit(solution)/shard_map/triangular_solve/custom-call.0 | solution.py:45
  269.6 11.7 %cholesky.200 = f32[128,128]{1,0:T(8,128)S(1)} custom-call(f32[128,128]{1,0:T(8,128)S(1)} %fusion.57), custom_call_target="Cholesky" | custom-call | tf_op jit(solution)/shard_map/jit(cholesky)/cholesky | solution.py:44
  283.3 9.8 %custom-call.20 = f32[1,128,128]{1,2,0:T(8,128)S(1)} custom-call(f32[1,128,128]{2,1,0:T(8,128)S(1)} %get-tuple-element.33), custom_call_target="InvertDiagBlocksLowerTriangular" | custom-call | tf_op jit(solution)/shard_map/triangular_solve/custom-call.0 | solution.py:45
  294.1 11.9 %cholesky.211 = f32[128,128]{1,0:T(8,128)S(1)} custom-call(f32[128,128]{1,0:T(8,128)S(1)} %fusion.55), custom_call_target="Cholesky" | custom-call | tf_op jit(solution)/shard_map/jit(cholesky)/cholesky | solution.py:44
  307.9 9.8 %custom-call.21 = f32[1,128,128]{1,2,0:T(8,128)S(1)} custom-call(f32[1,128,128]{2,1,0:T(8,128)S(1)} %get-tuple-element.31), custom_call_target="InvertDiagBlocksLowerTriangular" | custom-call | tf_op jit(solution)/shard_map/triangular_solve/custom-call.0 | solution.py:45
  325.0 11.3 %fusion.106 = f32[3072,512]{1,0:T(8,128)S(1)} fusion(f32[3072,512]{1,0:T(8,128)S(1)} %bitcast.241, f32[256,256]{1,0:T(8,128)S(1)} %select_maximum_fusion.7, f32[128,128]{1,0:T(8,128)S(1)} %copy.153, f32[128,128]{1,0:T(8,128)S(1)} %convolution_negate_fusion.2, f32[128,256]{1,0:T(8,128)S(1)} %concatenate.99, f32[256,256]{1,0:T(8,128)S(1)} %convolution_negate_fusion), kind=kOutput, calls=%fused_computation.235 | convolution fusion | flops 9665249280 | bytes 13369344 | tf_op jit(solution)/shard_map/dot_general | solution.py:152
  336.3 12.1 %fusion.119 = f32[3072,512]{1,0:T(8,128)} fusion(f32[3072,512]{1,0:T(8,128)S(1)} %fusion.106, f32[512,512]{1,0:T(8,128)S(1)} %fusion.105), kind=kOutput, calls=%fused_computation.243 | convolution fusion | flops 9663676416 | bytes 13631488 | tf_op jit(solution)/shard_map/dot_general | solution.py:156
  359.1 131.0 %all-to-all-done = f32[128,2,128,128]{3,2,1,0:T(8,128)} async-done(((f32[128,2,128,128]{3,2,1,0:T(8,128)}), f32[128,2,128,128]{3,2,1,0:T(8,128)}, u32[]{:S(2)}, u32[]{:S(2)}) %all-to-all-start) | async-done | bytes 16777248 | tf_op jit(solution)/shard_map/all_to_all | solution.py:157
  490.1 10.8 %fusion.115 = (f32[64,2,128,128]{3,2,1,0:T(8,128)}, f32[64,2,128,128]{3,2,1,0:T(8,128)}) fusion(f32[128,2,128,128]{3,2,1,0:T(8,128)} %all-to-all-done), kind=kLoop, calls=%fused_computation.239 | loop fusion | bytes 33554432 | tf_op jit(solution)/shard_map/slice | solution.py:174
  (201 shorter events, 113.6 us)
Async XLA Ops:
  7.2 133.2 %all-gather.3.cloned.1.call-start = ((), (), s32[]{:S(2)}) async-start(), calls=%async_computation.1 | async-start | bytes 6684672 | tf_op jit(solution)/shard_map/all_gather | solution.py:92
  11.0 139.0 %collective-permute-start = (f32[8,128,512]{2,1,0:T(8,128)}, f32[8,128,512]{2,1,0:T(8,128)}, u32[]{:S(2)}, u32[]{:S(2)}) collective-permute-start(f32[8,128,512]{2,1,0:T(8,128)} %slice_bitcast_fusion), channel_id=1, source_target_pairs={{0,0},{1,8},{2,16},{3,24},{4,32},{5,40},{6,48},{7,56},{8,1},{9,9},... | collective-permute-start | bytes 6291464 | tf_op jit(solution)/shard_map/ppermute | solution.py:89
  140.4 14.8 %copy-start = (f32[512,2048]{1,0:T(8,128)S(1)}, f32[512,2048]{1,0:T(8,128)}, u32[]{:S(2)}) copy-start(f32[512,2048]{1,0:T(8,128)} %fusion.3) | copy-start | bytes 12582916
  142.4 55.2 %collective-permute-start.1 = (f32[4,128,512]{2,1,0:T(8,128)S(1)}, f32[4,128,512]{2,1,0:T(8,128)S(1)}, u32[]{:S(2)}, u32[]{:S(2)}) collective-permute-start(f32[4,128,512]{2,1,0:T(8,128)S(1)} %dynamic-slice_bitcast_fusion), channel_id=1, source_target_pairs={{0,0},{1,8},{2,16},{3,24},{4,32},{5,40},{6,48},{7,56},{8,1},{9,9},... | collective-permute-start | bytes 3145736 | tf_op jit(solution)/shard_map/ppermute | solution.py:100
  197.6 1.0 copy-start.9
  197.6 15.6 %copy-start.8 = (s32[2,128]{1,0:T(2,128)S(1)}, s32[2,128]{1,0:T(2,128)}, u32[]{:S(2)}) copy-start(s32[2,128]{1,0:T(2,128)} %param.14) | copy-start | bytes 3076
  197.6 18.2 %copy-start.2 = (f32[512,512]{1,0:T(8,128)S(1)}, f32[512,512]{1,0:T(8,128)}, u32[]{:S(2)}) copy-start(f32[512,512]{1,0:T(8,128)} %param.12) | copy-start | bytes 3145732
  198.6 291.5 %all-to-all-start = ((f32[128,2,128,128]{3,2,1,0:T(8,128)}), f32[128,2,128,128]{3,2,1,0:T(8,128)}, u32[]{:S(2)}, u32[]{:S(2)}) async-start(f32[128,2,128,128]{3,2,1,0:T(8,128)} %bitcast.233), calls=%async_computation | async-start | bytes 33554432 | tf_op jit(solution)/shard_map/all_to_all | solution.py:157
  216.2 108.7 %slice-start = ((s8[6291456]{0:T(1024)(128)(4,1)}), s8[2097152]{0:T(1024)(128)(4,1)S(1)}, s32[]{:S(2)}) async-start(s8[6291456]{0:T(1024)(128)(4,1)} %bitcast.239), calls=%async_computation.2 | async-start | bytes 4194304
  241.4 0.8 copy-start.1
  318.1 6.9 %slice-start.1 = ((s8[6291456]{0:T(1024)(128)(4,1)}), s8[4194304]{0:T(1024)(128)(4,1)S(1)}, s32[]{:S(2)}) async-start(s8[6291456]{0:T(1024)(128)(4,1)} %bitcast.239), calls=%async_computation.3 | async-start | bytes 8388608
  318.6 17.7 %copy-start.3 = (f32[256,256]{1,0:T(8,128)}, f32[256,256]{1,0:T(8,128)S(1)}, u32[]{:S(2)}) copy-start(f32[256,256]{1,0:T(8,128)S(1)} %select_maximum_fusion.7) | copy-start | bytes 786436
  348.3 7.9 %copy-start.5 = (f32[512,128]{1,0:T(8,128)S(1)}, f32[512,128]{1,0:T(8,128)}, u32[]{:S(2)}) copy-start(f32[512,128]{1,0:T(8,128)} %get-tuple-element.55) | copy-start | bytes 786436
  348.3 7.9 %copy-start.7 = (f32[128,128]{1,0:T(8,128)S(1)}, f32[128,128]{1,0:T(8,128)}, u32[]{:S(2)}) copy-start(f32[128,128]{1,0:T(8,128)} %get-tuple-element.32) | copy-start | bytes 196612
  348.3 8.9 %copy-start.4 = (f32[256,256]{1,0:T(8,128)S(1)}, f32[256,256]{1,0:T(8,128)}, u32[]{:S(2)}) copy-start(f32[256,256]{1,0:T(8,128)} %copy-done.3) | copy-start | bytes 786436
  348.3 8.9 %copy-start.6 = (f32[24,1,1,1,8,512]{5,4,3,2,1,0:T(8,128)S(1)}, f32[24,1,1,1,8,512]{5,4,3,2,1,0:T(8,128)}, u32[]{:S(2)}) copy-start(f32[24,1,1,1,8,512]{5,4,3,2,1,0:T(8,128)} %param.13) | copy-start | bytes 1179652
Sparse Core Ops, SparseCore 0:
  9.7 130.6 all-gather.2
where the time goes:
time: 548 us; the launch traced here: 537 us
  other arithmetic  208 us (38%)
  waiting for transfers between devices  133 us (24%)
  local copies, waits for them, and re-layouts  77.5 us (14%)
  matrix products  76.2 us (14%)
  starting transfers between devices  26.9 us (5%)
  between operations  15.5 us (3%)
    all_to_all x1, waiting for transfers between devices, per_device(): lax.all_to_all(outgoing.reshape(-1, per_row * per_col, BLOCK_EXTENT, BLOC...  131 us
    another operation x24, other arithmetic, factor_and_inverse(): low = jnp.linalg.cholesky(work[:leaf, :leaf])  109 us
    another operation x16, other arithmetic, factor_and_inverse(): inv = lax.linalg.triangular_solve(low, eye, left_side=True, lower=True)  85.2 us
    dot_general x1, matrix products, per_device(): lax.dot_general(child_factor, child_columns, dims, precision=highest)  19.4 us
    gather x1, local copies, waits for them, and re-layouts, per_device(): outgoing = schur_blocks[send_row_index, :, send_col_index, :]  16.2 us
    all_to_all x1, starting transfers between devices, per_device(): lax.all_to_all(outgoing.reshape(-1, per_row * per_col, BLOCK_EXTENT, BLOC...  14.6 us
    unnamed x27, local copies, waits for them, and re-layouts  12.9 us
    dot_general x1, matrix products, per_device(): update = lax.dot_general(row_factor, column_factor, dims, precision=highest)  12.1 us
  transfers between devices with their start and end apart: 4, of which 2 were waited for; matrix products, arithmetic and copies ran while one was open for 60% of the time, Pallas kernels for 0%

commit v1 on v0

--- a/solution.py
+++ b/solution.py
@@ -2,6 +2,8 @@
 import jax.numpy as jnp
 from jax import lax
 from jax.sharding import PartitionSpec as P
+from jax.experimental import pallas as pl
+from jax.experimental.pallas import tpu as pltpu
 
 BLOCK_EXTENT = 128
 PB = 4
@@ -23,6 +25,48 @@
     present = jnp.any(chosen, axis=-1)
     picked = jnp.sum(jnp.where(chosen, values[..., None, None, :], 0), axis=-1)
     return jnp.where(present, picked, missing)
+
+
+WAVE = 32
+
+
+def _gather_blocks_kernel(row_ref, col_ref, src_ref, dst_ref, sems):
+    extent = dst_ref.shape[1]
+    waves = dst_ref.shape[0] // WAVE
+
+    def one_wave(wave, carry):
+        copies = []
+        for t in range(WAVE):
+            slot = wave * WAVE + t
+            row = row_ref[slot]
+            col = col_ref[slot]
+            copy = pltpu.make_async_copy(
+                src_ref.at[pl.ds(row * extent, extent), pl.ds(col * extent, extent)],
+                dst_ref.at[slot],
+                sems.at[t],
+            )
+            copy.start()
+            copies.append(copy)
+        for copy in copies:
+            copy.wait()
+        return carry
+
+    lax.fori_loop(0, waves, one_wave, 0)
+
+
+def gather_blocks(matrix, rows, cols, extent):
+    count = rows.shape[0]
+    return pl.pallas_call(
+        _gather_blocks_kernel,
+        out_shape=jax.ShapeDtypeStruct((count, extent, extent), matrix.dtype),
+        grid_spec=pltpu.PrefetchScalarGridSpec(
+            num_scalar_prefetch=2,
+            grid=(1,),
+            in_specs=[pl.BlockSpec(memory_space=pl.ANY)],
+            out_specs=pl.BlockSpec(memory_space=pl.ANY),
+            scratch_shapes=[pltpu.SemaphoreType.DMA((WAVE,))],
+        ),
+    )(rows, cols, matrix)
 
 
 def _dot_t(x, y):
@@ -108,7 +152,6 @@
     schur_part = child_window.reshape(row_local * BLOCK_EXTENT, col_local * BLOCK_EXTENT) - lax.dot_general(
         child_factor, child_columns, dims, precision=highest
     )
-    schur_blocks = schur_part.reshape(row_local, BLOCK_EXTENT, col_local, BLOCK_EXTENT)
     child_map = lax.dynamic_index_in_dim(index_maps, half_id, axis=0, keepdims=False)
     my_rows = lax.dynamic_index_in_dim(
         child_map.reshape(row_local, row_size), row_id, axis=1, keepdims=False
@@ -140,9 +183,15 @@
         per_col,
         parent_cols,
     )[:, :, 0, :]
-    send_row_index = jnp.minimum(send_rows, row_local - 1)[None, :, None, :, None]
-    send_col_index = jnp.minimum(send_cols, col_local - 1).reshape(2, row_size, per_col)[:, None, :, None, :]
-    outgoing = schur_blocks[send_row_index, :, send_col_index, :]
+    slot_shape = (2, row_size, row_size, per_row, per_col)
+    send_row_index = jnp.broadcast_to(
+        jnp.minimum(send_rows, row_local - 1)[None, :, None, :, None], slot_shape
+    ).reshape(-1)
+    send_col_index = jnp.broadcast_to(
+        jnp.minimum(send_cols, col_local - 1).reshape(2, row_size, per_col)[:, None, :, None, :],
+        slot_shape,
+    ).reshape(-1)
+    outgoing = gather_blocks(schur_part, send_row_index, send_col_index, BLOCK_EXTENT)
     outgoing, gathered, parent_col_rows, parent_diag = lax.optimization_barrier(
         (outgoing, gathered, parent_col_rows, parent_diag)
     )
@@ -161,7 +210,6 @@
         concat_axis=0,
         tiled=True,
     )
-    slot_shape = (2, row_size, row_size, per_row, per_col)
     slot_rows = jnp.broadcast_to(row_target[:, :, None, :, None], slot_shape).reshape(2, -1)
     slot_cols = jnp.broadcast_to(col_target[:, None, :, None, :], slot_shape).reshape(2, -1)
     slots = slot_rows.shape[1]
@@ -170,10 +218,10 @@
     )
     slot_of = jnp.sum(jnp.where(match, jnp.arange(slots, dtype=jnp.int32), 0), axis=-1)
     present = jnp.any(match, axis=-1)
-    flat_arrived = arrived.reshape(2, slots, BLOCK_EXTENT, BLOCK_EXTENT)
-    first = jnp.take(flat_arrived[0], slot_of[0].reshape(-1), axis=0, mode="clip")
-    second = jnp.take(flat_arrived[1], slot_of[1].reshape(-1), axis=0, mode="clip")
+    flat_arrived = arrived.reshape(2 * slots, BLOCK_EXTENT, BLOCK_EXTENT)
     block_shape = (parent_row_blocks, parent_cols, BLOCK_EXTENT, BLOCK_EXTENT)
+    first = jnp.take(flat_arrived, slot_of[0].reshape(-1), axis=0, mode="clip")
+    second = jnp.take(flat_arrived, slot_of[1].reshape(-1) + slots, axis=0, mode="clip")
     assembled = jnp.where(present[0, :, :, None, None], first.reshape(block_shape), 0.0) + jnp.where(
         present[1, :, :, None, None], second.reshape(block_shape), 0.0
     )

time: 548 us -> 1030 us (1.88)
  Pallas kernels: 0 us -> 518 us
  local copies, waits for them, and re-layouts: 77.5 us -> 49.7 us
    pallas_call x0 -> x1, Pallas kernels: none -> 518 us  [gather_blocks(): pl.pallas_call(_gather_blocks_kernel, out_shape=jax.ShapeDtypeStruct((cou...]
    gather x3 -> x2, local copies, waits for them, and re-layouts: 30.2 us -> 18.8 us  [the longest x1 9.42 us: per_device(): jnp.take(flat_arrived, slot_of[1].reshape(-1) + slots, axis=0, mode='clip')]
    slice x4 -> x1, local copies, waits for them, and re-layouts: 11 us -> 0.09 us  [per_device(): first = jnp.take(flat_arrived, slot_of[0].reshape(-1), axis=0, mode='clip')]
  transfers between devices with their start and end apart: 4 -> 4, of which waited for: 2 -> 2; matrix products, arithmetic and copies ran while one was open for 60% -> 28% of each run, Pallas kernels for 0% -> 51%
where the time goes in v1:
time: 1030 us; the launch traced here: 1020 us
  Pallas kernels  518 us (50%)
  other arithmetic  199 us (19%)
  waiting for transfers between devices  141 us (14%)
  matrix products  75.9 us (7%)
  local copies, waits for them, and re-layouts  49.7 us (5%)
  starting transfers between devices  20.5 us (2%)
  between operations  15.5 us (2%)
    pallas_call x1, Pallas kernels, gather_blocks(): pl.pallas_call(_gather_blocks_kernel, out_shape=jax.ShapeDtypeStruct((cou...  518 us
    all_to_all x1, waiting for transfers between devices, per_device(): lax.all_to_all(outgoing.reshape(-1, per_row * per_col, BLOCK_EXTENT, BLOC...  131 us
    another operation x24, other arithmetic, factor_and_inverse(): low = jnp.linalg.cholesky(work[:leaf, :leaf])  100 us
    another operation x16, other arithmetic, factor_and_inverse(): inv = lax.linalg.triangular_solve(low, eye, left_side=True, lower=True)  85.2 us
  transfers between devices with their start and end apart: 4, of which 2 were waited for; matrix products, arithmetic and copies ran while one was open for 28% of the time, Pallas kernels for 51%

profile of v1, /device:TPU:10, one launch (start us, length us, event | category | flops | bytes accessed | tf_op | source)
XLA Modules:
  0.0 1019.6 jit_solution(3183294847736963761)
XLA Ops:
  20.1 11.7 %cholesky.134 = f32[128,128]{1,0:T(8,128)S(1)} custom-call(f32[128,128]{1,0:T(8,128)S(1)} %fusion.68), custom_call_target="Cholesky" | custom-call | tf_op jit(solution)/shard_map/jit(cholesky)/cholesky | solution.py:88
  33.1 9.8 custom-call.12
  44.4 11.7 %cholesky.145 = f32[128,128]{1,0:T(8,128)S(1)} custom-call(f32[128,128]{1,0:T(8,128)S(1)} %fusion.66), custom_call_target="Cholesky" | custom-call | tf_op jit(solution)/shard_map/jit(cholesky)/cholesky | solution.py:88
  57.4 10.0 custom-call.13
  68.6 11.7 %cholesky.156 = f32[128,128]{1,0:T(8,128)S(1)} custom-call(f32[128,128]{1,0:T(8,128)S(1)} %fusion.64), custom_call_target="Cholesky" | custom-call | tf_op jit(solution)/shard_map/jit(cholesky)/cholesky | solution.py:88
  81.7 9.8 custom-call.14
  92.5 12.1 %cholesky.167 = f32[128,128]{1,0:T(8,128)S(1)} custom-call(f32[128,128]{1,0:T(8,128)S(1)} %fusion.62), custom_call_target="Cholesky" | custom-call | tf_op jit(solution)/shard_map/jit(cholesky)/cholesky | solution.py:88
  105.9 9.8 custom-call.15
  120.7 10.0 fusion.2
  130.7 9.6 all-gather.3.cloned.1.call-done
  155.4 19.3 %bitcast_subtract_fusion.src_ref = f32[2048,1024]{1,0:T(8,128)} fusion(f32[256,8,8,128]{3,2,1,0:T(8,128)} %bitcast.229, f32[512,2048]{1,0:T(8,128)S(1)} %copy-done, f32[512,1024]{1,0:T(8,128)S(1)} %fusion.1), kind=kOutput, calls=%fused_computation.2 | convolution fusion | flops 12886999040 | bytes 23068672 | tf_op jit(solution)/shard_map/dot_general | solution.py:152
  174.6 518.0 %shard_map.85 = f32[256,128,128]{2,1,0:T(8,128)} custom-call(s32[256]{0:T(256)} %broadcast_in_dim.149.row_ref, s32[256]{0:T(256)} %broadcast_in_dim.152.col_ref, f32[2048,1024]{1,0:T(8,128)} %bitcast_subtract_fusion.src_ref), custom_call_target="tpu_custom_call" | custom-call | tf_op jit(solution)/shard_map/pallas_call | solution.py:59
  705.1 11.7 %cholesky.178 = f32[128,128]{1,0:T(8,128)S(1)} custom-call(f32[128,128]{1,0:T(8,128)S(1)} %fusion.60), custom_call_target="Cholesky" | custom-call | tf_op jit(solution)/shard_map/jit(cholesky)/cholesky | solution.py:88
  718.1 9.8 custom-call.16
  731.9 12.1 %cholesky.189 = f32[128,128]{1,0:T(8,128)S(1)} custom-call(f32[128,128]{1,0:T(8,128)S(1)} %fusion.58), custom_call_target="Cholesky" | custom-call | tf_op jit(solution)/shard_map/jit(cholesky)/cholesky | solution.py:88
  745.4 9.8 custom-call.17
  758.3 11.7 %cholesky.200 = f32[128,128]{1,0:T(8,128)S(1)} custom-call(f32[128,128]{1,0:T(8,128)S(1)} %fusion.56), custom_call_target="Cholesky" | custom-call | tf_op jit(solution)/shard_map/jit(cholesky)/cholesky | solution.py:88
  772.0 9.8 custom-call.18
  782.8 11.9 %cholesky.211 = f32[128,128]{1,0:T(8,128)S(1)} custom-call(f32[128,128]{1,0:T(8,128)S(1)} %fusion.54), custom_call_target="Cholesky" | custom-call | tf_op jit(solution)/shard_map/jit(cholesky)/cholesky | solution.py:88
  796.6 9.8 custom-call.19
  813.7 11.3 %fusion.102 = f32[3072,512]{1,0:T(8,128)S(1)} fusion(f32[3072,512]{1,0:T(8,128)S(1)} %bitcast.228, f32[256,256]{1,0:T(8,128)S(1)} %select_maximum_fusion.7, f32[128,128]{1,0:T(8,128)S(1)} %copy.113, f32[128,128]{1,0:T(8,128)S(1)} %convolution_negate_fusion.2, f32[128,256]{1,0:T(8,128)S(1)} %concatenate.95, f32[256,256]{1,0:T(8,128)S(1)} %convolution_negate_fusion), kind=kOutput, calls=%fused_computation.227 | convolution fusion | flops 9665249280 | bytes 13369344 | tf_op jit(solution)/shard_map/dot_general | solution.py:201
  825.0 12.1 %fusion.114 = f32[3072,512]{1,0:T(8,128)} fusion(f32[3072,512]{1,0:T(8,128)S(1)} %fusion.102, f32[512,512]{1,0:T(8,128)S(1)} %fusion.101), kind=kOutput, calls=%fused_computation.234 | convolution fusion | flops 9663676416 | bytes 13631488 | tf_op jit(solution)/shard_map/dot_general | solution.py:205
  847.8 130.8 %all-to-all-done = f32[128,2,128,128]{3,2,1,0:T(8,128)} async-done(((f32[128,2,128,128]{3,2,1,0:T(8,128)}), f32[128,2,128,128]{3,2,1,0:T(8,128)}, u32[]{:S(2)}, u32[]{:S(2)}) %all-to-all-start) | async-done | bytes 16777248 | tf_op jit(solution)/shard_map/all_to_all | solution.py:206
  978.6 9.4 gather_fusion.1
  (196 shorter events, 110.3 us)
Async XLA Ops:
  7.2 133.2 %all-gather.3.cloned.1.call-start = ((), (), s32[]{:S(2)}) async-start(), calls=%async_computation.1 | async-start | bytes 6684672 | tf_op jit(solution)/shard_map/all_gather | solution.py:136
  11.0 139.2 %collective-permute-start = (f32[8,128,512]{2,1,0:T(8,128)}, f32[8,128,512]{2,1,0:T(8,128)}, u32[]{:S(2)}, u32[]{:S(2)}) collective-permute-start(f32[8,128,512]{2,1,0:T(8,128)} %slice_bitcast_fusion), channel_id=1, source_target_pairs={{0,0},{1,8},{2,16},{3,24},{4,32},{5,40},{6,48},{7,56},{8,1},{9,9},... | collective-permute-start | bytes 6291464 | tf_op jit(solution)/shard_map/ppermute | solution.py:133
  140.4 15.0 %copy-start = (f32[512,2048]{1,0:T(8,128)S(1)}, f32[512,2048]{1,0:T(8,128)}, u32[]{:S(2)}) copy-start(f32[512,2048]{1,0:T(8,128)} %fusion.2) | copy-start | bytes 12582916
  142.4 550.2 %collective-permute-start.1 = (f32[4,128,512]{2,1,0:T(8,128)S(1)}, f32[4,128,512]{2,1,0:T(8,128)S(1)}, u32[]{:S(2)}, u32[]{:S(2)}) collective-permute-start(f32[4,128,512]{2,1,0:T(8,128)S(1)} %dynamic-slice_bitcast_fusion), channel_id=1, source_target_pairs={{0,0},{1,8},{2,16},{3,24},{4,32},{5,40},{6,48},{7,56},{8,1},{9,9},... | collective-permute-start | bytes 3145736 | tf_op jit(solution)/shard_map/ppermute | solution.py:144
  692.7 1.0 copy-start.9
  692.7 9.1 copy-start.8
  692.7 11.9 %copy-start.2 = (f32[512,512]{1,0:T(8,128)S(1)}, f32[512,512]{1,0:T(8,128)}, u32[]{:S(2)}) copy-start(f32[512,512]{1,0:T(8,128)} %param.12) | copy-start | bytes 3145732
  693.6 285.0 %all-to-all-start = ((f32[128,2,128,128]{3,2,1,0:T(8,128)}), f32[128,2,128,128]{3,2,1,0:T(8,128)}, u32[]{:S(2)}, u32[]{:S(2)}) async-start(f32[128,2,128,128]{3,2,1,0:T(8,128)} %bitcast.223), calls=%async_computation | async-start | bytes 33554432 | tf_op jit(solution)/shard_map/all_to_all | solution.py:206
  704.9 108.7 %slice-start = ((s8[6291456]{0:T(1024)(128)(4,1)}), s8[2097152]{0:T(1024)(128)(4,1)S(1)}, s32[]{:S(2)}) async-start(s8[6291456]{0:T(1024)(128)(4,1)} %bitcast.226), calls=%async_computation.2 | async-start | bytes 4194304
  730.1 0.8 copy-start.1
  806.8 6.9 slice-start.1
  807.3 17.7 %copy-start.3 = (f32[256,256]{1,0:T(8,128)}, f32[256,256]{1,0:T(8,128)S(1)}, u32[]{:S(2)}) copy-start(f32[256,256]{1,0:T(8,128)S(1)} %select_maximum_fusion.7) | copy-start | bytes 786436
  837.1 7.9 copy-start.5
  837.1 7.9 copy-start.7
  837.1 8.9 copy-start.4
  837.1 8.9 copy-start.6
Sparse Core Ops, SparseCore 0:
  9.7 130.5 all-gather.2

commit v2 on v0

--- a/solution.py
+++ b/solution.py
@@ -84,9 +84,14 @@
     parent_cols = WB // group_size
     per_row = 2 * (SB // group_size) // row_size
     per_col = (WB // group_size + row_size - 1) // row_size
-    transpose_perm = [(i * col_size + j, j * row_size + i) for i in range(row_size) for j in range(col_size)]
+    transpose_perm = [
+        (i * col_size + j, j * row_size + i) for i in range(row_size) for j in range(col_size) if i != j
+    ]
+    on_diagonal = row_id == col_id
     child_lead = child_panel[0, :col_local, 0]
-    child_col_rows = lax.ppermute(child_lead, ("row", "col"), transpose_perm)
+    child_col_rows = jnp.where(
+        on_diagonal, child_lead, lax.ppermute(child_lead, ("row", "col"), transpose_perm)
+    )
     sub_rows = parent_lead_panel.shape[4]
     own_rows = parent_lead_panel.reshape(-1, panel_width)
     gathered = lax.all_gather(
@@ -97,7 +102,9 @@
     )
     paired = gathered[: 2 * parent_cols].reshape(parent_cols, 2, BLOCK_EXTENT, panel_width)
     offered = lax.dynamic_index_in_dim(paired, half_id, axis=1, keepdims=False)
-    parent_col_rows = lax.ppermute(offered, ("row", "col"), transpose_perm)
+    parent_col_rows = jnp.where(
+        on_diagonal, offered, lax.ppermute(offered, ("row", "col"), transpose_perm)
+    )
     child_low, child_inv = factor_and_inverse(child_diag[0], BLOCK_EXTENT)
     child_rows = child_panel.reshape(-1, panel_width)
     dims = (((1,), (1,)), ((), ()))
@@ -108,7 +115,6 @@
     schur_part = child_window.reshape(row_local * BLOCK_EXTENT, col_local * BLOCK_EXTENT) - lax.dot_general(
         child_factor, child_columns, dims, precision=highest
     )
-    schur_blocks = schur_part.reshape(row_local, BLOCK_EXTENT, col_local, BLOCK_EXTENT)
     child_map = lax.dynamic_index_in_dim(index_maps, half_id, axis=0, keepdims=False)
     my_rows = lax.dynamic_index_in_dim(
         child_map.reshape(row_local, row_size), row_id, axis=1, keepdims=False
@@ -140,6 +146,7 @@
         per_col,
         parent_cols,
     )[:, :, 0, :]
+    schur_blocks = schur_part.reshape(row_local, BLOCK_EXTENT, col_local, BLOCK_EXTENT)
     send_row_index = jnp.minimum(send_rows, row_local - 1)[None, :, None, :, None]
     send_col_index = jnp.minimum(send_cols, col_local - 1).reshape(2, row_size, per_col)[:, None, :, None, :]
     outgoing = schur_blocks[send_row_index, :, send_col_index, :]
@@ -170,10 +177,10 @@
     )
     slot_of = jnp.sum(jnp.where(match, jnp.arange(slots, dtype=jnp.int32), 0), axis=-1)
     present = jnp.any(match, axis=-1)
-    flat_arrived = arrived.reshape(2, slots, BLOCK_EXTENT, BLOCK_EXTENT)
-    first = jnp.take(flat_arrived[0], slot_of[0].reshape(-1), axis=0, mode="clip")
-    second = jnp.take(flat_arrived[1], slot_of[1].reshape(-1), axis=0, mode="clip")
+    flat_arrived = arrived.reshape(2 * slots, BLOCK_EXTENT, BLOCK_EXTENT)
     block_shape = (parent_row_blocks, parent_cols, BLOCK_EXTENT, BLOCK_EXTENT)
+    first = jnp.take(flat_arrived, slot_of[0].reshape(-1), axis=0, mode="clip")
+    second = jnp.take(flat_arrived, slot_of[1].reshape(-1) + slots, axis=0, mode="clip")
     assembled = jnp.where(present[0, :, :, None, None], first.reshape(block_shape), 0.0) + jnp.where(
         present[1, :, :, None, None], second.reshape(block_shape), 0.0
     )

time: 548 us -> 548 us (level)
  matrix products: 76.2 us -> 87.3 us
  starting transfers between devices: 26.9 us -> 20 us
  local copies, waits for them, and re-layouts: 77.5 us -> 71.6 us
    dot_general x1, matrix products: 19.4 us -> 31.8 us  [per_device(): lax.dot_general(child_factor, child_columns, dims, precision=highest)]
    slice x4 -> x1, local copies, waits for them, and re-layouts: 11 us -> 0.09 us  [per_device(): first = jnp.take(flat_arrived, slot_of[0].reshape(-1), axis=0, mode='clip')]
    unnamed x27 -> x31, local copies, waits for them, and re-layouts: 12.9 us -> 12 us
  transfers between devices with their start and end apart: 4 -> 4, of which waited for: 2 -> 1; matrix products, arithmetic and copies ran while one was open for 60% -> 62% of each run, Pallas kernels for 0% -> 0%
where the time goes in v2:
time: 548 us; the launch traced here: 539 us
  other arithmetic  213 us (39%)
  waiting for transfers between devices  132 us (24%)
  matrix products  87.3 us (16%)
  local copies, waits for them, and re-layouts  71.6 us (13%)
  starting transfers between devices  20 us (4%)
  between operations  15.5 us (3%)
    all_to_all x1, waiting for transfers between devices, per_device(): lax.all_to_all(outgoing.reshape(-1, per_row * per_col, BLOCK_EXTENT, BLOC...  131 us
    another operation x24, other arithmetic, factor_and_inverse(): low = jnp.linalg.cholesky(work[:leaf, :leaf])  109 us
    another operation x16, other arithmetic, factor_and_inverse(): inv = lax.linalg.triangular_solve(low, eye, left_side=True, lower=True)  85.2 us
    dot_general x1, matrix products, per_device(): lax.dot_general(child_factor, child_columns, dims, precision=highest)  31.8 us
    gather x1, local copies, waits for them, and re-layouts, per_device(): outgoing = schur_blocks[send_row_index, :, send_col_index, :]  16.1 us
    dot_general x1, matrix products, per_device(): update = lax.dot_general(row_factor, column_factor, dims, precision=highest)  12.1 us
    unnamed x31, local copies, waits for them, and re-layouts  12 us
    dot_general x1, matrix products, per_device(): lax.dot_general(gathered.reshape(-1, panel_width), parent_inv, dims, prec...  11.3 us
  transfers between devices with their start and end apart: 4, of which 1 were waited for; matrix products, arithmetic and copies ran while one was open for 62% of the time, Pallas kernels for 0%

profile of v2, /device:TPU:10, one launch (start us, length us, event | category | flops | bytes accessed | tf_op | source)
XLA Modules:
  0.0 538.6 jit_solution(11404851646020074242)
XLA Ops:
  21.0 11.7 %cholesky.134 = f32[128,128]{1,0:T(8,128)S(1)} custom-call(f32[128,128]{1,0:T(8,128)S(1)} %fusion.69), custom_call_target="Cholesky" | custom-call | tf_op jit(solution)/shard_map/jit(cholesky)/cholesky | solution.py:44
  34.1 9.8 %custom-call.14 = f32[1,128,128]{1,2,0:T(8,128)S(1)} custom-call(f32[1,128,128]{2,1,0:T(8,128)S(1)} %get-tuple-element.45), custom_call_target="InvertDiagBlocksLowerTriangular" | custom-call | tf_op jit(solution)/shard_map/triangular_solve/custom-call.0 | solution.py:45
  45.4 11.7 %cholesky.145 = f32[128,128]{1,0:T(8,128)S(1)} custom-call(f32[128,128]{1,0:T(8,128)S(1)} %fusion.67), custom_call_target="Cholesky" | custom-call | tf_op jit(solution)/shard_map/jit(cholesky)/cholesky | solution.py:44
  58.5 10.0 %custom-call.15 = f32[1,128,128]{1,2,0:T(8,128)S(1)} custom-call(f32[1,128,128]{2,1,0:T(8,128)S(1)} %get-tuple-element.43), custom_call_target="InvertDiagBlocksLowerTriangular" | custom-call | tf_op jit(solution)/shard_map/triangular_solve/custom-call.0 | solution.py:45
  69.9 11.7 %cholesky.156 = f32[128,128]{1,0:T(8,128)S(1)} custom-call(f32[128,128]{1,0:T(8,128)S(1)} %fusion.65), custom_call_target="Cholesky" | custom-call | tf_op jit(solution)/shard_map/jit(cholesky)/cholesky | solution.py:44
  83.0 9.8 %custom-call.16 = f32[1,128,128]{1,2,0:T(8,128)S(1)} custom-call(f32[1,128,128]{2,1,0:T(8,128)S(1)} %fusion.44), custom_call_target="InvertDiagBlocksLowerTriangular" | custom-call | tf_op jit(solution)/shard_map/triangular_solve/custom-call.0 | solution.py:45
  93.8 21.5 %cholesky.167 = f32[128,128]{1,0:T(8,128)S(1)} custom-call(f32[128,128]{1,0:T(8,128)S(1)} %fusion.63), custom_call_target="Cholesky" | custom-call | tf_op jit(solution)/shard_map/jit(cholesky)/cholesky | solution.py:44
  116.6 9.8 %custom-call.17 = f32[1,128,128]{1,2,0:T(8,128)S(1)} custom-call(f32[1,128,128]{2,1,0:T(8,128)S(1)} %fusion.45), custom_call_target="InvertDiagBlocksLowerTriangular" | custom-call | tf_op jit(solution)/shard_map/triangular_solve/custom-call.0 | solution.py:45
  129.0 10.5 %fusion.3 = f32[512,2048]{1,0:T(8,128)} fusion(f32[2048,512]{1,0:T(8,128)} %bitcast.240, f32[256,256]{1,0:T(8,128)S(1)} %select_maximum_fusion.9, f32[128,128]{1,0:T(8,128)S(1)} %copy.131, f32[128,128]{1,0:T(8,128)S(1)} %convolution_negate_fusion.4, f32[128,256]{1,0:T(8,128)S(1)} %concatenate.86, f32[256,256]{1,0:T(8,128)S(1)} %convolution_negate_fusion.1), kind=kOutput, calls=%fused_computation.30 | convolution fusion | flops 6444023808 | bytes 9175040 | tf_op jit(solution)/shard_map/dot_general | solution.py:111
  153.9 31.8 %fusion = f32[256,8,8,128]{3,1,2,0:T(8,128)S(1)} fusion(f32[256,8,8,128]{3,2,1,0:T(8,128)} %bitcast.244, f32[512,2048]{1,0:T(8,128)S(1)} %copy-done, f32[1024,512]{1,0:T(8,128)S(1)} %fusion.2), kind=kOutput, calls=%fused_computation.4 | convolution fusion | flops 12886999040 | bytes 23068672 | tf_op jit(solution)/shard_map/dot_general | solution.py:115
  192.5 16.1 %gather_fusion = f32[256,128,128]{2,1,0:T(8,128)} fusion(f32[16,128,8,128]{3,1,2,0:T(8,128)} %copy.137, s32[256]{0:T(256)S(1)} %reshape.464), kind=kCustom, calls=%fused_computation | custom fusion | bytes 33556480 | tf_op jit(solution)/shard_map/gather | solution.py:152
  211.1 9.7 %all-to-all-start = ((f32[128,2,128,128]{3,2,1,0:T(8,128)}), f32[128,2,128,128]{3,2,1,0:T(8,128)}, u32[]{:S(2)}, u32[]{:S(2)}) async-start(f32[128,2,128,128]{3,2,1,0:T(8,128)} %bitcast.236), calls=%async_computation | async-start | bytes 33554432 | tf_op jit(solution)/shard_map/all_to_all | solution.py:164
  224.1 11.7 %cholesky.178 = f32[128,128]{1,0:T(8,128)S(1)} custom-call(f32[128,128]{1,0:T(8,128)S(1)} %fusion.61), custom_call_target="Cholesky" | custom-call | tf_op jit(solution)/shard_map/jit(cholesky)/cholesky | solution.py:44
  237.2 9.8 %custom-call.18 = f32[1,128,128]{1,2,0:T(8,128)S(1)} custom-call(f32[1,128,128]{2,1,0:T(8,128)S(1)} %get-tuple-element.37), custom_call_target="InvertDiagBlocksLowerTriangular" | custom-call | tf_op jit(solution)/shard_map/triangular_solve/custom-call.0 | solution.py:45
  251.0 12.1 %cholesky.189 = f32[128,128]{1,0:T(8,128)S(1)} custom-call(f32[128,128]{1,0:T(8,128)S(1)} %fusion.59), custom_call_target="Cholesky" | custom-call | tf_op jit(solution)/shard_map/jit(cholesky)/cholesky | solution.py:44
  264.4 9.8 %custom-call.19 = f32[1,128,128]{1,2,0:T(8,128)S(1)} custom-call(f32[1,128,128]{2,1,0:T(8,128)S(1)} %get-tuple-element.35), custom_call_target="InvertDiagBlocksLowerTriangular" | custom-call | tf_op jit(solution)/shard_map/triangular_solve/custom-call.0 | solution.py:45
  277.4 11.7 %cholesky.200 = f32[128,128]{1,0:T(8,128)S(1)} custom-call(f32[128,128]{1,0:T(8,128)S(1)} %fusion.57), custom_call_target="Cholesky" | custom-call | tf_op jit(solution)/shard_map/jit(cholesky)/cholesky | solution.py:44
  291.0 9.8 %custom-call.20 = f32[1,128,128]{1,2,0:T(8,128)S(1)} custom-call(f32[1,128,128]{2,1,0:T(8,128)S(1)} %get-tuple-element.33), custom_call_target="InvertDiagBlocksLowerTriangular" | custom-call | tf_op jit(solution)/shard_map/triangular_solve/custom-call.0 | solution.py:45
  301.8 11.9 %cholesky.211 = f32[128,128]{1,0:T(8,128)S(1)} custom-call(f32[128,128]{1,0:T(8,128)S(1)} %fusion.55), custom_call_target="Cholesky" | custom-call | tf_op jit(solution)/shard_map/jit(cholesky)/cholesky | solution.py:44
  315.7 9.8 %custom-call.21 = f32[1,128,128]{1,2,0:T(8,128)S(1)} custom-call(f32[1,128,128]{2,1,0:T(8,128)S(1)} %get-tuple-element.31), custom_call_target="InvertDiagBlocksLowerTriangular" | custom-call | tf_op jit(solution)/shard_map/triangular_solve/custom-call.0 | solution.py:45
  332.7 11.3 %fusion.106 = f32[3072,512]{1,0:T(8,128)S(1)} fusion(f32[3072,512]{1,0:T(8,128)S(1)} %bitcast.243, f32[256,256]{1,0:T(8,128)S(1)} %select_maximum_fusion.7, f32[128,128]{1,0:T(8,128)S(1)} %copy.153, f32[128,128]{1,0:T(8,128)S(1)} %convolution_negate_fusion.2, f32[128,256]{1,0:T(8,128)S(1)} %concatenate.99, f32[256,256]{1,0:T(8,128)S(1)} %convolution_negate_fusion), kind=kOutput, calls=%fused_computation.238 | convolution fusion | flops 9665249280 | bytes 13369344 | tf_op jit(solution)/shard_map/dot_general | solution.py:159
  344.0 12.1 %fusion.118 = f32[3072,512]{1,0:T(8,128)} fusion(f32[3072,512]{1,0:T(8,128)S(1)} %fusion.106, f32[512,512]{1,0:T(8,128)S(1)} %fusion.105), kind=kOutput, calls=%fused_computation.245 | convolution fusion | flops 9663676416 | bytes 13631488 | tf_op jit(solution)/shard_map/dot_general | solution.py:163
  366.8 130.8 %all-to-all-done = f32[128,2,128,128]{3,2,1,0:T(8,128)} async-done(((f32[128,2,128,128]{3,2,1,0:T(8,128)}), f32[128,2,128,128]{3,2,1,0:T(8,128)}, u32[]{:S(2)}, u32[]{:S(2)}) %all-to-all-start) | async-done | bytes 16777248 | tf_op jit(solution)/shard_map/all_to_all | solution.py:164
  497.6 9.4 %gather_fusion.2 = f32[96,128,128]{2,1,0:T(8,128)} fusion(f32[256,128,128]{2,1,0:T(8,128)} %bitcast.27, s32[1024]{0:T(1024)S(1)} %pad_clamp_fusion), kind=kCustom, calls=%fused_computation.2 | custom fusion | bytes 12583296 | tf_op jit(solution)/shard_map/jit(_take)/gather | solution.py:183
  (206 shorter events, 108.7 us)
Async XLA Ops:
  7.2 134.5 %all-gather.3.cloned.1.call-start = ((), (), s32[]{:S(2)}) async-start(), calls=%async_computation.1 | async-start | bytes 6684672 | tf_op jit(solution)/shard_map/all_gather | solution.py:97
  11.0 128.5 %collective-permute-start = (f32[8,128,512]{2,1,0:T(8,128)}, f32[8,128,512]{2,1,0:T(8,128)}, u32[]{:S(2)}, u32[]{:S(2)}) collective-permute-start(f32[8,128,512]{2,1,0:T(8,128)} %slice_bitcast_fusion), channel_id=1, source_target_pairs={{1,8},{2,16},{3,24},{4,32},{5,40},{6,48},{7,56},{8,1},{10,17},{11,... | collective-permute-start | bytes 6291464 | tf_op jit(solution)/shard_map/ppermute | solution.py:93
  128.1 11.4 %copy-start.1 = (f32[1,16,1,128,512]{4,3,2,1,0:T(8,128)S(1)}, f32[1,16,1,128,512]{4,3,2,1,0:T(8,128)}, u32[]{:S(2)}) copy-start(f32[1,16,1,128,512]{4,3,2,1,0:T(8,128)} %param.10) | copy-start | bytes 12582916
  141.7 12.3 %copy-start = (f32[512,2048]{1,0:T(8,128)S(1)}, f32[512,2048]{1,0:T(8,128)}, u32[]{:S(2)}) copy-start(f32[512,2048]{1,0:T(8,128)} %fusion.3) | copy-start | bytes 12582916
  143.6 10.2 %copy-start.2 = (f32[8,1,1,1,128,512]{5,4,3,2,1,0:T(8,128)}, f32[8,1,1,1,128,512]{5,4,3,2,1,0:T(8,128)S(1)}, u32[]{:S(2)}) copy-start(f32[8,1,1,1,128,512]{5,4,3,2,1,0:T(8,128)S(1)} %slice.154) | copy-start | bytes 6291460
  144.8 63.8 %collective-permute-start.1 = (f32[4,128,512]{2,1,0:T(8,128)}, f32[4,128,512]{2,1,0:T(8,128)}, u32[]{:S(2)}, u32[]{:S(2)}) collective-permute-start(f32[4,128,512]{2,1,0:T(8,128)} %dynamic-slice_bitcast_fusion), channel_id=1, source_target_pairs={{1,8},{2,16},{3,24},{4,32},{5,40},{6,48},{7,56},{8,1},{10,17},{11,... | collective-permute-start | bytes 3145736 | tf_op jit(solution)/shard_map/ppermute | solution.py:106
  192.5 16.2 %copy-start.3 = (f32[8,1,1,1,128,512]{5,4,3,2,1,0:T(8,128)S(1)}, f32[8,1,1,1,128,512]{5,4,3,2,1,0:T(8,128)}, u32[]{:S(2)}) copy-start(f32[8,1,1,1,128,512]{5,4,3,2,1,0:T(8,128)} %copy-done.2) | copy-start | bytes 6291460
  211.1 9.7 %copy-start.11 = (s32[2,128]{1,0:T(2,128)S(1)}, s32[2,128]{1,0:T(2,128)}, u32[]{:S(2)}) copy-start(s32[2,128]{1,0:T(2,128)} %param.14) | copy-start | bytes 3076
  211.1 12.6 %copy-start.5 = (f32[512,512]{1,0:T(8,128)S(1)}, f32[512,512]{1,0:T(8,128)}, u32[]{:S(2)}) copy-start(f32[512,512]{1,0:T(8,128)} %param.12) | copy-start | bytes 3145732
  211.1 286.6 %all-to-all-start = ((f32[128,2,128,128]{3,2,1,0:T(8,128)}), f32[128,2,128,128]{3,2,1,0:T(8,128)}, u32[]{:S(2)}, u32[]{:S(2)}) async-start(f32[128,2,128,128]{3,2,1,0:T(8,128)} %bitcast.236), calls=%async_computation | async-start | bytes 33554432 | tf_op jit(solution)/shard_map/all_to_all | solution.py:164
  224.0 108.7 %slice-start = ((s8[6291456]{0:T(1024)(128)(4,1)}), s8[2097152]{0:T(1024)(128)(4,1)S(1)}, s32[]{:S(2)}) async-start(s8[6291456]{0:T(1024)(128)(4,1)} %bitcast.241), calls=%async_computation.2 | async-start | bytes 4194304
  249.2 0.8 copy-start.4
  325.8 6.9 %slice-start.1 = ((s8[6291456]{0:T(1024)(128)(4,1)}), s8[4194304]{0:T(1024)(128)(4,1)S(1)}, s32[]{:S(2)}) async-start(s8[6291456]{0:T(1024)(128)(4,1)} %bitcast.241), calls=%async_computation.3 | async-start | bytes 8388608
  326.4 17.6 %copy-start.6 = (f32[256,256]{1,0:T(8,128)}, f32[256,256]{1,0:T(8,128)S(1)}, u32[]{:S(2)}) copy-start(f32[256,256]{1,0:T(8,128)S(1)} %select_maximum_fusion.7) | copy-start | bytes 786436
  356.1 7.9 %copy-start.8 = (f32[512,128]{1,0:T(8,128)S(1)}, f32[512,128]{1,0:T(8,128)}, u32[]{:S(2)}) copy-start(f32[512,128]{1,0:T(8,128)} %get-tuple-element.53) | copy-start | bytes 786436
  356.1 7.9 %copy-start.10 = (f32[128,128]{1,0:T(8,128)S(1)}, f32[128,128]{1,0:T(8,128)}, u32[]{:S(2)}) copy-start(f32[128,128]{1,0:T(8,128)} %get-tuple-element.32) | copy-start | bytes 196612
  356.1 8.9 %copy-start.7 = (f32[256,256]{1,0:T(8,128)S(1)}, f32[256,256]{1,0:T(8,128)}, u32[]{:S(2)}) copy-start(f32[256,256]{1,0:T(8,128)} %copy-done.6) | copy-start | bytes 786436
  356.1 8.9 %copy-start.9 = (f32[24,1,1,1,8,512]{5,4,3,2,1,0:T(8,128)S(1)}, f32[24,1,1,1,8,512]{5,4,3,2,1,0:T(8,128)}, u32[]{:S(2)}) copy-start(f32[24,1,1,1,8,512]{5,4,3,2,1,0:T(8,128)} %param.13) | copy-start | bytes 1179652
Sparse Core Ops, SparseCore 0:
  9.7 130.6 all-gather.2

commit v3 on v2

--- a/solution.py
+++ b/solution.py
@@ -108,12 +108,13 @@
     child_low, child_inv = factor_and_inverse(child_diag[0], BLOCK_EXTENT)
     child_rows = child_panel.reshape(-1, panel_width)
     dims = (((1,), (1,)), ((), ()))
-    child_factor = lax.dot_general(child_rows, child_inv, dims, precision=highest)
+    high = lax.Precision.HIGH
+    child_factor = lax.dot_general(child_rows, child_inv, dims, precision=high)
     child_columns = lax.dot_general(
-        child_col_rows.reshape(-1, panel_width), child_inv, dims, precision=highest
+        child_col_rows.reshape(-1, panel_width), child_inv, dims, precision=high
     )
     schur_part = child_window.reshape(row_local * BLOCK_EXTENT, col_local * BLOCK_EXTENT) - lax.dot_general(
-        child_factor, child_columns, dims, precision=highest
+        child_factor, child_columns, dims, precision=high
     )
     child_map = lax.dynamic_index_in_dim(index_maps, half_id, axis=0, keepdims=False)
     my_rows = lax.dynamic_index_in_dim(

time: 548 us -> 540 us (0.985)
  matrix products: 87.3 us -> 68.8 us
  waiting for transfers between devices: 132 us -> 147 us
  other arithmetic: 213 us -> 203 us
    dot_general x2, matrix products: 42.3 us -> 25.3 us  [the longest x1 17.7 us: per_device(): lax.dot_general(child_factor, child_columns, dims, precision=high)]
    all_gather x1, waiting for transfers between devices: 0.02 us -> 11.1 us  [per_device(): lax.all_gather(parent_lead_panel.reshape(parent_row_blocks, sub_rows, pan...]
    another operation x24, other arithmetic: 109 us -> 99.8 us  [factor_and_inverse(): low = jnp.linalg.cholesky(work[:leaf, :leaf])]
  transfers between devices with their start and end apart: 4 -> 4, of which waited for: 1 -> 3; matrix products, arithmetic and copies ran while one was open for 62% -> 57% of each run, Pallas kernels for 0% -> 0%
where the time goes in v3:
time: 540 us; the launch traced here: 531 us
  other arithmetic  203 us (38%)
  waiting for transfers between devices  147 us (27%)
  local copies, waits for them, and re-layouts  71.5 us (13%)
  matrix products  68.8 us (13%)
  starting transfers between devices  24.4 us (5%)
  between operations  15.2 us (3%)
    all_to_all x1, waiting for transfers between devices, per_device(): lax.all_to_all(outgoing.reshape(-1, per_row * per_col, BLOCK_EXTENT, BLOC...  131 us
    another operation x24, other arithmetic, factor_and_inverse(): low = jnp.linalg.cholesky(work[:leaf, :leaf])  99.8 us
    another operation x16, other arithmetic, factor_and_inverse(): inv = lax.linalg.triangular_solve(low, eye, left_side=True, lower=True)  85.1 us
    dot_general x1, matrix products, per_device(): lax.dot_general(child_factor, child_columns, dims, precision=high)  17.7 us
    gather x1, local copies, waits for them, and re-layouts, per_device(): outgoing = schur_blocks[send_row_index, :, send_col_index, :]  16.1 us
    all_to_all x1, starting transfers between devices, per_device(): lax.all_to_all(outgoing.reshape(-1, per_row * per_col, BLOCK_EXTENT, BLOC...  12.9 us
    dot_general x1, matrix products, per_device(): update = lax.dot_general(row_factor, column_factor, dims, precision=highest)  12.1 us
    unnamed x31, local copies, waits for them, and re-layouts  12 us
  transfers between devices with their start and end apart: 4, of which 3 were waited for; matrix products, arithmetic and copies ran while one was open for 57% of the time, Pallas kernels for 0%

profile of v3, /device:TPU:10, one launch (start us, length us, event | category | flops | bytes accessed | tf_op | source)
XLA Modules:
  0.0 530.7 jit_solution(14542223603125577747)
XLA Ops:
  21.0 11.7 %cholesky.134 = f32[128,128]{1,0:T(8,128)S(1)} custom-call(f32[128,128]{1,0:T(8,128)S(1)} %fusion.69), custom_call_target="Cholesky" | custom-call | tf_op jit(solution)/shard_map/jit(cholesky)/cholesky | solution.py:44
  34.1 9.8 %custom-call.14 = f32[1,128,128]{1,2,0:T(8,128)S(1)} custom-call(f32[1,128,128]{2,1,0:T(8,128)S(1)} %get-tuple-element.45), custom_call_target="InvertDiagBlocksLowerTriangular" | custom-call | tf_op jit(solution)/shard_map/triangular_solve/custom-call.0 | solution.py:45
  45.4 11.7 %cholesky.145 = f32[128,128]{1,0:T(8,128)S(1)} custom-call(f32[128,128]{1,0:T(8,128)S(1)} %fusion.67), custom_call_target="Cholesky" | custom-call | tf_op jit(solution)/shard_map/jit(cholesky)/cholesky | solution.py:44
  58.5 9.9 %custom-call.15 = f32[1,128,128]{1,2,0:T(8,128)S(1)} custom-call(f32[1,128,128]{2,1,0:T(8,128)S(1)} %get-tuple-element.43), custom_call_target="InvertDiagBlocksLowerTriangular" | custom-call | tf_op jit(solution)/shard_map/triangular_solve/custom-call.0 | solution.py:45
  69.8 11.7 %cholesky.156 = f32[128,128]{1,0:T(8,128)S(1)} custom-call(f32[128,128]{1,0:T(8,128)S(1)} %fusion.65), custom_call_target="Cholesky" | custom-call | tf_op jit(solution)/shard_map/jit(cholesky)/cholesky | solution.py:44
  82.9 9.8 %custom-call.16 = f32[1,128,128]{1,2,0:T(8,128)S(1)} custom-call(f32[1,128,128]{2,1,0:T(8,128)S(1)} %fusion.44), custom_call_target="InvertDiagBlocksLowerTriangular" | custom-call | tf_op jit(solution)/shard_map/triangular_solve/custom-call.0 | solution.py:45
  93.7 12.1 %cholesky.167 = f32[128,128]{1,0:T(8,128)S(1)} custom-call(f32[128,128]{1,0:T(8,128)S(1)} %fusion.63), custom_call_target="Cholesky" | custom-call | tf_op jit(solution)/shard_map/jit(cholesky)/cholesky | solution.py:44
  107.1 9.8 %custom-call.17 = f32[1,128,128]{1,2,0:T(8,128)S(1)} custom-call(f32[1,128,128]{2,1,0:T(8,128)S(1)} %fusion.45), custom_call_target="InvertDiagBlocksLowerTriangular" | custom-call | tf_op jit(solution)/shard_map/triangular_solve/custom-call.0 | solution.py:45
  129.2 11.1 %all-gather.3.cloned.1.call-done = f32[24,1,1,1,128,512]{5,4,3,2,1,0:T(8,128)} async-done(((f32[24,1,1,1,8,512]{5,4,3,2,1,0:T(8,128)}), f32[24,1,1,1,128,512]{5,4,3,2,1,0:T(8,128)}) %all-gather.3.cloned.1.call-update) | async-done | bytes 6291472 | tf_op jit(solution)/shard_map/all_gather | solution.py:97
  152.2 17.7 %fusion = f32[256,8,8,128]{3,1,2,0:T(8,128)S(1)} fusion(f32[256,8,8,128]{3,2,1,0:T(8,128)} %bitcast.247, f32[512,2048]{1,0:T(8,128)S(1)} %copy-done.1, f32[1024,512]{1,0:T(8,128)S(1)} %fusion.2), kind=kOutput, calls=%fused_computation.4 | convolution fusion | flops 6444548096 | bytes 23068672 | tf_op jit(solution)/shard_map/dot_general | solution.py:116
  176.7 16.1 %gather_fusion = f32[256,128,128]{2,1,0:T(8,128)} fusion(f32[16,128,8,128]{3,1,2,0:T(8,128)} %copy.137, s32[256]{0:T(256)S(1)} %reshape.464), kind=kCustom, calls=%fused_computation | custom fusion | bytes 33556480 | tf_op jit(solution)/shard_map/gather | solution.py:153
  200.2 12.9 %all-to-all-start = ((f32[128,2,128,128]{3,2,1,0:T(8,128)}), f32[128,2,128,128]{3,2,1,0:T(8,128)}, u32[]{:S(2)}, u32[]{:S(2)}) async-start(f32[128,2,128,128]{3,2,1,0:T(8,128)} %bitcast.236), calls=%async_computation | async-start | bytes 33554432 | tf_op jit(solution)/shard_map/all_to_all | solution.py:165
  216.6 11.7 %cholesky.178 = f32[128,128]{1,0:T(8,128)S(1)} custom-call(f32[128,128]{1,0:T(8,128)S(1)} %fusion.61), custom_call_target="Cholesky" | custom-call | tf_op jit(solution)/shard_map/jit(cholesky)/cholesky | solution.py:44
  229.7 9.8 %custom-call.18 = f32[1,128,128]{1,2,0:T(8,128)S(1)} custom-call(f32[1,128,128]{2,1,0:T(8,128)S(1)} %get-tuple-element.37), custom_call_target="InvertDiagBlocksLowerTriangular" | custom-call | tf_op jit(solution)/shard_map/triangular_solve/custom-call.0 | solution.py:45
  243.5 11.9 %cholesky.189 = f32[128,128]{1,0:T(8,128)S(1)} custom-call(f32[128,128]{1,0:T(8,128)S(1)} %fusion.59), custom_call_target="Cholesky" | custom-call | tf_op jit(solution)/shard_map/jit(cholesky)/cholesky | solution.py:44
  256.7 9.8 %custom-call.19 = f32[1,128,128]{1,2,0:T(8,128)S(1)} custom-call(f32[1,128,128]{2,1,0:T(8,128)S(1)} %get-tuple-element.35), custom_call_target="InvertDiagBlocksLowerTriangular" | custom-call | tf_op jit(solution)/shard_map/triangular_solve/custom-call.0 | solution.py:45
  269.6 11.7 %cholesky.200 = f32[128,128]{1,0:T(8,128)S(1)} custom-call(f32[128,128]{1,0:T(8,128)S(1)} %fusion.57), custom_call_target="Cholesky" | custom-call | tf_op jit(solution)/shard_map/jit(cholesky)/cholesky | solution.py:44
  283.3 9.8 %custom-call.20 = f32[1,128,128]{1,2,0:T(8,128)S(1)} custom-call(f32[1,128,128]{2,1,0:T(8,128)S(1)} %get-tuple-element.33), custom_call_target="InvertDiagBlocksLowerTriangular" | custom-call | tf_op jit(solution)/shard_map/triangular_solve/custom-call.0 | solution.py:45
  294.1 11.9 %cholesky.211 = f32[128,128]{1,0:T(8,128)S(1)} custom-call(f32[128,128]{1,0:T(8,128)S(1)} %fusion.55), custom_call_target="Cholesky" | custom-call | tf_op jit(solution)/shard_map/jit(cholesky)/cholesky | solution.py:44
  308.0 9.8 %custom-call.21 = f32[1,128,128]{1,2,0:T(8,128)S(1)} custom-call(f32[1,128,128]{2,1,0:T(8,128)S(1)} %get-tuple-element.31), custom_call_target="InvertDiagBlocksLowerTriangular" | custom-call | tf_op jit(solution)/shard_map/triangular_solve/custom-call.0 | solution.py:45
  325.0 11.5 %fusion.106 = f32[3072,512]{1,0:T(8,128)S(1)} fusion(f32[3072,512]{1,0:T(8,128)S(1)} %bitcast.243, f32[256,256]{1,0:T(8,128)S(1)} %select_maximum_fusion.7, f32[128,128]{1,0:T(8,128)S(1)} %copy.153, f32[128,128]{1,0:T(8,128)S(1)} %convolution_negate_fusion.2, f32[128,256]{1,0:T(8,128)S(1)} %concatenate.99, f32[256,256]{1,0:T(8,128)S(1)} %convolution_negate_fusion), kind=kOutput, calls=%fused_computation.238 | convolution fusion | flops 9665249280 | bytes 13369344 | tf_op jit(solution)/shard_map/dot_general | solution.py:160
  336.6 12.1 %fusion.118 = f32[3072,512]{1,0:T(8,128)} fusion(f32[3072,512]{1,0:T(8,128)S(1)} %fusion.106, f32[512,512]{1,0:T(8,128)S(1)} %fusion.105), kind=kOutput, calls=%fused_computation.245 | convolution fusion | flops 9663676416 | bytes 13631488 | tf_op jit(solution)/shard_map/dot_general | solution.py:164
  359.2 130.7 %all-to-all-done = f32[128,2,128,128]{3,2,1,0:T(8,128)} async-done(((f32[128,2,128,128]{3,2,1,0:T(8,128)}), f32[128,2,128,128]{3,2,1,0:T(8,128)}, u32[]{:S(2)}, u32[]{:S(2)}) %all-to-all-start) | async-done | bytes 16777248 | tf_op jit(solution)/shard_map/all_to_all | solution.py:165
  489.9 9.4 %gather_fusion.2 = f32[96,128,128]{2,1,0:T(8,128)} fusion(f32[256,128,128]{2,1,0:T(8,128)} %bitcast.27, s32[1024]{0:T(1024)S(1)} %pad_clamp_fusion), kind=kCustom, calls=%fused_computation.2 | custom fusion | bytes 12583296 | tf_op jit(solution)/shard_map/jit(_take)/gather | solution.py:184
  (206 shorter events, 120.8 us)
Async XLA Ops:
  7.2 133.2 %all-gather.3.cloned.1.call-start = ((), (), s32[]{:S(2)}) async-start(), calls=%async_computation.1 | async-start | bytes 6684672 | tf_op jit(solution)/shard_map/all_gather | solution.py:97
  11.0 116.1 %collective-permute-start = (f32[8,128,512]{2,1,0:T(8,128)}, f32[8,128,512]{2,1,0:T(8,128)}, u32[]{:S(2)}, u32[]{:S(2)}) collective-permute-start(f32[8,128,512]{2,1,0:T(8,128)} %slice_bitcast_fusion), channel_id=1, source_target_pairs={{1,8},{2,16},{3,24},{4,32},{5,40},{6,48},{7,56},{8,1},{10,17},{11,... | collective-permute-start | bytes 6291464 | tf_op jit(solution)/shard_map/ppermute | solution.py:93
  117.4 9.7 %copy-start = (f32[1,16,1,128,512]{4,3,2,1,0:T(8,128)S(1)}, f32[1,16,1,128,512]{4,3,2,1,0:T(8,128)}, u32[]{:S(2)}) copy-start(f32[1,16,1,128,512]{4,3,2,1,0:T(8,128)} %param.10) | copy-start | bytes 12582916
  140.4 11.8 %copy-start.1 = (f32[512,2048]{1,0:T(8,128)S(1)}, f32[512,2048]{1,0:T(8,128)}, u32[]{:S(2)}) copy-start(f32[512,2048]{1,0:T(8,128)} %fusion.3) | copy-start | bytes 12582916
  142.4 9.8 %copy-start.2 = (f32[8,1,1,1,128,512]{5,4,3,2,1,0:T(8,128)}, f32[8,1,1,1,128,512]{5,4,3,2,1,0:T(8,128)S(1)}, u32[]{:S(2)}) copy-start(f32[8,1,1,1,128,512]{5,4,3,2,1,0:T(8,128)S(1)} %slice.154) | copy-start | bytes 6291460
  143.5 54.2 %collective-permute-start.1 = (f32[4,128,512]{2,1,0:T(8,128)}, f32[4,128,512]{2,1,0:T(8,128)}, u32[]{:S(2)}, u32[]{:S(2)}) collective-permute-start(f32[4,128,512]{2,1,0:T(8,128)} %dynamic-slice_bitcast_fusion), channel_id=1, source_target_pairs={{1,8},{2,16},{3,24},{4,32},{5,40},{6,48},{7,56},{8,1},{10,17},{11,... | collective-permute-start | bytes 3145736 | tf_op jit(solution)/shard_map/ppermute | solution.py:106
  176.7 21.1 %copy-start.3 = (f32[8,1,1,1,128,512]{5,4,3,2,1,0:T(8,128)S(1)}, f32[8,1,1,1,128,512]{5,4,3,2,1,0:T(8,128)}, u32[]{:S(2)}) copy-start(f32[8,1,1,1,128,512]{5,4,3,2,1,0:T(8,128)} %copy-done.2) | copy-start | bytes 6291460
  200.2 12.9 %copy-start.11 = (s32[2,128]{1,0:T(2,128)S(1)}, s32[2,128]{1,0:T(2,128)}, u32[]{:S(2)}) copy-start(s32[2,128]{1,0:T(2,128)} %param.14) | copy-start | bytes 3076
  200.2 16.0 %copy-start.5 = (f32[512,512]{1,0:T(8,128)S(1)}, f32[512,512]{1,0:T(8,128)}, u32[]{:S(2)}) copy-start(f32[512,512]{1,0:T(8,128)} %param.12) | copy-start | bytes 3145732
  200.2 289.8 %all-to-all-start = ((f32[128,2,128,128]{3,2,1,0:T(8,128)}), f32[128,2,128,128]{3,2,1,0:T(8,128)}, u32[]{:S(2)}, u32[]{:S(2)}) async-start(f32[128,2,128,128]{3,2,1,0:T(8,128)} %bitcast.236), calls=%async_computation | async-start | bytes 33554432 | tf_op jit(solution)/shard_map/all_to_all | solution.py:165
  216.5 108.5 %slice-start = ((s8[6291456]{0:T(1024)(128)(4,1)}), s8[2097152]{0:T(1024)(128)(4,1)S(1)}, s32[]{:S(2)}) async-start(s8[6291456]{0:T(1024)(128)(4,1)} %bitcast.241), calls=%async_computation.2 | async-start | bytes 4194304
  241.7 0.8 copy-start.4
  318.2 6.9 %slice-start.1 = ((s8[6291456]{0:T(1024)(128)(4,1)}), s8[4194304]{0:T(1024)(128)(4,1)S(1)}, s32[]{:S(2)}) async-start(s8[6291456]{0:T(1024)(128)(4,1)} %bitcast.241), calls=%async_computation.3 | async-start | bytes 8388608
  318.7 17.8 %copy-start.6 = (f32[256,256]{1,0:T(8,128)}, f32[256,256]{1,0:T(8,128)S(1)}, u32[]{:S(2)}) copy-start(f32[256,256]{1,0:T(8,128)S(1)} %select_maximum_fusion.7) | copy-start | bytes 786436
  348.6 7.8 %copy-start.8 = (f32[512,128]{1,0:T(8,128)S(1)}, f32[512,128]{1,0:T(8,128)}, u32[]{:S(2)}) copy-start(f32[512,128]{1,0:T(8,128)} %get-tuple-element.53) | copy-start | bytes 786436
  348.6 7.8 %copy-start.10 = (f32[128,128]{1,0:T(8,128)S(1)}, f32[128,128]{1,0:T(8,128)}, u32[]{:S(2)}) copy-start(f32[128,128]{1,0:T(8,128)} %get-tuple-element.32) | copy-start | bytes 196612
  348.6 8.9 %copy-start.7 = (f32[256,256]{1,0:T(8,128)S(1)}, f32[256,256]{1,0:T(8,128)}, u32[]{:S(2)}) copy-start(f32[256,256]{1,0:T(8,128)} %copy-done.6) | copy-start | bytes 786436
  348.6 8.9 %copy-start.9 = (f32[24,1,1,1,8,512]{5,4,3,2,1,0:T(8,128)S(1)}, f32[24,1,1,1,8,512]{5,4,3,2,1,0:T(8,128)}, u32[]{:S(2)}) copy-start(f32[24,1,1,1,8,512]{5,4,3,2,1,0:T(8,128)} %param.13) | copy-start | bytes 1179652
Sparse Core Ops, SparseCore 0:
  9.7 130.6 all-gather.2

commit v4 on v3

--- a/solution.py
+++ b/solution.py
@@ -151,9 +151,7 @@
     send_row_index = jnp.minimum(send_rows, row_local - 1)[None, :, None, :, None]
     send_col_index = jnp.minimum(send_cols, col_local - 1).reshape(2, row_size, per_col)[:, None, :, None, :]
     outgoing = schur_blocks[send_row_index, :, send_col_index, :]
-    outgoing, gathered, parent_col_rows, parent_diag = lax.optimization_barrier(
-        (outgoing, gathered, parent_col_rows, parent_diag)
-    )
+    outgoing, gathered, parent_diag = lax.optimization_barrier((outgoing, gathered, parent_diag))
     pivot_lower_factor, parent_inv = factor_and_inverse(parent_diag, BLOCK_EXTENT)
     solved = lax.dot_general(own_rows, parent_inv, dims, precision=highest)
     parent_factor = solved.reshape(parent_lead_panel.shape)

time: 540 us -> 573 us (1.061)
  the two profiles are of different devices: /device:TPU:10 before, /device:TPU:44 now
where the time goes in v4:
time: 573 us; the launch traced here: 564 us
  other arithmetic  203 us (35%)
  waiting for transfers between devices  184 us (32%)
  local copies, waits for them, and re-layouts  72.1 us (13%)
  matrix products  63.6 us (11%)
  starting transfers between devices  25.7 us (4%)
  between operations  15.3 us (3%)
    ppermute x1, waiting for transfers between devices, per_device(): lax.ppermute(offered, ('row', 'col'), transpose_perm)  184 us
    another operation x24, other arithmetic, factor_and_inverse(): low = jnp.linalg.cholesky(work[:leaf, :leaf])  99.6 us
    another operation x16, other arithmetic, factor_and_inverse(): inv = lax.linalg.triangular_solve(low, eye, left_side=True, lower=True)  86 us
    all_to_all x1, starting transfers between devices, per_device(): lax.all_to_all(outgoing.reshape(-1, per_row * per_col, BLOCK_EXTENT, BLOC...  20 us
    gather x1, local copies, waits for them, and re-layouts, per_device(): outgoing = schur_blocks[send_row_index, :, send_col_index, :]  16 us
    dot_general x1, matrix products, per_device(): lax.dot_general(child_factor, child_columns, dims, precision=high)  15.5 us
    unnamed x23, local copies, waits for them, and re-layouts  13.3 us
    dot_general x1, matrix products, per_device(): update = lax.dot_general(row_factor, column_factor, dims, precision=highest)  12.3 us
  transfers between devices with their start and end apart: 4, of which 1 were waited for; matrix products, arithmetic and copies ran while one was open for 54% of the time, Pallas kernels for 0%

profile of v4, /device:TPU:44, one launch (start us, length us, event | category | flops | bytes accessed | tf_op | source)
XLA Modules:
  0.0 564.0 jit_solution(5940967338981305074)
XLA Ops:
  19.0 11.7 %cholesky.134 = f32[128,128]{1,0:T(8,128)S(1)} custom-call(f32[128,128]{1,0:T(8,128)S(1)} %fusion.69), custom_call_target="Cholesky" | custom-call | tf_op jit(solution)/shard_map/jit(cholesky)/cholesky | solution.py:44
  32.1 9.8 %custom-call.14 = f32[1,128,128]{1,2,0:T(8,128)S(1)} custom-call(f32[1,128,128]{2,1,0:T(8,128)S(1)} %get-tuple-element.43), custom_call_target="InvertDiagBlocksLowerTriangular" | custom-call | tf_op jit(solution)/shard_map/triangular_solve/custom-call.0 | solution.py:45
  43.4 11.7 %cholesky.145 = f32[128,128]{1,0:T(8,128)S(1)} custom-call(f32[128,128]{1,0:T(8,128)S(1)} %fusion.67), custom_call_target="Cholesky" | custom-call | tf_op jit(solution)/shard_map/jit(cholesky)/cholesky | solution.py:44
  56.5 10.2 %custom-call.15 = f32[1,128,128]{1,2,0:T(8,128)S(1)} custom-call(f32[1,128,128]{2,1,0:T(8,128)S(1)} %get-tuple-element.41), custom_call_target="InvertDiagBlocksLowerTriangular" | custom-call | tf_op jit(solution)/shard_map/triangular_solve/custom-call.0 | solution.py:45
  68.1 11.7 %cholesky.156 = f32[128,128]{1,0:T(8,128)S(1)} custom-call(f32[128,128]{1,0:T(8,128)S(1)} %fusion.65), custom_call_target="Cholesky" | custom-call | tf_op jit(solution)/shard_map/jit(cholesky)/cholesky | solution.py:44
  81.1 9.8 %custom-call.16 = f32[1,128,128]{1,2,0:T(8,128)S(1)} custom-call(f32[1,128,128]{2,1,0:T(8,128)S(1)} %fusion.44), custom_call_target="InvertDiagBlocksLowerTriangular" | custom-call | tf_op jit(solution)/shard_map/triangular_solve/custom-call.0 | solution.py:45
  92.0 11.9 %cholesky.167 = f32[128,128]{1,0:T(8,128)S(1)} custom-call(f32[128,128]{1,0:T(8,128)S(1)} %fusion.63), custom_call_target="Cholesky" | custom-call | tf_op jit(solution)/shard_map/jit(cholesky)/cholesky | solution.py:44
  105.2 9.8 %custom-call.17 = f32[1,128,128]{1,2,0:T(8,128)S(1)} custom-call(f32[1,128,128]{2,1,0:T(8,128)S(1)} %fusion.45), custom_call_target="InvertDiagBlocksLowerTriangular" | custom-call | tf_op jit(solution)/shard_map/triangular_solve/custom-call.0 | solution.py:45
  127.6 15.5 %fusion = f32[256,8,8,128]{3,1,2,0:T(8,128)S(1)} fusion(f32[256,8,8,128]{3,2,1,0:T(8,128)S(1)} %bitcast.249, f32[512,2048]{1,0:T(8,128)S(1)} %fusion.3, f32[1024,512]{1,0:T(8,128)S(1)} %fusion.2), kind=kOutput, calls=%fused_computation.4 | convolution fusion | flops 6444548096 | bytes 23068672 | tf_op jit(solution)/shard_map/dot_general | solution.py:116
  149.8 16.0 %gather_fusion = f32[256,128,128]{2,1,0:T(8,128)} fusion(f32[16,128,8,128]{3,1,2,0:T(8,128)} %copy.137, s32[256]{0:T(256)S(1)} %reshape.464), kind=kCustom, calls=%fused_computation | custom fusion | bytes 33556480 | tf_op jit(solution)/shard_map/gather | solution.py:153
  165.8 20.0 %all-to-all-start = ((f32[128,2,128,128]{3,2,1,0:T(8,128)}), f32[128,2,128,128]{3,2,1,0:T(8,128)}, u32[]{:S(2)}, u32[]{:S(2)}) async-start(f32[128,2,128,128]{3,2,1,0:T(8,128)} %bitcast.236), calls=%async_computation | async-start | bytes 33554432 | tf_op jit(solution)/shard_map/all_to_all | solution.py:163
  196.2 11.7 %cholesky.178 = f32[128,128]{1,0:T(8,128)S(1)} custom-call(f32[128,128]{1,0:T(8,128)S(1)} %fusion.61), custom_call_target="Cholesky" | custom-call | tf_op jit(solution)/shard_map/jit(cholesky)/cholesky | solution.py:44
  209.3 9.8 %custom-call.18 = f32[1,128,128]{1,2,0:T(8,128)S(1)} custom-call(f32[1,128,128]{2,1,0:T(8,128)S(1)} %get-tuple-element.35), custom_call_target="InvertDiagBlocksLowerTriangular" | custom-call | tf_op jit(solution)/shard_map/triangular_solve/custom-call.0 | solution.py:45
  222.2 11.7 %cholesky.189 = f32[128,128]{1,0:T(8,128)S(1)} custom-call(f32[128,128]{1,0:T(8,128)S(1)} %fusion.59), custom_call_target="Cholesky" | custom-call | tf_op jit(solution)/shard_map/jit(cholesky)/cholesky | solution.py:44
  235.7 10.0 %custom-call.19 = f32[1,128,128]{1,2,0:T(8,128)S(1)} custom-call(f32[1,128,128]{2,1,0:T(8,128)S(1)} %get-tuple-element.33), custom_call_target="InvertDiagBlocksLowerTriangular" | custom-call | tf_op jit(solution)/shard_map/triangular_solve/custom-call.0 | solution.py:45
  248.8 11.7 %cholesky.200 = f32[128,128]{1,0:T(8,128)S(1)} custom-call(f32[128,128]{1,0:T(8,128)S(1)} %fusion.57), custom_call_target="Cholesky" | custom-call | tf_op jit(solution)/shard_map/jit(cholesky)/cholesky | solution.py:44
  262.4 9.8 %custom-call.20 = f32[1,128,128]{1,2,0:T(8,128)S(1)} custom-call(f32[1,128,128]{2,1,0:T(8,128)S(1)} %get-tuple-element.31), custom_call_target="InvertDiagBlocksLowerTriangular" | custom-call | tf_op jit(solution)/shard_map/triangular_solve/custom-call.0 | solution.py:45
  273.2 12.1 %cholesky.211 = f32[128,128]{1,0:T(8,128)S(1)} custom-call(f32[128,128]{1,0:T(8,128)S(1)} %fusion.55), custom_call_target="Cholesky" | custom-call | tf_op jit(solution)/shard_map/jit(cholesky)/cholesky | solution.py:44
  287.3 9.8 %custom-call.21 = f32[1,128,128]{1,2,0:T(8,128)S(1)} custom-call(f32[1,128,128]{2,1,0:T(8,128)S(1)} %get-tuple-element.29), custom_call_target="InvertDiagBlocksLowerTriangular" | custom-call | tf_op jit(solution)/shard_map/triangular_solve/custom-call.0 | solution.py:45
  305.3 11.2 %fusion.106 = f32[3072,512]{1,0:T(8,128)S(1)} fusion(f32[3072,512]{1,0:T(8,128)S(1)} %bitcast.243, f32[256,256]{1,0:T(8,128)S(1)} %select_maximum_fusion.7, f32[128,128]{1,0:T(8,128)S(1)} %copy.153, f32[128,128]{1,0:T(8,128)S(1)} %convolution_negate_fusion.2, f32[128,256]{1,0:T(8,128)S(1)} %concatenate.99, f32[256,256]{1,0:T(8,128)S(1)} %convolution_negate_fusion), kind=kOutput, calls=%fused_computation.238 | convolution fusion | flops 9665249280 | bytes 13369344 | tf_op jit(solution)/shard_map/dot_general | solution.py:158
  316.5 183.6 %collective-permute-done.1 = f32[4,128,512]{2,1,0:T(8,128)} collective-permute-done((f32[4,128,512]{2,1,0:T(8,128)}, f32[4,128,512]{2,1,0:T(8,128)}, u32[]{:S(2)}, u32[]{:S(2)}) %collective-permute-start.1) | collective-permute-done | bytes 1048608 | tf_op jit(solution)/shard_map/ppermute | solution.py:106
  503.5 12.3 %fusion.118 = f32[3072,512]{1,0:T(8,128)} fusion(f32[3072,512]{1,0:T(8,128)S(1)} %fusion.106, f32[512,512]{1,0:T(8,128)S(1)} %fusion.105), kind=kOutput, calls=%fused_computation.245 | convolution fusion | flops 9663676416 | bytes 13631488 | tf_op jit(solution)/shard_map/dot_general | solution.py:162
  523.3 9.4 %gather_fusion.2 = f32[96,128,128]{2,1,0:T(8,128)} fusion(f32[256,128,128]{2,1,0:T(8,128)} %bitcast.25, s32[1024]{0:T(1024)S(1)} %pad_clamp_fusion), kind=kCustom, calls=%fused_computation.2 | custom fusion | bytes 12583296 | tf_op jit(solution)/shard_map/jit(_take)/gather | solution.py:182
  532.7 9.4 %gather_fusion.1 = f32[96,128,128]{2,1,0:T(8,128)} fusion(f32[256,128,128]{2,1,0:T(8,128)} %bitcast.25, s32[1024]{0:T(1024)S(1)} %pad_clamp_fusion.1), kind=kCustom, calls=%fused_computation.1 | custom fusion | bytes 12583296 | tf_op jit(solution)/shard_map/jit(_take)/gather | solution.py:181
  (199 shorter events, 98.1 us)
Async XLA Ops:
  7.2 158.6 %all-gather.3.cloned.1.call-start = ((), (), s32[]{:S(2)}) async-start(), calls=%async_computation.1 | async-start | bytes 6684672 | tf_op jit(solution)/shard_map/all_gather | solution.py:97
  11.0 112.4 %collective-permute-start = (f32[8,128,512]{2,1,0:T(8,128)}, f32[8,128,512]{2,1,0:T(8,128)}, u32[]{:S(2)}, u32[]{:S(2)}) collective-permute-start(f32[8,128,512]{2,1,0:T(8,128)} %slice_bitcast_fusion), channel_id=1, source_target_pairs={{1,8},{2,16},{3,24},{4,32},{5,40},{6,48},{7,56},{8,1},{10,17},{11,... | collective-permute-start | bytes 6291464 | tf_op jit(solution)/shard_map/ppermute | solution.py:93
  115.5 7.9 %copy-start = (f32[1,16,1,128,512]{4,3,2,1,0:T(8,128)S(1)}, f32[1,16,1,128,512]{4,3,2,1,0:T(8,128)}, u32[]{:S(2)}) copy-start(f32[1,16,1,128,512]{4,3,2,1,0:T(8,128)} %param.10) | copy-start | bytes 12582916
  117.6 9.9 %slice-start.2 = ((s8[8388608]{0:T(1024)(128)(4,1)}), s8[4194304]{0:T(1024)(128)(4,1)S(1)}, s32[]{:S(2)}) async-start(s8[8388608]{0:T(1024)(128)(4,1)} %bitcast.247), calls=%async_computation.4 | async-start | bytes 8388608
  123.3 4.2 slice-start.3
  165.8 20.0 %copy-start.5 = (s32[2,128]{1,0:T(2,128)S(1)}, s32[2,128]{1,0:T(2,128)}, u32[]{:S(2)}) copy-start(s32[2,128]{1,0:T(2,128)} %param.14) | copy-start | bytes 3076
  165.8 357.4 %all-to-all-start = ((f32[128,2,128,128]{3,2,1,0:T(8,128)}), f32[128,2,128,128]{3,2,1,0:T(8,128)}, u32[]{:S(2)}, u32[]{:S(2)}) async-start(f32[128,2,128,128]{3,2,1,0:T(8,128)} %bitcast.236), calls=%async_computation | async-start | bytes 33554432 | tf_op jit(solution)/shard_map/all_to_all | solution.py:163
  185.8 9.9 %copy-start.4 = (f32[512,512]{1,0:T(8,128)S(1)}, f32[512,512]{1,0:T(8,128)}, u32[]{:S(2)}) copy-start(f32[512,512]{1,0:T(8,128)} %param.12) | copy-start | bytes 3145732
  190.3 1.3 copy-start.1
  192.7 307.4 %collective-permute-start.1 = (f32[4,128,512]{2,1,0:T(8,128)}, f32[4,128,512]{2,1,0:T(8,128)}, u32[]{:S(2)}, u32[]{:S(2)}) collective-permute-start(f32[4,128,512]{2,1,0:T(8,128)} %dynamic-slice_bitcast_fusion), channel_id=1, source_target_pairs={{1,8},{2,16},{3,24},{4,32},{5,40},{6,48},{7,56},{8,1},{10,17},{11,... | collective-permute-start | bytes 3145736 | tf_op jit(solution)/shard_map/ppermute | solution.py:106
  219.7 85.5 %slice-start = ((s8[6291456]{0:T(1024)(128)(4,1)}), s8[2097152]{0:T(1024)(128)(4,1)S(1)}, s32[]{:S(2)}) async-start(s8[6291456]{0:T(1024)(128)(4,1)} %bitcast.241), calls=%async_computation.2 | async-start | bytes 4194304
  220.4 0.8 copy-start.3
  298.0 7.3 %slice-start.1 = ((s8[6291456]{0:T(1024)(128)(4,1)}), s8[4194304]{0:T(1024)(128)(4,1)S(1)}, s32[]{:S(2)}) async-start(s8[6291456]{0:T(1024)(128)(4,1)} %bitcast.241), calls=%async_computation.3 | async-start | bytes 8388608
  305.2 194.9 %copy-start.2 = (f32[8,1,1,1,128,512]{5,4,3,2,1,0:T(8,128)S(1)}, f32[8,1,1,1,128,512]{5,4,3,2,1,0:T(8,128)}, u32[]{:S(2)}) copy-start(f32[8,1,1,1,128,512]{5,4,3,2,1,0:T(8,128)} %copy-done.1) | copy-start | bytes 6291460
Sparse Core Ops, SparseCore 0:
  9.7 131.5 all-gather.2

commit v5 on v3

--- a/solution.py
+++ b/solution.py
@@ -100,11 +100,6 @@
         axis=1,
         tiled=True,
     )
-    paired = gathered[: 2 * parent_cols].reshape(parent_cols, 2, BLOCK_EXTENT, panel_width)
-    offered = lax.dynamic_index_in_dim(paired, half_id, axis=1, keepdims=False)
-    parent_col_rows = jnp.where(
-        on_diagonal, offered, lax.ppermute(offered, ("row", "col"), transpose_perm)
-    )
     child_low, child_inv = factor_and_inverse(child_diag[0], BLOCK_EXTENT)
     child_rows = child_panel.reshape(-1, panel_width)
     dims = (((1,), (1,)), ((), ()))
@@ -115,6 +110,12 @@
     )
     schur_part = child_window.reshape(row_local * BLOCK_EXTENT, col_local * BLOCK_EXTENT) - lax.dot_general(
         child_factor, child_columns, dims, precision=high
+    )
+    gathered_late, schur_part = lax.optimization_barrier((gathered, schur_part))
+    paired = gathered_late[: 2 * parent_cols].reshape(parent_cols, 2, BLOCK_EXTENT, panel_width)
+    offered = lax.dynamic_index_in_dim(paired, half_id, axis=1, keepdims=False)
+    parent_col_rows = jnp.where(
+        on_diagonal, offered, lax.ppermute(offered, ("row", "col"), transpose_perm)
     )
     child_map = lax.dynamic_index_in_dim(index_maps, half_id, axis=0, keepdims=False)
     my_rows = lax.dynamic_index_in_dim(

time: 540 us -> 546 us (1.011)
  other arithmetic: 203 us -> 215 us
  waiting for transfers between devices: 147 us -> 155 us
  starting transfers between devices: 24.4 us -> 17.4 us
    ppermute x1, waiting for transfers between devices: 4.94 us -> 23.9 us  [per_device(): lax.ppermute(offered, ('row', 'col'), transpose_perm)]
    another operation x24, other arithmetic: 99.8 us -> 111 us  [factor_and_inverse(): low = jnp.linalg.cholesky(work[:leaf, :leaf])]
    all_gather x1, waiting for transfers between devices: 11.1 us -> 0.01 us  [per_device(): lax.all_gather(parent_lead_panel.reshape(parent_row_blocks, sub_rows, pan...]
    unnamed x31 -> x29, local copies, waits for them, and re-layouts: 12 us -> 15.5 us
  transfers between devices with their start and end apart: 4 -> 4, of which waited for: 3 -> 2; matrix products, arithmetic and copies ran while one was open for 57% -> 58% of each run, Pallas kernels for 0% -> 0%
where the time goes in v5:
time: 546 us; the launch traced here: 542 us
  other arithmetic  215 us (39%)
  waiting for transfers between devices  155 us (28%)
  local copies, waits for them, and re-layouts  73.6 us (13%)
  matrix products  65.5 us (12%)
  starting transfers between devices  17.4 us (3%)
  between operations  15.3 us (3%)
    all_to_all x1, waiting for transfers between devices, per_device(): lax.all_to_all(outgoing.reshape(-1, per_row * per_col, BLOCK_EXTENT, BLOC...  131 us
    another operation x24, other arithmetic, factor_and_inverse(): low = jnp.linalg.cholesky(work[:leaf, :leaf])  111 us
    another operation x16, other arithmetic, factor_and_inverse(): inv = lax.linalg.triangular_solve(low, eye, left_side=True, lower=True)  85.2 us
    ppermute x1, waiting for transfers between devices, per_device(): lax.ppermute(offered, ('row', 'col'), transpose_perm)  23.9 us
    dot_general x1, matrix products, per_device(): lax.dot_general(child_factor, child_columns, dims, precision=high)  16.7 us
    gather x1, local copies, waits for them, and re-layouts, per_device(): outgoing = schur_blocks[send_row_index, :, send_col_index, :]  16 us
    unnamed x29, local copies, waits for them, and re-layouts  15.5 us
    dot_general x1, matrix products, per_device(): update = lax.dot_general(row_factor, column_factor, dims, precision=highest)  12.1 us
  transfers between devices with their start and end apart: 4, of which 2 were waited for; matrix products, arithmetic and copies ran while one was open for 58% of the time, Pallas kernels for 0%

profile of v5, /device:TPU:10, one launch (start us, length us, event | category | flops | bytes accessed | tf_op | source)
XLA Modules:
  0.0 542.0 jit_solution(18003422550287843633)
XLA Ops:
  19.7 11.7 %cholesky.134 = f32[128,128]{1,0:T(8,128)S(1)} custom-call(f32[128,128]{1,0:T(8,128)S(1)} %fusion.68), custom_call_target="Cholesky" | custom-call | tf_op jit(solution)/shard_map/jit(cholesky)/cholesky | solution.py:44
  32.7 9.8 %custom-call.14 = f32[1,128,128]{1,2,0:T(8,128)S(1)} custom-call(f32[1,128,128]{2,1,0:T(8,128)S(1)} %get-tuple-element.49), custom_call_target="InvertDiagBlocksLowerTriangular" | custom-call | tf_op jit(solution)/shard_map/triangular_solve/custom-call.0 | solution.py:45
  44.0 11.7 %cholesky.145 = f32[128,128]{1,0:T(8,128)S(1)} custom-call(f32[128,128]{1,0:T(8,128)S(1)} %fusion.66), custom_call_target="Cholesky" | custom-call | tf_op jit(solution)/shard_map/jit(cholesky)/cholesky | solution.py:44
  57.0 10.0 %custom-call.15 = f32[1,128,128]{1,2,0:T(8,128)S(1)} custom-call(f32[1,128,128]{2,1,0:T(8,128)S(1)} %get-tuple-element.47), custom_call_target="InvertDiagBlocksLowerTriangular" | custom-call | tf_op jit(solution)/shard_map/triangular_solve/custom-call.0 | solution.py:45
  68.4 11.7 %cholesky.156 = f32[128,128]{1,0:T(8,128)S(1)} custom-call(f32[128,128]{1,0:T(8,128)S(1)} %fusion.64), custom_call_target="Cholesky" | custom-call | tf_op jit(solution)/shard_map/jit(cholesky)/cholesky | solution.py:44
  81.4 9.8 %custom-call.16 = f32[1,128,128]{1,2,0:T(8,128)S(1)} custom-call(f32[1,128,128]{2,1,0:T(8,128)S(1)} %fusion.43), custom_call_target="InvertDiagBlocksLowerTriangular" | custom-call | tf_op jit(solution)/shard_map/triangular_solve/custom-call.0 | solution.py:45
  92.2 23.4 %cholesky.167 = f32[128,128]{1,0:T(8,128)S(1)} custom-call(f32[128,128]{1,0:T(8,128)S(1)} %fusion.62), custom_call_target="Cholesky" | custom-call | tf_op jit(solution)/shard_map/jit(cholesky)/cholesky | solution.py:44
  116.9 9.8 %custom-call.17 = f32[1,128,128]{1,2,0:T(8,128)S(1)} custom-call(f32[1,128,128]{2,1,0:T(8,128)S(1)} %fusion.44), custom_call_target="InvertDiagBlocksLowerTriangular" | custom-call | tf_op jit(solution)/shard_map/triangular_solve/custom-call.0 | solution.py:45
  139.8 16.7 %bitcast_subtract_fusion = f32[2048,1024]{1,0:T(8,128)} fusion(f32[256,8,8,128]{3,2,1,0:T(8,128)S(1)} %bitcast.248, f32[512,2048]{1,0:T(8,128)S(1)} %fusion.2, f32[1024,512]{1,0:T(8,128)S(1)} %fusion.1), kind=kOutput, calls=%fused_computation.3 | convolution fusion | flops 6444548096 | bytes 23068672 | tf_op jit(solution)/shard_map/dot_general | solution.py:111
  172.9 16.0 %gather_fusion = f32[256,128,128]{2,1,0:T(8,128)} fusion(f32[16,128,8,128]{3,1,2,0:T(8,128)} %copy.137, s32[256]{0:T(256)S(1)} %reshape.464), kind=kCustom, calls=%fused_computation | custom fusion | bytes 33556480 | tf_op jit(solution)/shard_map/gather | solution.py:154
  188.9 23.9 %collective-permute-done.1 = f32[4,128,512]{2,1,0:T(8,128)} collective-permute-done((f32[4,128,512]{2,1,0:T(8,128)S(1)}, f32[4,128,512]{2,1,0:T(8,128)}, u32[]{:S(2)}, u32[]{:S(2)}) %collective-permute-start.1) | collective-permute-done | bytes 1048608 | tf_op jit(solution)/shard_map/ppermute | solution.py:118
  227.7 11.7 %cholesky.178 = f32[128,128]{1,0:T(8,128)S(1)} custom-call(f32[128,128]{1,0:T(8,128)S(1)} %fusion.60), custom_call_target="Cholesky" | custom-call | tf_op jit(solution)/shard_map/jit(cholesky)/cholesky | solution.py:44
  240.8 9.8 %custom-call.18 = f32[1,128,128]{1,2,0:T(8,128)S(1)} custom-call(f32[1,128,128]{2,1,0:T(8,128)S(1)} %get-tuple-element.41), custom_call_target="InvertDiagBlocksLowerTriangular" | custom-call | tf_op jit(solution)/shard_map/triangular_solve/custom-call.0 | solution.py:45
  254.6 11.9 %cholesky.189 = f32[128,128]{1,0:T(8,128)S(1)} custom-call(f32[128,128]{1,0:T(8,128)S(1)} %fusion.58), custom_call_target="Cholesky" | custom-call | tf_op jit(solution)/shard_map/jit(cholesky)/cholesky | solution.py:44
  267.8 9.8 %custom-call.19 = f32[1,128,128]{1,2,0:T(8,128)S(1)} custom-call(f32[1,128,128]{2,1,0:T(8,128)S(1)} %get-tuple-element.39), custom_call_target="InvertDiagBlocksLowerTriangular" | custom-call | tf_op jit(solution)/shard_map/triangular_solve/custom-call.0 | solution.py:45
  280.8 11.7 %cholesky.200 = f32[128,128]{1,0:T(8,128)S(1)} custom-call(f32[128,128]{1,0:T(8,128)S(1)} %fusion.56), custom_call_target="Cholesky" | custom-call | tf_op jit(solution)/shard_map/jit(cholesky)/cholesky | solution.py:44
  294.5 9.8 %custom-call.20 = f32[1,128,128]{1,2,0:T(8,128)S(1)} custom-call(f32[1,128,128]{2,1,0:T(8,128)S(1)} %get-tuple-element.37), custom_call_target="InvertDiagBlocksLowerTriangular" | custom-call | tf_op jit(solution)/shard_map/triangular_solve/custom-call.0 | solution.py:45
  305.3 12.1 %cholesky.211 = f32[128,128]{1,0:T(8,128)S(1)} custom-call(f32[128,128]{1,0:T(8,128)S(1)} %fusion.54), custom_call_target="Cholesky" | custom-call | tf_op jit(solution)/shard_map/jit(cholesky)/cholesky | solution.py:44
  319.3 9.8 %custom-call.21 = f32[1,128,128]{1,2,0:T(8,128)S(1)} custom-call(f32[1,128,128]{2,1,0:T(8,128)S(1)} %get-tuple-element.35), custom_call_target="InvertDiagBlocksLowerTriangular" | custom-call | tf_op jit(solution)/shard_map/triangular_solve/custom-call.0 | solution.py:45
  336.4 11.3 %fusion.105 = f32[3072,512]{1,0:T(8,128)S(1)} fusion(f32[3072,512]{1,0:T(8,128)S(1)} %bitcast.242, f32[256,256]{1,0:T(8,128)S(1)} %select_maximum_fusion.7, f32[128,128]{1,0:T(8,128)S(1)} %copy.153, f32[128,128]{1,0:T(8,128)S(1)} %convolution_negate_fusion.2, f32[128,256]{1,0:T(8,128)S(1)} %concatenate.99, f32[256,256]{1,0:T(8,128)S(1)} %convolution_negate_fusion), kind=kOutput, calls=%fused_computation.237 | convolution fusion | flops 9665249280 | bytes 13369344 | tf_op jit(solution)/shard_map/dot_general | solution.py:161
  347.7 12.1 %fusion.117 = f32[3072,512]{1,0:T(8,128)} fusion(f32[3072,512]{1,0:T(8,128)S(1)} %fusion.105, f32[512,512]{1,0:T(8,128)S(1)} %fusion.104), kind=kOutput, calls=%fused_computation.244 | convolution fusion | flops 9663676416 | bytes 13631488 | tf_op jit(solution)/shard_map/dot_general | solution.py:165
  370.4 130.9 %all-to-all-done = f32[128,2,128,128]{3,2,1,0:T(8,128)} async-done(((f32[128,2,128,128]{3,2,1,0:T(8,128)}), f32[128,2,128,128]{3,2,1,0:T(8,128)}, u32[]{:S(2)}, u32[]{:S(2)}) %all-to-all-start) | async-done | bytes 16777248 | tf_op jit(solution)/shard_map/all_to_all | solution.py:166
  501.3 9.4 %gather_fusion.2 = f32[96,128,128]{2,1,0:T(8,128)} fusion(f32[256,128,128]{2,1,0:T(8,128)} %bitcast.27, s32[1024]{0:T(1024)S(1)} %pad_clamp_fusion), kind=kCustom, calls=%fused_computation.2 | custom fusion | bytes 12583296 | tf_op jit(solution)/shard_map/jit(_take)/gather | solution.py:185
  510.7 9.4 %gather_fusion.1 = f32[96,128,128]{2,1,0:T(8,128)} fusion(f32[256,128,128]{2,1,0:T(8,128)} %bitcast.27, s32[1024]{0:T(1024)S(1)} %pad_clamp_fusion.1), kind=kCustom, calls=%fused_computation.1 | custom fusion | bytes 12583296 | tf_op jit(solution)/shard_map/jit(_take)/gather | solution.py:184
  (205 shorter events, 112.5 us)
Async XLA Ops:
  7.2 149.3 %all-gather.3.cloned.1.call-start = ((), (), s32[]{:S(2)}) async-start(), calls=%async_computation.1 | async-start | bytes 6684672 | tf_op jit(solution)/shard_map/all_gather | solution.py:97
  11.0 124.6 %collective-permute-start = (f32[8,128,512]{2,1,0:T(8,128)}, f32[8,128,512]{2,1,0:T(8,128)}, u32[]{:S(2)}, u32[]{:S(2)}) collective-permute-start(f32[8,128,512]{2,1,0:T(8,128)} %slice_bitcast_fusion), channel_id=1, source_target_pairs={{1,8},{2,16},{3,24},{4,32},{5,40},{6,48},{7,56},{8,1},{10,17},{11,... | collective-permute-start | bytes 6291464 | tf_op jit(solution)/shard_map/ppermute | solution.py:93
  127.9 7.7 %copy-start = (f32[1,16,1,128,512]{4,3,2,1,0:T(8,128)S(1)}, f32[1,16,1,128,512]{4,3,2,1,0:T(8,128)}, u32[]{:S(2)}) copy-start(f32[1,16,1,128,512]{4,3,2,1,0:T(8,128)} %param.10) | copy-start | bytes 12582916
  130.1 9.7 %slice-start.2 = ((s8[8388608]{0:T(1024)(128)(4,1)}), s8[4194304]{0:T(1024)(128)(4,1)S(1)}, s32[]{:S(2)}) async-start(s8[8388608]{0:T(1024)(128)(4,1)} %bitcast.246), calls=%async_computation.4 | async-start | bytes 8388608
  135.6 4.2 slice-start.3
  158.4 54.4 %collective-permute-start.1 = (f32[4,128,512]{2,1,0:T(8,128)S(1)}, f32[4,128,512]{2,1,0:T(8,128)}, u32[]{:S(2)}, u32[]{:S(2)}) collective-permute-start(f32[4,128,512]{2,1,0:T(8,128)S(1)} %dynamic-slice_bitcast_fusion), channel_id=1, source_target_pairs={{1,8},{2,16},{3,24},{4,32},{5,40},{6,48},{7,56},{8,1},{10,17},{11,... | collective-permute-start | bytes 3145736 | tf_op jit(solution)/shard_map/ppermute | solution.py:118
  215.2 9.2 %copy-start.8 = (s32[2,128]{1,0:T(2,128)S(1)}, s32[2,128]{1,0:T(2,128)}, u32[]{:S(2)}) copy-start(s32[2,128]{1,0:T(2,128)} %param.14) | copy-start | bytes 3076
  215.2 12.0 %copy-start.2 = (f32[512,512]{1,0:T(8,128)S(1)}, f32[512,512]{1,0:T(8,128)}, u32[]{:S(2)}) copy-start(f32[512,512]{1,0:T(8,128)} %param.12) | copy-start | bytes 3145732
  215.2 286.1 %all-to-all-start = ((f32[128,2,128,128]{3,2,1,0:T(8,128)}), f32[128,2,128,128]{3,2,1,0:T(8,128)}, u32[]{:S(2)}, u32[]{:S(2)}) async-start(f32[128,2,128,128]{3,2,1,0:T(8,128)} %bitcast.233), calls=%async_computation | async-start | bytes 33554432 | tf_op jit(solution)/shard_map/all_to_all | solution.py:166
  227.6 108.8 %slice-start = ((s8[6291456]{0:T(1024)(128)(4,1)}), s8[2097152]{0:T(1024)(128)(4,1)S(1)}, s32[]{:S(2)}) async-start(s8[6291456]{0:T(1024)(128)(4,1)} %bitcast.240), calls=%async_computation.2 | async-start | bytes 4194304
  252.8 0.8 copy-start.1
  329.5 6.9 %slice-start.1 = ((s8[6291456]{0:T(1024)(128)(4,1)}), s8[4194304]{0:T(1024)(128)(4,1)S(1)}, s32[]{:S(2)}) async-start(s8[6291456]{0:T(1024)(128)(4,1)} %bitcast.240), calls=%async_computation.3 | async-start | bytes 8388608
  330.0 17.6 %copy-start.3 = (f32[256,256]{1,0:T(8,128)}, f32[256,256]{1,0:T(8,128)S(1)}, u32[]{:S(2)}) copy-start(f32[256,256]{1,0:T(8,128)S(1)} %select_maximum_fusion.7) | copy-start | bytes 786436
  359.7 7.8 %copy-start.5 = (f32[512,128]{1,0:T(8,128)S(1)}, f32[512,128]{1,0:T(8,128)}, u32[]{:S(2)}) copy-start(f32[512,128]{1,0:T(8,128)} %get-tuple-element.57) | copy-start | bytes 786436
  359.7 7.8 %copy-start.7 = (f32[128,128]{1,0:T(8,128)S(1)}, f32[128,128]{1,0:T(8,128)}, u32[]{:S(2)}) copy-start(f32[128,128]{1,0:T(8,128)} %get-tuple-element.36) | copy-start | bytes 196612
  359.7 8.9 %copy-start.4 = (f32[256,256]{1,0:T(8,128)S(1)}, f32[256,256]{1,0:T(8,128)}, u32[]{:S(2)}) copy-start(f32[256,256]{1,0:T(8,128)} %copy-done.3) | copy-start | bytes 786436
  359.7 8.9 %copy-start.6 = (f32[24,1,1,1,8,512]{5,4,3,2,1,0:T(8,128)S(1)}, f32[24,1,1,1,8,512]{5,4,3,2,1,0:T(8,128)}, u32[]{:S(2)}) copy-start(f32[24,1,1,1,8,512]{5,4,3,2,1,0:T(8,128)} %param.13) | copy-start | bytes 1179652
Sparse Core Ops, SparseCore 0:
  9.7 130.5 all-gather.2

commit v6 on v3

--- a/solution.py
+++ b/solution.py
@@ -100,10 +100,13 @@
         axis=1,
         tiled=True,
     )
-    paired = gathered[: 2 * parent_cols].reshape(parent_cols, 2, BLOCK_EXTENT, panel_width)
-    offered = lax.dynamic_index_in_dim(paired, half_id, axis=1, keepdims=False)
-    parent_col_rows = jnp.where(
-        on_diagonal, offered, lax.ppermute(offered, ("row", "col"), transpose_perm)
+    leading_parent = parent_lead_panel.reshape(parent_row_blocks, sub_rows, panel_width)[: 2 * parent_cols]
+    transposed = jnp.where(
+        on_diagonal, leading_parent, lax.ppermute(leading_parent, ("row", "col"), transpose_perm)
+    )
+    column_blocks = lax.all_gather(transposed, ("half", "row"), axis=1, tiled=True)
+    parent_col_rows = lax.dynamic_index_in_dim(
+        column_blocks.reshape(parent_cols, 2, BLOCK_EXTENT, panel_width), half_id, axis=1, keepdims=False
     )
     child_low, child_inv = factor_and_inverse(child_diag[0], BLOCK_EXTENT)
     child_rows = child_panel.reshape(-1, panel_width)

time: 540 us -> 539 us (level)
  waiting for transfers between devices: 147 us -> 157 us
    all_gather x1, waiting for transfers between devices: 11.1 us -> 17.6 us  [per_device(): lax.all_gather(parent_lead_panel.reshape(parent_row_blocks, sub_rows, pan...]
  transfers between devices with their start and end apart: 4 -> 5, of which waited for: 3 -> 3; matrix products, arithmetic and copies ran while one was open for 57% -> 57% of each run, Pallas kernels for 0% -> 0%
where the time goes in v6:
time: 539 us; the launch traced here: 529 us
  other arithmetic  203 us (38%)
  waiting for transfers between devices  157 us (29%)
  local copies, waits for them, and re-layouts  70.5 us (13%)
  matrix products  64.4 us (12%)
  starting transfers between devices  19 us (4%)
  between operations  15.3 us (3%)
    all_to_all x1, waiting for transfers between devices, per_device(): lax.all_to_all(outgoing.reshape(-1, per_row * per_col, BLOCK_EXTENT, BLOC...  131 us
    another operation x24, other arithmetic, factor_and_inverse(): low = jnp.linalg.cholesky(work[:leaf, :leaf])  100 us
    another operation x16, other arithmetic, factor_and_inverse(): inv = lax.linalg.triangular_solve(low, eye, left_side=True, lower=True)  85.2 us
    all_gather x1, waiting for transfers between devices, per_device(): lax.all_gather(parent_lead_panel.reshape(parent_row_blocks, sub_rows, pan...  17.6 us
    gather x1, local copies, waits for them, and re-layouts, per_device(): outgoing = schur_blocks[send_row_index, :, send_col_index, :]  16.2 us
    dot_general x1, matrix products, per_device(): lax.dot_general(child_factor, child_columns, dims, precision=high)  15.4 us
    dot_general x1, matrix products, per_device(): update = lax.dot_general(row_factor, column_factor, dims, precision=highest)  12.1 us
    dot_general x1, matrix products, per_device(): lax.dot_general(gathered.reshape(-1, panel_width), parent_inv, dims, prec...  11.3 us
  transfers between devices with their start and end apart: 5, of which 3 were waited for; matrix products, arithmetic and copies ran while one was open for 57% of the time, Pallas kernels for 0%

profile of v6, /device:TPU:10, one launch (start us, length us, event | category | flops | bytes accessed | tf_op | source)
XLA Modules:
  0.0 529.2 jit_solution(2536918463805677017)
XLA Ops:
  35.1 11.7 %cholesky.134 = f32[128,128]{1,0:T(8,128)S(1)} custom-call(f32[128,128]{1,0:T(8,128)S(1)} %fusion.69), custom_call_target="Cholesky" | custom-call | tf_op jit(solution)/shard_map/jit(cholesky)/cholesky | solution.py:44
  48.1 9.8 %custom-call.14 = f32[1,128,128]{1,2,0:T(8,128)S(1)} custom-call(f32[1,128,128]{2,1,0:T(8,128)S(1)} %get-tuple-element.45), custom_call_target="InvertDiagBlocksLowerTriangular" | custom-call | tf_op jit(solution)/shard_map/triangular_solve/custom-call.0 | solution.py:45
  59.5 11.7 %cholesky.145 = f32[128,128]{1,0:T(8,128)S(1)} custom-call(f32[128,128]{1,0:T(8,128)S(1)} %fusion.67), custom_call_target="Cholesky" | custom-call | tf_op jit(solution)/shard_map/jit(cholesky)/cholesky | solution.py:44
  72.5 10.1 %custom-call.15 = f32[1,128,128]{1,2,0:T(8,128)S(1)} custom-call(f32[1,128,128]{2,1,0:T(8,128)S(1)} %get-tuple-element.43), custom_call_target="InvertDiagBlocksLowerTriangular" | custom-call | tf_op jit(solution)/shard_map/triangular_solve/custom-call.0 | solution.py:45
  84.0 11.7 %cholesky.156 = f32[128,128]{1,0:T(8,128)S(1)} custom-call(f32[128,128]{1,0:T(8,128)S(1)} %fusion.65), custom_call_target="Cholesky" | custom-call | tf_op jit(solution)/shard_map/jit(cholesky)/cholesky | solution.py:44
  97.1 9.8 %custom-call.16 = f32[1,128,128]{1,2,0:T(8,128)S(1)} custom-call(f32[1,128,128]{2,1,0:T(8,128)S(1)} %fusion.44), custom_call_target="InvertDiagBlocksLowerTriangular" | custom-call | tf_op jit(solution)/shard_map/triangular_solve/custom-call.0 | solution.py:45
  107.9 12.2 %cholesky.167 = f32[128,128]{1,0:T(8,128)S(1)} custom-call(f32[128,128]{1,0:T(8,128)S(1)} %fusion.63), custom_call_target="Cholesky" | custom-call | tf_op jit(solution)/shard_map/jit(cholesky)/cholesky | solution.py:44
  121.4 9.8 %custom-call.17 = f32[1,128,128]{1,2,0:T(8,128)S(1)} custom-call(f32[1,128,128]{2,1,0:T(8,128)S(1)} %fusion.45), custom_call_target="InvertDiagBlocksLowerTriangular" | custom-call | tf_op jit(solution)/shard_map/triangular_solve/custom-call.0 | solution.py:45
  143.7 15.4 %fusion = f32[256,8,8,128]{3,1,2,0:T(8,128)S(1)} fusion(f32[256,8,8,128]{3,2,1,0:T(8,128)S(1)} %bitcast.246, f32[512,2048]{1,0:T(8,128)S(1)} %fusion.3, f32[1024,512]{1,0:T(8,128)S(1)} %fusion.2), kind=kOutput, calls=%fused_computation.4 | convolution fusion | flops 6444548096 | bytes 23068672 | tf_op jit(solution)/shard_map/dot_general | solution.py:119
  165.9 16.2 %gather_fusion = f32[256,128,128]{2,1,0:T(8,128)} fusion(f32[16,128,8,128]{3,1,2,0:T(8,128)} %copy.137, s32[256]{0:T(256)S(1)} %reshape.466), kind=kCustom, calls=%fused_computation | custom fusion | bytes 33556480 | tf_op jit(solution)/shard_map/gather | solution.py:156
  184.4 17.6 %all-gather.6.cloned.1.call-done = f32[24,1,1,1,128,512]{5,4,3,2,1,0:T(8,128)} async-done(((f32[24,1,1,1,8,512]{5,4,3,2,1,0:T(8,128)}), f32[24,1,1,1,128,512]{5,4,3,2,1,0:T(8,128)}) %all-gather.6.cloned.1.call-update) | async-done | bytes 6291472 | tf_op jit(solution)/shard_map/all_gather | solution.py:97
  202.0 9.6 %all-to-all-start = ((f32[128,2,128,128]{3,2,1,0:T(8,128)}), f32[128,2,128,128]{3,2,1,0:T(8,128)}, u32[]{:S(2)}, u32[]{:S(2)}) async-start(f32[128,2,128,128]{3,2,1,0:T(8,128)} %bitcast.238), calls=%async_computation | async-start | bytes 33554432 | tf_op jit(solution)/shard_map/all_to_all | solution.py:168
  214.8 11.7 %cholesky.178 = f32[128,128]{1,0:T(8,128)S(1)} custom-call(f32[128,128]{1,0:T(8,128)S(1)} %fusion.61), custom_call_target="Cholesky" | custom-call | tf_op jit(solution)/shard_map/jit(cholesky)/cholesky | solution.py:44
  227.9 9.8 %custom-call.18 = f32[1,128,128]{1,2,0:T(8,128)S(1)} custom-call(f32[1,128,128]{2,1,0:T(8,128)S(1)} %get-tuple-element.37), custom_call_target="InvertDiagBlocksLowerTriangular" | custom-call | tf_op jit(solution)/shard_map/triangular_solve/custom-call.0 | solution.py:45
  241.7 11.9 %cholesky.189 = f32[128,128]{1,0:T(8,128)S(1)} custom-call(f32[128,128]{1,0:T(8,128)S(1)} %fusion.59), custom_call_target="Cholesky" | custom-call | tf_op jit(solution)/shard_map/jit(cholesky)/cholesky | solution.py:44
  254.9 9.8 %custom-call.19 = f32[1,128,128]{1,2,0:T(8,128)S(1)} custom-call(f32[1,128,128]{2,1,0:T(8,128)S(1)} %get-tuple-element.35), custom_call_target="InvertDiagBlocksLowerTriangular" | custom-call | tf_op jit(solution)/shard_map/triangular_solve/custom-call.0 | solution.py:45
  267.9 11.7 %cholesky.200 = f32[128,128]{1,0:T(8,128)S(1)} custom-call(f32[128,128]{1,0:T(8,128)S(1)} %fusion.57), custom_call_target="Cholesky" | custom-call | tf_op jit(solution)/shard_map/jit(cholesky)/cholesky | solution.py:44
  281.6 9.8 %custom-call.20 = f32[1,128,128]{1,2,0:T(8,128)S(1)} custom-call(f32[1,128,128]{2,1,0:T(8,128)S(1)} %get-tuple-element.33), custom_call_target="InvertDiagBlocksLowerTriangular" | custom-call | tf_op jit(solution)/shard_map/triangular_solve/custom-call.0 | solution.py:45
  292.4 12.1 %cholesky.211 = f32[128,128]{1,0:T(8,128)S(1)} custom-call(f32[128,128]{1,0:T(8,128)S(1)} %fusion.55), custom_call_target="Cholesky" | custom-call | tf_op jit(solution)/shard_map/jit(cholesky)/cholesky | solution.py:44
  306.4 9.8 %custom-call.21 = f32[1,128,128]{1,2,0:T(8,128)S(1)} custom-call(f32[1,128,128]{2,1,0:T(8,128)S(1)} %get-tuple-element.31), custom_call_target="InvertDiagBlocksLowerTriangular" | custom-call | tf_op jit(solution)/shard_map/triangular_solve/custom-call.0 | solution.py:45
  323.5 11.3 %fusion.106 = f32[3072,512]{1,0:T(8,128)S(1)} fusion(f32[3072,512]{1,0:T(8,128)S(1)} %bitcast.249, f32[256,256]{1,0:T(8,128)S(1)} %select_maximum_fusion.7, f32[128,128]{1,0:T(8,128)S(1)} %copy.153, f32[128,128]{1,0:T(8,128)S(1)} %convolution_negate_fusion.2, f32[128,256]{1,0:T(8,128)S(1)} %concatenate.99, f32[256,256]{1,0:T(8,128)S(1)} %convolution_negate_fusion), kind=kOutput, calls=%fused_computation.239 | convolution fusion | flops 9665249280 | bytes 13369344 | tf_op jit(solution)/shard_map/dot_general | solution.py:163
  334.8 12.1 %fusion.118 = f32[3072,512]{1,0:T(8,128)} fusion(f32[3072,512]{1,0:T(8,128)S(1)} %fusion.106, f32[512,512]{1,0:T(8,128)S(1)} %fusion.105), kind=kOutput, calls=%fused_computation.246 | convolution fusion | flops 9663676416 | bytes 13631488 | tf_op jit(solution)/shard_map/dot_general | solution.py:167
  357.5 130.9 %all-to-all-done = f32[128,2,128,128]{3,2,1,0:T(8,128)} async-done(((f32[128,2,128,128]{3,2,1,0:T(8,128)}), f32[128,2,128,128]{3,2,1,0:T(8,128)}, u32[]{:S(2)}, u32[]{:S(2)}) %all-to-all-start) | async-done | bytes 16777248 | tf_op jit(solution)/shard_map/all_to_all | solution.py:168
  488.4 9.4 %gather_fusion.2 = f32[96,128,128]{2,1,0:T(8,128)} fusion(f32[256,128,128]{2,1,0:T(8,128)} %bitcast.28, s32[1024]{0:T(1024)S(1)} %pad_clamp_fusion), kind=kCustom, calls=%fused_computation.2 | custom fusion | bytes 12583296 | tf_op jit(solution)/shard_map/jit(_take)/gather | solution.py:187
  (209 shorter events, 117.9 us)
Async XLA Ops:
  7.2 27.4 %copy-start.6 = (f32[1,512,512]{2,1,0:T(8,128)S(1)}, f32[1,512,512]{2,1,0:T(8,128)}, u32[]{:S(2)}) copy-start(f32[1,512,512]{2,1,0:T(8,128)} %param.9) | copy-start | bytes 3145732
  7.2 174.9 %all-gather.4.cloned.1.call-start = ((), (), s32[]{:S(2)}) async-start(), calls=%async_computation.1 | async-start | bytes 2228224 | tf_op jit(solution)/shard_map/all_gather | solution.py:107
  8.2 12.5 %collective-permute-start.1 = (f32[8,8,512]{2,1,0:T(8,128)S(1)}, f32[8,8,512]{2,1,0:T(8,128)S(1)}, u32[]{:S(2)}, u32[]{:S(2)}) collective-permute-start(f32[8,8,512]{2,1,0:T(8,128)S(1)} %slice_bitcast_fusion.1), channel_id=1, source_target_pairs={{1,8},{2,16},{3,24},{4,32},{5,40},{6,48},{7,56},{8,1},{10,17},{11,... | collective-permute-start | bytes 393224 | tf_op jit(solution)/shard_map/ppermute | solution.py:105
  22.3 179.6 %all-gather.6.cloned.1.call-start = ((), (), s32[]{:S(2)}) async-start(), calls=%async_computation.2 | async-start | bytes 6684672 | tf_op jit(solution)/shard_map/all_gather | solution.py:97
  26.2 113.4 %collective-permute-start = (f32[8,128,512]{2,1,0:T(8,128)}, f32[8,128,512]{2,1,0:T(8,128)}, u32[]{:S(2)}, u32[]{:S(2)}) collective-permute-start(f32[8,128,512]{2,1,0:T(8,128)} %slice_bitcast_fusion), channel_id=1, source_target_pairs={{1,8},{2,16},{3,24},{4,32},{5,40},{6,48},{7,56},{8,1},{10,17},{11,... | collective-permute-start | bytes 6291464 | tf_op jit(solution)/shard_map/ppermute | solution.py:93
  131.7 7.9 %copy-start = (f32[1,16,1,128,512]{4,3,2,1,0:T(8,128)S(1)}, f32[1,16,1,128,512]{4,3,2,1,0:T(8,128)}, u32[]{:S(2)}) copy-start(f32[1,16,1,128,512]{4,3,2,1,0:T(8,128)} %param.10) | copy-start | bytes 12582916
  133.9 9.8 %slice-start = ((s8[8388608]{0:T(1024)(128)(4,1)}), s8[4194304]{0:T(1024)(128)(4,1)S(1)}, s32[]{:S(2)}) async-start(s8[8388608]{0:T(1024)(128)(4,1)} %bitcast.244), calls=%async_computation.3 | async-start | bytes 8388608
  139.5 4.2 slice-start.1
  202.0 9.6 %copy-start.9 = (s32[2,128]{1,0:T(2,128)S(1)}, s32[2,128]{1,0:T(2,128)}, u32[]{:S(2)}) copy-start(s32[2,128]{1,0:T(2,128)} %param.14) | copy-start | bytes 3076
  202.0 12.4 %copy-start.2 = (f32[512,512]{1,0:T(8,128)S(1)}, f32[512,512]{1,0:T(8,128)}, u32[]{:S(2)}) copy-start(f32[512,512]{1,0:T(8,128)} %param.12) | copy-start | bytes 3145732
  202.0 286.4 %all-to-all-start = ((f32[128,2,128,128]{3,2,1,0:T(8,128)}), f32[128,2,128,128]{3,2,1,0:T(8,128)}, u32[]{:S(2)}, u32[]{:S(2)}) async-start(f32[128,2,128,128]{3,2,1,0:T(8,128)} %bitcast.238), calls=%async_computation | async-start | bytes 33554432 | tf_op jit(solution)/shard_map/all_to_all | solution.py:168
  214.7 108.8 %slice-start.2 = ((s8[6291456]{0:T(1024)(128)(4,1)}), s8[2097152]{0:T(1024)(128)(4,1)S(1)}, s32[]{:S(2)}) async-start(s8[6291456]{0:T(1024)(128)(4,1)} %bitcast.247), calls=%async_computation.5 | async-start | bytes 4194304
  239.9 0.8 copy-start.1
  316.6 6.9 %slice-start.3 = ((s8[6291456]{0:T(1024)(128)(4,1)}), s8[4194304]{0:T(1024)(128)(4,1)S(1)}, s32[]{:S(2)}) async-start(s8[6291456]{0:T(1024)(128)(4,1)} %bitcast.247), calls=%async_computation.6 | async-start | bytes 8388608
  317.1 17.6 %copy-start.4 = (f32[256,256]{1,0:T(8,128)}, f32[256,256]{1,0:T(8,128)S(1)}, u32[]{:S(2)}) copy-start(f32[256,256]{1,0:T(8,128)S(1)} %select_maximum_fusion.7) | copy-start | bytes 786436
  346.8 7.8 %copy-start.7 = (f32[512,128]{1,0:T(8,128)S(1)}, f32[512,128]{1,0:T(8,128)}, u32[]{:S(2)}) copy-start(f32[512,128]{1,0:T(8,128)} %get-tuple-element.55) | copy-start | bytes 786436
  346.8 7.8 %copy-start.8 = (f32[128,128]{1,0:T(8,128)S(1)}, f32[128,128]{1,0:T(8,128)}, u32[]{:S(2)}) copy-start(f32[128,128]{1,0:T(8,128)} %get-tuple-element.32) | copy-start | bytes 196612
  346.8 8.9 %copy-start.3 = (f32[24,1,1,1,8,512]{5,4,3,2,1,0:T(8,128)S(1)}, f32[24,1,1,1,8,512]{5,4,3,2,1,0:T(8,128)}, u32[]{:S(2)}) copy-start(f32[24,1,1,1,8,512]{5,4,3,2,1,0:T(8,128)} %param.13) | copy-start | bytes 1179652
  346.8 8.9 %copy-start.5 = (f32[256,256]{1,0:T(8,128)S(1)}, f32[256,256]{1,0:T(8,128)}, u32[]{:S(2)}) copy-start(f32[256,256]{1,0:T(8,128)} %copy-done.4) | copy-start | bytes 786436
Sparse Core Ops, SparseCore 0:
  22.4 136.6 all-gather.3
  160.9 41.0 all-gather.5

commit v7 on v6

--- a/solution.py
+++ b/solution.py
@@ -181,15 +181,17 @@
     )
     slot_of = jnp.sum(jnp.where(match, jnp.arange(slots, dtype=jnp.int32), 0), axis=-1)
     present = jnp.any(match, axis=-1)
-    flat_arrived = arrived.reshape(2 * slots, BLOCK_EXTENT, BLOCK_EXTENT)
-    block_shape = (parent_row_blocks, parent_cols, BLOCK_EXTENT, BLOCK_EXTENT)
-    first = jnp.take(flat_arrived, slot_of[0].reshape(-1), axis=0, mode="clip")
-    second = jnp.take(flat_arrived, slot_of[1].reshape(-1) + slots, axis=0, mode="clip")
-    assembled = jnp.where(present[0, :, :, None, None], first.reshape(block_shape), 0.0) + jnp.where(
-        present[1, :, :, None, None], second.reshape(block_shape), 0.0
-    )
-    updated = assembled.transpose(0, 2, 1, 3) - update.reshape(
-        parent_row_blocks, BLOCK_EXTENT, parent_cols, BLOCK_EXTENT
+    rows_arrived = arrived.reshape(2 * slots * BLOCK_EXTENT, BLOCK_EXTENT)
+    inside = jnp.arange(BLOCK_EXTENT, dtype=jnp.int32)[None, :, None]
+    first_rows = slot_of[0][:, None, :] * BLOCK_EXTENT + inside
+    second_rows = (slot_of[1][:, None, :] + slots) * BLOCK_EXTENT + inside
+    out_shape = (parent_row_blocks, BLOCK_EXTENT, parent_cols, BLOCK_EXTENT)
+    first = jnp.take(rows_arrived, first_rows.reshape(-1), axis=0, mode="clip").reshape(out_shape)
+    second = jnp.take(rows_arrived, second_rows.reshape(-1), axis=0, mode="clip").reshape(out_shape)
+    updated = (
+        jnp.where(present[0][:, None, :, None], first, 0.0)
+        + jnp.where(present[1][:, None, :, None], second, 0.0)
+        - update.reshape(out_shape)
     )
     return (
         updated.reshape(parent_row_blocks, 1, BLOCK_EXTENT, parent_cols, 1, 1, BLOCK_EXTENT),

time: 539 us -> 614 us (1.14)
  local copies, waits for them, and re-layouts: 70.5 us -> 141 us
  other arithmetic: 203 us -> 212 us
    gather x2, local copies, waits for them, and re-layouts: 18.8 us -> 94 us  [the longest x1 47.2 us: per_device(): jnp.take(rows_arrived, first_rows.reshape(-1), axis=0, mode='clip')]
    sub x0 -> x1, other arithmetic: none -> 15.2 us  [per_device(): jnp.where(present[0][:, None, :, None], first, 0.0)]
    unnamed x31 -> x32, local copies, waits for them, and re-layouts: 10.8 us -> 3.29 us
    reshape x1 -> x0, other arithmetic: 7.37 us -> none  [per_device(): updated.reshape(parent_row_blocks, 1, BLOCK_EXTENT, parent_cols, 1, 1, BL...]
  transfers between devices with their start and end apart: 5 -> 5, of which waited for: 3 -> 3; matrix products, arithmetic and copies ran while one was open for 57% -> 50% of each run, Pallas kernels for 0% -> 0%
where the time goes in v7:
time: 614 us; the launch traced here: 605 us
  other arithmetic  212 us (35%)
  waiting for transfers between devices  152 us (25%)
  local copies, waits for them, and re-layouts  141 us (23%)
  matrix products  65.1 us (11%)
  starting transfers between devices  19 us (3%)
  between operations  15.3 us (2%)
    all_to_all x1, waiting for transfers between devices, per_device(): lax.all_to_all(outgoing.reshape(-1, per_row * per_col, BLOCK_EXTENT, BLOC...  126 us
    another operation x24, other arithmetic, factor_and_inverse(): low = jnp.linalg.cholesky(work[:leaf, :leaf])  99.5 us
    another operation x16, other arithmetic, factor_and_inverse(): inv = lax.linalg.triangular_solve(low, eye, left_side=True, lower=True)  85.4 us
    gather x1, local copies, waits for them, and re-layouts, per_device(): jnp.take(rows_arrived, first_rows.reshape(-1), axis=0, mode='clip')  47.2 us
    gather x1, local copies, waits for them, and re-layouts, per_device(): jnp.take(rows_arrived, second_rows.reshape(-1), axis=0, mode='clip')  46.8 us
    all_gather x1, waiting for transfers between devices, per_device(): lax.all_gather(parent_lead_panel.reshape(parent_row_blocks, sub_rows, pan...  17.7 us
    gather x1, local copies, waits for them, and re-layouts, per_device(): outgoing = schur_blocks[send_row_index, :, send_col_index, :]  16.2 us
    dot_general x1, matrix products, per_device(): lax.dot_general(child_factor, child_columns, dims, precision=high)  15.5 us
  transfers between devices with their start and end apart: 5, of which 3 were waited for; matrix products, arithmetic and copies ran while one was open for 50% of the time, Pallas kernels for 0%

profile of v7, /device:TPU:10, one launch (start us, length us, event | category | flops | bytes accessed | tf_op | source)
XLA Modules:
  0.0 604.7 jit_solution(4363272029716927056)
XLA Ops:
  35.1 11.7 %cholesky.134 = f32[128,128]{1,0:T(8,128)S(1)} custom-call(f32[128,128]{1,0:T(8,128)S(1)} %fusion.70), custom_call_target="Cholesky" | custom-call | tf_op jit(solution)/shard_map/jit(cholesky)/cholesky | solution.py:44
  48.1 9.8 %custom-call.14 = f32[1,128,128]{1,2,0:T(8,128)S(1)} custom-call(f32[1,128,128]{2,1,0:T(8,128)S(1)} %get-tuple-element.45), custom_call_target="InvertDiagBlocksLowerTriangular" | custom-call | tf_op jit(solution)/shard_map/triangular_solve/custom-call.0 | solution.py:45
  59.5 11.7 %cholesky.145 = f32[128,128]{1,0:T(8,128)S(1)} custom-call(f32[128,128]{1,0:T(8,128)S(1)} %fusion.68), custom_call_target="Cholesky" | custom-call | tf_op jit(solution)/shard_map/jit(cholesky)/cholesky | solution.py:44
  72.5 10.2 %custom-call.15 = f32[1,128,128]{1,2,0:T(8,128)S(1)} custom-call(f32[1,128,128]{2,1,0:T(8,128)S(1)} %get-tuple-element.43), custom_call_target="InvertDiagBlocksLowerTriangular" | custom-call | tf_op jit(solution)/shard_map/triangular_solve/custom-call.0 | solution.py:45
  84.2 11.7 %cholesky.156 = f32[128,128]{1,0:T(8,128)S(1)} custom-call(f32[128,128]{1,0:T(8,128)S(1)} %fusion.66), custom_call_target="Cholesky" | custom-call | tf_op jit(solution)/shard_map/jit(cholesky)/cholesky | solution.py:44
  97.2 9.8 %custom-call.16 = f32[1,128,128]{1,2,0:T(8,128)S(1)} custom-call(f32[1,128,128]{2,1,0:T(8,128)S(1)} %fusion.45), custom_call_target="InvertDiagBlocksLowerTriangular" | custom-call | tf_op jit(solution)/shard_map/triangular_solve/custom-call.0 | solution.py:45
  108.0 11.9 %cholesky.167 = f32[128,128]{1,0:T(8,128)S(1)} custom-call(f32[128,128]{1,0:T(8,128)S(1)} %fusion.64), custom_call_target="Cholesky" | custom-call | tf_op jit(solution)/shard_map/jit(cholesky)/cholesky | solution.py:44
  121.2 9.8 %custom-call.17 = f32[1,128,128]{1,2,0:T(8,128)S(1)} custom-call(f32[1,128,128]{2,1,0:T(8,128)S(1)} %fusion.46), custom_call_target="InvertDiagBlocksLowerTriangular" | custom-call | tf_op jit(solution)/shard_map/triangular_solve/custom-call.0 | solution.py:45
  143.6 15.5 %fusion = f32[256,8,8,128]{3,1,2,0:T(8,128)S(1)} fusion(f32[256,8,8,128]{3,2,1,0:T(8,128)S(1)} %bitcast.250, f32[512,2048]{1,0:T(8,128)S(1)} %fusion.4, f32[1024,512]{1,0:T(8,128)S(1)} %fusion.3), kind=kOutput, calls=%fused_computation.6 | convolution fusion | flops 6444548096 | bytes 23068672 | tf_op jit(solution)/shard_map/dot_general | solution.py:119
  165.8 16.2 %gather_fusion = f32[256,128,128]{2,1,0:T(8,128)} fusion(f32[16,128,8,128]{3,1,2,0:T(8,128)} %copy.149, s32[256]{0:T(256)S(1)} %reshape.553), kind=kCustom, calls=%fused_computation | custom fusion | bytes 33556480 | tf_op jit(solution)/shard_map/gather | solution.py:156
  184.3 17.7 %all-gather.6.cloned.1.call-done = f32[24,1,1,1,128,512]{5,4,3,2,1,0:T(8,128)} async-done(((f32[24,1,1,1,8,512]{5,4,3,2,1,0:T(8,128)}), f32[24,1,1,1,128,512]{5,4,3,2,1,0:T(8,128)}) %all-gather.6.cloned.1.call-update) | async-done | bytes 6291472 | tf_op jit(solution)/shard_map/all_gather | solution.py:97
  219.7 11.7 %cholesky.178 = f32[128,128]{1,0:T(8,128)S(1)} custom-call(f32[128,128]{1,0:T(8,128)S(1)} %fusion.62), custom_call_target="Cholesky" | custom-call | tf_op jit(solution)/shard_map/jit(cholesky)/cholesky | solution.py:44
  232.7 9.8 %custom-call.18 = f32[1,128,128]{1,2,0:T(8,128)S(1)} custom-call(f32[1,128,128]{2,1,0:T(8,128)S(1)} %get-tuple-element.37), custom_call_target="InvertDiagBlocksLowerTriangular" | custom-call | tf_op jit(solution)/shard_map/triangular_solve/custom-call.0 | solution.py:45
  246.5 11.9 %cholesky.189 = f32[128,128]{1,0:T(8,128)S(1)} custom-call(f32[128,128]{1,0:T(8,128)S(1)} %fusion.60), custom_call_target="Cholesky" | custom-call | tf_op jit(solution)/shard_map/jit(cholesky)/cholesky | solution.py:44
  259.8 9.8 %custom-call.19 = f32[1,128,128]{1,2,0:T(8,128)S(1)} custom-call(f32[1,128,128]{2,1,0:T(8,128)S(1)} %get-tuple-element.35), custom_call_target="InvertDiagBlocksLowerTriangular" | custom-call | tf_op jit(solution)/shard_map/triangular_solve/custom-call.0 | solution.py:45
  272.7 11.7 %cholesky.200 = f32[128,128]{1,0:T(8,128)S(1)} custom-call(f32[128,128]{1,0:T(8,128)S(1)} %fusion.58), custom_call_target="Cholesky" | custom-call | tf_op jit(solution)/shard_map/jit(cholesky)/cholesky | solution.py:44
  286.4 9.8 %custom-call.20 = f32[1,128,128]{1,2,0:T(8,128)S(1)} custom-call(f32[1,128,128]{2,1,0:T(8,128)S(1)} %get-tuple-element.33), custom_call_target="InvertDiagBlocksLowerTriangular" | custom-call | tf_op jit(solution)/shard_map/triangular_solve/custom-call.0 | solution.py:45
  297.6 11.7 %cholesky.211 = f32[128,128]{1,0:T(8,128)S(1)} custom-call(f32[128,128]{1,0:T(8,128)S(1)} %fusion.56), custom_call_target="Cholesky" | custom-call | tf_op jit(solution)/shard_map/jit(cholesky)/cholesky | solution.py:44
  328.4 11.2 %fusion.110 = f32[3072,512]{1,0:T(8,128)S(1)} fusion(f32[3072,512]{1,0:T(8,128)S(1)} %bitcast.253, f32[256,256]{1,0:T(8,128)S(1)} %select_maximum_fusion.7, f32[128,128]{1,0:T(8,128)S(1)} %copy.167, f32[128,128]{1,0:T(8,128)S(1)} %convolution_negate_fusion.2, f32[128,256]{1,0:T(8,128)S(1)} %concatenate.99, f32[256,256]{1,0:T(8,128)S(1)} %convolution_negate_fusion), kind=kOutput, calls=%fused_computation.247 | convolution fusion | flops 9665249280 | bytes 13369344 | tf_op jit(solution)/shard_map/dot_general | solution.py:163
  339.6 12.3 %fusion.121 = f32[3072,512]{1,0:T(8,128)} fusion(f32[3072,512]{1,0:T(8,128)S(1)} %fusion.110, f32[512,512]{1,0:T(8,128)S(1)} %fusion.109), kind=kOutput, calls=%fused_computation.253 | convolution fusion | flops 9663676416 | bytes 13631488 | tf_op jit(solution)/shard_map/dot_general | solution.py:167
  362.4 126.1 %all-to-all-done = f32[128,2,128,128]{3,2,1,0:T(8,128)} async-done(((f32[128,2,128,128]{3,2,1,0:T(8,128)}), f32[128,2,128,128]{3,2,1,0:T(8,128)}, u32[]{:S(2)}, u32[]{:S(2)}) %all-to-all-start) | async-done | bytes 16777248 | tf_op jit(solution)/shard_map/all_to_all | solution.py:168
  488.5 46.8 %gather_fusion.2 = f32[12288,128]{1,0:T(8,128)} fusion(f32[32768,128]{1,0:T(8,128)} %bitcast.28, s32[12288]{0:T(1024)S(1)} %copy-done.9), kind=kCustom, calls=%fused_computation.2 | custom fusion | bytes 12632064 | tf_op jit(solution)/shard_map/jit(_take)/gather | solution.py:190
  535.3 47.2 %gather_fusion.1 = f32[12288,128]{1,0:T(8,128)} fusion(f32[32768,128]{1,0:T(8,128)} %bitcast.28, s32[12288]{0:T(1024)S(1)} %copy-done.8), kind=kCustom, calls=%fused_computation.1 | custom fusion | bytes 12632064 | tf_op jit(solution)/shard_map/jit(_take)/gather | solution.py:189
  582.4 15.2 %fusion.2 = f32[24,1,128,4,1,1,128]{6,5,4,3,2,1,0:T(1,128)} fusion(f32[24,1,128,4,1,1,128]{6,5,4,3,2,1,0:T(1,128)} %bitcast.245, f32[24,1,128,4,1,1,128]{6,5,4,3,2,1,0:T(1,128)} %bitcast.244, pred[24,4]{1,0:T(8,128)(4,1)S(1)} %copy.131, f32[24,1,128,4,1,1,128]{6,5,4,3,2,1,0:T(1,128)} %bitcast.243, pred[24,4]{1,0:T(8,128)(4,1)S(1)} %copy.152), kind=kLoop, calls=%fused_computation.8 | loop fusion | flops 6291456 | bytes 25166016 | tf_op jit(solution)/shard_map/sub | solution.py:192
  (212 shorter events, 118.1 us)
Async XLA Ops:
  7.2 27.4 %copy-start.5 = (f32[1,512,512]{2,1,0:T(8,128)S(1)}, f32[1,512,512]{2,1,0:T(8,128)}, u32[]{:S(2)}) copy-start(f32[1,512,512]{2,1,0:T(8,128)} %param.9) | copy-start | bytes 3145732
  7.2 174.9 %all-gather.4.cloned.1.call-start = ((), (), s32[]{:S(2)}) async-start(), calls=%async_computation.1 | async-start | bytes 2228224 | tf_op jit(solution)/shard_map/all_gather | solution.py:107
  8.2 12.5 %collective-permute-start.1 = (f32[8,8,512]{2,1,0:T(8,128)S(1)}, f32[8,8,512]{2,1,0:T(8,128)S(1)}, u32[]{:S(2)}, u32[]{:S(2)}) collective-permute-start(f32[8,8,512]{2,1,0:T(8,128)S(1)} %slice_bitcast_fusion.1), channel_id=1, source_target_pairs={{1,8},{2,16},{3,24},{4,32},{5,40},{6,48},{7,56},{8,1},{10,17},{11,... | collective-permute-start | bytes 393224 | tf_op jit(solution)/shard_map/ppermute | solution.py:105
  22.3 179.7 %all-gather.6.cloned.1.call-start = ((), (), s32[]{:S(2)}) async-start(), calls=%async_computation.2 | async-start | bytes 6684672 | tf_op jit(solution)/shard_map/all_gather | solution.py:97
  26.2 113.3 %collective-permute-start = (f32[8,128,512]{2,1,0:T(8,128)}, f32[8,128,512]{2,1,0:T(8,128)}, u32[]{:S(2)}, u32[]{:S(2)}) collective-permute-start(f32[8,128,512]{2,1,0:T(8,128)} %slice_bitcast_fusion), channel_id=1, source_target_pairs={{1,8},{2,16},{3,24},{4,32},{5,40},{6,48},{7,56},{8,1},{10,17},{11,... | collective-permute-start | bytes 6291464 | tf_op jit(solution)/shard_map/ppermute | solution.py:93
  131.5 7.9 %copy-start = (f32[1,16,1,128,512]{4,3,2,1,0:T(8,128)S(1)}, f32[1,16,1,128,512]{4,3,2,1,0:T(8,128)}, u32[]{:S(2)}) copy-start(f32[1,16,1,128,512]{4,3,2,1,0:T(8,128)} %param.10) | copy-start | bytes 12582916
  133.7 9.9 %slice-start = ((s8[8388608]{0:T(1024)(128)(4,1)}), s8[4194304]{0:T(1024)(128)(4,1)S(1)}, s32[]{:S(2)}) async-start(s8[8388608]{0:T(1024)(128)(4,1)} %bitcast.248), calls=%async_computation.3 | async-start | bytes 8388608
  139.4 4.1 slice-start.1
  202.0 9.6 %copy-start.10 = (s32[2,128]{1,0:T(2,128)S(1)}, s32[2,128]{1,0:T(2,128)}, u32[]{:S(2)}) copy-start(s32[2,128]{1,0:T(2,128)} %param.14) | copy-start | bytes 3076
  202.0 286.4 %all-to-all-start = ((f32[128,2,128,128]{3,2,1,0:T(8,128)}), f32[128,2,128,128]{3,2,1,0:T(8,128)}, u32[]{:S(2)}, u32[]{:S(2)}) async-start(f32[128,2,128,128]{3,2,1,0:T(8,128)} %bitcast.241), calls=%async_computation | async-start | bytes 33554432 | tf_op jit(solution)/shard_map/all_to_all | solution.py:168
  219.5 108.8 %slice-start.2 = ((s8[6291456]{0:T(1024)(128)(4,1)}), s8[2097152]{0:T(1024)(128)(4,1)S(1)}, s32[]{:S(2)}) async-start(s8[6291456]{0:T(1024)(128)(4,1)} %bitcast.251), calls=%async_computation.5 | async-start | bytes 4194304
  244.8 0.8 copy-start.1
  321.5 6.9 %slice-start.3 = ((s8[6291456]{0:T(1024)(128)(4,1)}), s8[4194304]{0:T(1024)(128)(4,1)S(1)}, s32[]{:S(2)}) async-start(s8[6291456]{0:T(1024)(128)(4,1)} %bitcast.251), calls=%async_computation.6 | async-start | bytes 8388608
  322.0 17.6 %copy-start.3 = (f32[256,256]{1,0:T(8,128)}, f32[256,256]{1,0:T(8,128)S(1)}, u32[]{:S(2)}) copy-start(f32[256,256]{1,0:T(8,128)S(1)} %select_maximum_fusion.7) | copy-start | bytes 786436
  351.9 7.6 %copy-start.6 = (f32[512,128]{1,0:T(8,128)S(1)}, f32[512,128]{1,0:T(8,128)}, u32[]{:S(2)}) copy-start(f32[512,128]{1,0:T(8,128)} %get-tuple-element.55) | copy-start | bytes 786436
  351.9 7.6 %copy-start.7 = (f32[128,128]{1,0:T(8,128)S(1)}, f32[128,128]{1,0:T(8,128)}, u32[]{:S(2)}) copy-start(f32[128,128]{1,0:T(8,128)} %get-tuple-element.32) | copy-start | bytes 196612
  351.9 8.7 %copy-start.2 = (f32[24,1,1,1,8,512]{5,4,3,2,1,0:T(8,128)S(1)}, f32[24,1,1,1,8,512]{5,4,3,2,1,0:T(8,128)}, u32[]{:S(2)}) copy-start(f32[24,1,1,1,8,512]{5,4,3,2,1,0:T(8,128)} %param.13) | copy-start | bytes 1179652
  351.9 8.7 %copy-start.4 = (f32[256,256]{1,0:T(8,128)S(1)}, f32[256,256]{1,0:T(8,128)}, u32[]{:S(2)}) copy-start(f32[256,256]{1,0:T(8,128)} %copy-done.3) | copy-start | bytes 786436
  351.9 136.6 %copy-start.9 = (s32[12288]{0:T(1024)S(1)}, s32[12288]{0:T(1024)}, u32[]{:S(2)}) copy-start(s32[12288]{0:T(1024)} %broadcast_clamp_fusion) | copy-start | bytes 147460
  488.5 46.8 %copy-start.8 = (s32[12288]{0:T(1024)S(1)}, s32[12288]{0:T(1024)}, u32[]{:S(2)}) copy-start(s32[12288]{0:T(1024)} %broadcast_clamp_fusion.1) | copy-start | bytes 147460
Sparse Core Ops, SparseCore 0:
  22.4 136.7 all-gather.3
  160.9 41.0 all-gather.5

commit v8 on v5

--- a/solution.py
+++ b/solution.py
@@ -111,11 +111,14 @@
     schur_part = child_window.reshape(row_local * BLOCK_EXTENT, col_local * BLOCK_EXTENT) - lax.dot_general(
         child_factor, child_columns, dims, precision=high
     )
-    gathered_late, schur_part = lax.optimization_barrier((gathered, schur_part))
-    paired = gathered_late[: 2 * parent_cols].reshape(parent_cols, 2, BLOCK_EXTENT, panel_width)
-    offered = lax.dynamic_index_in_dim(paired, half_id, axis=1, keepdims=False)
-    parent_col_rows = jnp.where(
-        on_diagonal, offered, lax.ppermute(offered, ("row", "col"), transpose_perm)
+    leading_parent = parent_lead_panel.reshape(parent_row_blocks, sub_rows, panel_width)[: 2 * parent_cols]
+    leading_parent, schur_part = lax.optimization_barrier((leading_parent, schur_part))
+    transposed = jnp.where(
+        on_diagonal, leading_parent, lax.ppermute(leading_parent, ("row", "col"), transpose_perm)
+    )
+    column_blocks = lax.all_gather(transposed, ("half", "row"), axis=1, tiled=True)
+    parent_col_rows = lax.dynamic_index_in_dim(
+        column_blocks.reshape(parent_cols, 2, BLOCK_EXTENT, panel_width), half_id, axis=1, keepdims=False
     )
     child_map = lax.dynamic_index_in_dim(index_maps, half_id, axis=0, keepdims=False)
     my_rows = lax.dynamic_index_in_dim(

time: 546 us -> 592 us (1.084)
  waiting for transfers between devices: 155 us -> 203 us
    all_gather x1, waiting for transfers between devices: 0.01 us -> 40.6 us  [per_device(): lax.all_gather(parent_lead_panel.reshape(parent_row_blocks, sub_rows, pan...]
    all_gather x0 -> x1, waiting for transfers between devices: none -> 21.7 us  [per_device(): lax.all_gather(transposed, ('half', 'row'), axis=1, tiled=True)]
    ppermute x1, waiting for transfers between devices: 23.9 us -> 9.31 us  [per_device(): lax.ppermute(leading_parent, ('row', 'col'), transpose_perm)]
  transfers between devices with their start and end apart: 4 -> 5, of which waited for: 2 -> 4; matrix products, arithmetic and copies ran while one was open for 58% -> 50% of each run, Pallas kernels for 0% -> 0%
where the time goes in v8:
time: 592 us; the launch traced here: 588 us
  other arithmetic  213 us (36%)
  waiting for transfers between devices  203 us (34%)
  local copies, waits for them, and re-layouts  74.1 us (13%)
  matrix products  65.5 us (11%)
  starting transfers between devices  17.7 us (3%)
  between operations  15.3 us (3%)
    all_to_all x1, waiting for transfers between devices, per_device(): lax.all_to_all(outgoing.reshape(-1, per_row * per_col, BLOCK_EXTENT, BLOC...  131 us
    another operation x24, other arithmetic, factor_and_inverse(): low = jnp.linalg.cholesky(work[:leaf, :leaf])  111 us
    another operation x16, other arithmetic, factor_and_inverse(): inv = lax.linalg.triangular_solve(low, eye, left_side=True, lower=True)  85.2 us
    all_gather x1, waiting for transfers between devices, per_device(): lax.all_gather(parent_lead_panel.reshape(parent_row_blocks, sub_rows, pan...  40.6 us
    all_gather x1, waiting for transfers between devices, per_device(): lax.all_gather(transposed, ('half', 'row'), axis=1, tiled=True)  21.7 us
    dot_general x1, matrix products, per_device(): lax.dot_general(child_factor, child_columns, dims, precision=high)  16.7 us
    gather x1, local copies, waits for them, and re-layouts, per_device(): outgoing = schur_blocks[send_row_index, :, send_col_index, :]  16 us
    unnamed x29, local copies, waits for them, and re-layouts  15.4 us
  transfers between devices with their start and end apart: 5, of which 4 were waited for; matrix products, arithmetic and copies ran while one was open for 50% of the time, Pallas kernels for 0%

profile of v8, /device:TPU:10, one launch (start us, length us, event | category | flops | bytes accessed | tf_op | source)
XLA Modules:
  0.0 588.1 jit_solution(877429703570291696)
XLA Ops:
  16.6 11.7 %cholesky.134 = f32[128,128]{1,0:T(8,128)S(1)} custom-call(f32[128,128]{1,0:T(8,128)S(1)} %fusion.68), custom_call_target="Cholesky" | custom-call | tf_op jit(solution)/shard_map/jit(cholesky)/cholesky | solution.py:44
  29.7 9.8 %custom-call.14 = f32[1,128,128]{1,2,0:T(8,128)S(1)} custom-call(f32[1,128,128]{2,1,0:T(8,128)S(1)} %get-tuple-element.49), custom_call_target="InvertDiagBlocksLowerTriangular" | custom-call | tf_op jit(solution)/shard_map/triangular_solve/custom-call.0 | solution.py:45
  40.9 11.7 %cholesky.145 = f32[128,128]{1,0:T(8,128)S(1)} custom-call(f32[128,128]{1,0:T(8,128)S(1)} %fusion.66), custom_call_target="Cholesky" | custom-call | tf_op jit(solution)/shard_map/jit(cholesky)/cholesky | solution.py:44
  54.0 10.0 %custom-call.15 = f32[1,128,128]{1,2,0:T(8,128)S(1)} custom-call(f32[1,128,128]{2,1,0:T(8,128)S(1)} %get-tuple-element.47), custom_call_target="InvertDiagBlocksLowerTriangular" | custom-call | tf_op jit(solution)/shard_map/triangular_solve/custom-call.0 | solution.py:45
  65.3 11.7 %cholesky.156 = f32[128,128]{1,0:T(8,128)S(1)} custom-call(f32[128,128]{1,0:T(8,128)S(1)} %fusion.64), custom_call_target="Cholesky" | custom-call | tf_op jit(solution)/shard_map/jit(cholesky)/cholesky | solution.py:44
  78.4 9.8 %custom-call.16 = f32[1,128,128]{1,2,0:T(8,128)S(1)} custom-call(f32[1,128,128]{2,1,0:T(8,128)S(1)} %fusion.43), custom_call_target="InvertDiagBlocksLowerTriangular" | custom-call | tf_op jit(solution)/shard_map/triangular_solve/custom-call.0 | solution.py:45
  89.1 23.0 %cholesky.167 = f32[128,128]{1,0:T(8,128)S(1)} custom-call(f32[128,128]{1,0:T(8,128)S(1)} %fusion.62), custom_call_target="Cholesky" | custom-call | tf_op jit(solution)/shard_map/jit(cholesky)/cholesky | solution.py:44
  113.5 9.8 %custom-call.17 = f32[1,128,128]{1,2,0:T(8,128)S(1)} custom-call(f32[1,128,128]{2,1,0:T(8,128)S(1)} %fusion.44), custom_call_target="InvertDiagBlocksLowerTriangular" | custom-call | tf_op jit(solution)/shard_map/triangular_solve/custom-call.0 | solution.py:45
  136.8 16.7 %bitcast_subtract_fusion = f32[2048,1024]{1,0:T(8,128)} fusion(f32[256,8,8,128]{3,2,1,0:T(8,128)S(1)} %bitcast.242, f32[512,2048]{1,0:T(8,128)S(1)} %fusion.2, f32[1024,512]{1,0:T(8,128)S(1)} %fusion.1), kind=kOutput, calls=%fused_computation.3 | convolution fusion | flops 6444548096 | bytes 23068672 | tf_op jit(solution)/shard_map/dot_general | solution.py:111
  180.4 16.0 %gather_fusion = f32[256,128,128]{2,1,0:T(8,128)} fusion(f32[16,128,8,128]{3,1,2,0:T(8,128)} %copy.137, s32[256]{0:T(256)S(1)} %reshape.466), kind=kCustom, calls=%fused_computation | custom fusion | bytes 33556480 | tf_op jit(solution)/shard_map/gather | solution.py:157
  196.4 21.7 %all-gather.4.cloned.1.call-done = f32[8,128,512]{2,1,0:T(8,128)} async-done(((f32[8,8,512]{2,1,0:T(8,128)}), f32[8,128,512]{2,1,0:T(8,128)}) %all-gather.4.cloned.1.call-update) | async-done | bytes 2097168 | tf_op jit(solution)/shard_map/all_gather | solution.py:119
  220.4 40.6 %all-gather.6.cloned.1.call-done = f32[24,1,1,1,128,512]{5,4,3,2,1,0:T(8,128)} async-done(((f32[24,1,1,1,8,512]{5,4,3,2,1,0:T(8,128)}), f32[24,1,1,1,128,512]{5,4,3,2,1,0:T(8,128)}) %all-gather.6.cloned.1.call-update) | async-done | bytes 6291472 | tf_op jit(solution)/shard_map/all_gather | solution.py:97
  260.9 9.6 %all-to-all-start = ((f32[128,2,128,128]{3,2,1,0:T(8,128)}), f32[128,2,128,128]{3,2,1,0:T(8,128)}, u32[]{:S(2)}, u32[]{:S(2)}) async-start(f32[128,2,128,128]{3,2,1,0:T(8,128)} %bitcast.233), calls=%async_computation | async-start | bytes 33554432 | tf_op jit(solution)/shard_map/all_to_all | solution.py:169
  273.8 11.7 %cholesky.178 = f32[128,128]{1,0:T(8,128)S(1)} custom-call(f32[128,128]{1,0:T(8,128)S(1)} %fusion.60), custom_call_target="Cholesky" | custom-call | tf_op jit(solution)/shard_map/jit(cholesky)/cholesky | solution.py:44
  286.9 9.8 %custom-call.18 = f32[1,128,128]{1,2,0:T(8,128)S(1)} custom-call(f32[1,128,128]{2,1,0:T(8,128)S(1)} %get-tuple-element.41), custom_call_target="InvertDiagBlocksLowerTriangular" | custom-call | tf_op jit(solution)/shard_map/triangular_solve/custom-call.0 | solution.py:45
  300.7 11.9 %cholesky.189 = f32[128,128]{1,0:T(8,128)S(1)} custom-call(f32[128,128]{1,0:T(8,128)S(1)} %fusion.58), custom_call_target="Cholesky" | custom-call | tf_op jit(solution)/shard_map/jit(cholesky)/cholesky | solution.py:44
  313.9 9.8 %custom-call.19 = f32[1,128,128]{1,2,0:T(8,128)S(1)} custom-call(f32[1,128,128]{2,1,0:T(8,128)S(1)} %get-tuple-element.39), custom_call_target="InvertDiagBlocksLowerTriangular" | custom-call | tf_op jit(solution)/shard_map/triangular_solve/custom-call.0 | solution.py:45
  326.9 11.7 %cholesky.200 = f32[128,128]{1,0:T(8,128)S(1)} custom-call(f32[128,128]{1,0:T(8,128)S(1)} %fusion.56), custom_call_target="Cholesky" | custom-call | tf_op jit(solution)/shard_map/jit(cholesky)/cholesky | solution.py:44
  340.5 9.8 %custom-call.20 = f32[1,128,128]{1,2,0:T(8,128)S(1)} custom-call(f32[1,128,128]{2,1,0:T(8,128)S(1)} %get-tuple-element.37), custom_call_target="InvertDiagBlocksLowerTriangular" | custom-call | tf_op jit(solution)/shard_map/triangular_solve/custom-call.0 | solution.py:45
  351.3 12.1 %cholesky.211 = f32[128,128]{1,0:T(8,128)S(1)} custom-call(f32[128,128]{1,0:T(8,128)S(1)} %fusion.54), custom_call_target="Cholesky" | custom-call | tf_op jit(solution)/shard_map/jit(cholesky)/cholesky | solution.py:44
  365.4 9.8 %custom-call.21 = f32[1,128,128]{1,2,0:T(8,128)S(1)} custom-call(f32[1,128,128]{2,1,0:T(8,128)S(1)} %get-tuple-element.35), custom_call_target="InvertDiagBlocksLowerTriangular" | custom-call | tf_op jit(solution)/shard_map/triangular_solve/custom-call.0 | solution.py:45
  382.5 11.3 %fusion.105 = f32[3072,512]{1,0:T(8,128)S(1)} fusion(f32[3072,512]{1,0:T(8,128)S(1)} %bitcast.245, f32[256,256]{1,0:T(8,128)S(1)} %select_maximum_fusion.7, f32[128,128]{1,0:T(8,128)S(1)} %copy.153, f32[128,128]{1,0:T(8,128)S(1)} %convolution_negate_fusion.2, f32[128,256]{1,0:T(8,128)S(1)} %concatenate.99, f32[256,256]{1,0:T(8,128)S(1)} %convolution_negate_fusion), kind=kOutput, calls=%fused_computation.238 | convolution fusion | flops 9665249280 | bytes 13369344 | tf_op jit(solution)/shard_map/dot_general | solution.py:164
  393.7 12.1 %fusion.117 = f32[3072,512]{1,0:T(8,128)} fusion(f32[3072,512]{1,0:T(8,128)S(1)} %fusion.105, f32[512,512]{1,0:T(8,128)S(1)} %fusion.104), kind=kOutput, calls=%fused_computation.245 | convolution fusion | flops 9663676416 | bytes 13631488 | tf_op jit(solution)/shard_map/dot_general | solution.py:168
  416.5 130.9 %all-to-all-done = f32[128,2,128,128]{3,2,1,0:T(8,128)} async-done(((f32[128,2,128,128]{3,2,1,0:T(8,128)}), f32[128,2,128,128]{3,2,1,0:T(8,128)}, u32[]{:S(2)}, u32[]{:S(2)}) %all-to-all-start) | async-done | bytes 16777248 | tf_op jit(solution)/shard_map/all_to_all | solution.py:169
  (207 shorter events, 129.8 us)
Async XLA Ops:
  7.2 211.0 %all-gather.4.cloned.1.call-start = ((), (), s32[]{:S(2)}) async-start(), calls=%async_computation.1 | async-start | bytes 2228224 | tf_op jit(solution)/shard_map/all_gather | solution.py:119
  10.3 122.3 %collective-permute-start = (f32[8,128,512]{2,1,0:T(8,128)}, f32[8,128,512]{2,1,0:T(8,128)}, u32[]{:S(2)}, u32[]{:S(2)}) collective-permute-start(f32[8,128,512]{2,1,0:T(8,128)} %slice_bitcast_fusion), channel_id=1, source_target_pairs={{1,8},{2,16},{3,24},{4,32},{5,40},{6,48},{7,56},{8,1},{10,17},{11,... | collective-permute-start | bytes 6291464 | tf_op jit(solution)/shard_map/ppermute | solution.py:93
  124.1 8.6 %copy-start = (f32[1,16,1,128,512]{4,3,2,1,0:T(8,128)S(1)}, f32[1,16,1,128,512]{4,3,2,1,0:T(8,128)}, u32[]{:S(2)}) copy-start(f32[1,16,1,128,512]{4,3,2,1,0:T(8,128)} %param.10) | copy-start | bytes 12582916
  127.1 9.7 %slice-start = ((s8[8388608]{0:T(1024)(128)(4,1)}), s8[4194304]{0:T(1024)(128)(4,1)S(1)}, s32[]{:S(2)}) async-start(s8[8388608]{0:T(1024)(128)(4,1)} %bitcast.240), calls=%async_computation.3 | async-start | bytes 8388608
  132.6 4.2 slice-start.1
  136.8 31.0 %copy-start.8 = (s32[2,128]{1,0:T(2,128)S(1)}, s32[2,128]{1,0:T(2,128)}, u32[]{:S(2)}) copy-start(s32[2,128]{1,0:T(2,128)} %param.14) | copy-start | bytes 3076
  153.5 12.3 %collective-permute-start.1 = (f32[8,8,512]{2,1,0:T(8,128)S(1)}, f32[8,8,512]{2,1,0:T(8,128)S(1)}, u32[]{:S(2)}, u32[]{:S(2)}) collective-permute-start(f32[8,8,512]{2,1,0:T(8,128)S(1)} %slice_bitcast_fusion.1), channel_id=1, source_target_pairs={{1,8},{2,16},{3,24},{4,32},{5,40},{6,48},{7,56},{8,1},{10,17},{11,... | collective-permute-start | bytes 393224 | tf_op jit(solution)/shard_map/ppermute | solution.py:117
  166.5 94.5 %all-gather.6.cloned.1.call-start = ((), (), s32[]{:S(2)}) async-start(), calls=%async_computation.2 | async-start | bytes 6684672 | tf_op jit(solution)/shard_map/all_gather | solution.py:97
  260.9 12.4 %copy-start.2 = (f32[512,512]{1,0:T(8,128)S(1)}, f32[512,512]{1,0:T(8,128)}, u32[]{:S(2)}) copy-start(f32[512,512]{1,0:T(8,128)} %param.12) | copy-start | bytes 3145732
  260.9 286.4 %all-to-all-start = ((f32[128,2,128,128]{3,2,1,0:T(8,128)}), f32[128,2,128,128]{3,2,1,0:T(8,128)}, u32[]{:S(2)}, u32[]{:S(2)}) async-start(f32[128,2,128,128]{3,2,1,0:T(8,128)} %bitcast.233), calls=%async_computation | async-start | bytes 33554432 | tf_op jit(solution)/shard_map/all_to_all | solution.py:169
  273.7 108.8 %slice-start.2 = ((s8[6291456]{0:T(1024)(128)(4,1)}), s8[2097152]{0:T(1024)(128)(4,1)S(1)}, s32[]{:S(2)}) async-start(s8[6291456]{0:T(1024)(128)(4,1)} %bitcast.243), calls=%async_computation.5 | async-start | bytes 4194304
  298.9 0.8 copy-start.1
  375.6 6.9 %slice-start.3 = ((s8[6291456]{0:T(1024)(128)(4,1)}), s8[4194304]{0:T(1024)(128)(4,1)S(1)}, s32[]{:S(2)}) async-start(s8[6291456]{0:T(1024)(128)(4,1)} %bitcast.243), calls=%async_computation.6 | async-start | bytes 8388608
  376.1 17.6 %copy-start.3 = (f32[256,256]{1,0:T(8,128)}, f32[256,256]{1,0:T(8,128)S(1)}, u32[]{:S(2)}) copy-start(f32[256,256]{1,0:T(8,128)S(1)} %select_maximum_fusion.7) | copy-start | bytes 786436
  405.8 7.8 %copy-start.5 = (f32[512,128]{1,0:T(8,128)S(1)}, f32[512,128]{1,0:T(8,128)}, u32[]{:S(2)}) copy-start(f32[512,128]{1,0:T(8,128)} %get-tuple-element.59) | copy-start | bytes 786436
  405.8 7.8 %copy-start.7 = (f32[128,128]{1,0:T(8,128)S(1)}, f32[128,128]{1,0:T(8,128)}, u32[]{:S(2)}) copy-start(f32[128,128]{1,0:T(8,128)} %get-tuple-element.36) | copy-start | bytes 196612
  405.8 8.9 %copy-start.4 = (f32[256,256]{1,0:T(8,128)S(1)}, f32[256,256]{1,0:T(8,128)}, u32[]{:S(2)}) copy-start(f32[256,256]{1,0:T(8,128)} %copy-done.3) | copy-start | bytes 786436
  405.8 8.9 %copy-start.6 = (f32[24,1,1,1,8,512]{5,4,3,2,1,0:T(8,128)S(1)}, f32[24,1,1,1,8,512]{5,4,3,2,1,0:T(8,128)}, u32[]{:S(2)}) copy-start(f32[24,1,1,1,8,512]{5,4,3,2,1,0:T(8,128)} %param.13) | copy-start | bytes 1179652
Sparse Core Ops, SparseCore 0:
  166.6 51.4 all-gather.3
  219.8 41.0 all-gather.5

commit v9 on v6

--- a/solution.py
+++ b/solution.py
@@ -89,9 +89,10 @@
     ]
     on_diagonal = row_id == col_id
     child_lead = child_panel[0, :col_local, 0]
+    whole_panel = child_panel[0, :, 0]
     child_col_rows = jnp.where(
-        on_diagonal, child_lead, lax.ppermute(child_lead, ("row", "col"), transpose_perm)
-    )
+        on_diagonal, whole_panel, lax.ppermute(whole_panel, ("row", "col"), transpose_perm)
+    )[:col_local]
     sub_rows = parent_lead_panel.shape[4]
     own_rows = parent_lead_panel.reshape(-1, panel_width)
     gathered = lax.all_gather(

time: 539 us -> 631 us (1.17)
  waiting for transfers between devices: 157 us -> 237 us
  other arithmetic: 203 us -> 215 us
    all_gather x1, waiting for transfers between devices: 0.01 us -> 97.4 us  [per_device(): lax.all_gather(transposed, ('half', 'row'), axis=1, tiled=True)]
    all_gather x1, waiting for transfers between devices: 17.6 us -> 0.01 us  [per_device(): lax.all_gather(parent_lead_panel.reshape(parent_row_blocks, sub_rows, pan...]
    another operation x24, other arithmetic: 100 us -> 112 us  [factor_and_inverse(): low = jnp.linalg.cholesky(work[:leaf, :leaf])]
  transfers between devices with their start and end apart: 5 -> 5, of which waited for: 3 -> 3; matrix products, arithmetic and copies ran while one was open for 57% -> 51% of each run, Pallas kernels for 0% -> 0%
where the time goes in v9:
time: 631 us; the launch traced here: 621 us
  waiting for transfers between devices  237 us (38%)
  other arithmetic  215 us (34%)
  matrix products  68.8 us (11%)
  local copies, waits for them, and re-layouts  68.6 us (11%)
  starting transfers between devices  17 us (3%)
  between operations  15.3 us (2%)
    all_to_all x1, waiting for transfers between devices, per_device(): lax.all_to_all(outgoing.reshape(-1, per_row * per_col, BLOCK_EXTENT, BLOC...  131 us
    another operation x24, other arithmetic, factor_and_inverse(): low = jnp.linalg.cholesky(work[:leaf, :leaf])  112 us
    all_gather x1, waiting for transfers between devices, per_device(): lax.all_gather(transposed, ('half', 'row'), axis=1, tiled=True)  97.4 us
    another operation x16, other arithmetic, factor_and_inverse(): inv = lax.linalg.triangular_solve(low, eye, left_side=True, lower=True)  85.2 us
    dot_general x1, matrix products, per_device(): lax.dot_general(child_factor, child_columns, dims, precision=high)  17.9 us
    gather x1, local copies, waits for them, and re-layouts, per_device(): outgoing = schur_blocks[send_row_index, :, send_col_index, :]  16.2 us
  transfers between devices with their start and end apart: 5, of which 3 were waited for; matrix products, arithmetic and copies ran while one was open for 51% of the time, Pallas kernels for 0%

profile of v9, /device:TPU:10, one launch (start us, length us, event | category | flops | bytes accessed | tf_op | source)
XLA Modules:
  0.0 621.3 jit_solution(2975020562166313542)
XLA Ops:
  32.4 11.7 %cholesky.134 = f32[128,128]{1,0:T(8,128)S(1)} custom-call(f32[128,128]{1,0:T(8,128)S(1)} %fusion.69), custom_call_target="Cholesky" | custom-call | tf_op jit(solution)/shard_map/jit(cholesky)/cholesky | solution.py:44
  45.5 9.8 %custom-call.14 = f32[1,128,128]{1,2,0:T(8,128)S(1)} custom-call(f32[1,128,128]{2,1,0:T(8,128)S(1)} %get-tuple-element.45), custom_call_target="InvertDiagBlocksLowerTriangular" | custom-call | tf_op jit(solution)/shard_map/triangular_solve/custom-call.0 | solution.py:45
  56.7 11.7 %cholesky.145 = f32[128,128]{1,0:T(8,128)S(1)} custom-call(f32[128,128]{1,0:T(8,128)S(1)} %fusion.67), custom_call_target="Cholesky" | custom-call | tf_op jit(solution)/shard_map/jit(cholesky)/cholesky | solution.py:44
  69.8 10.0 %custom-call.15 = f32[1,128,128]{1,2,0:T(8,128)S(1)} custom-call(f32[1,128,128]{2,1,0:T(8,128)S(1)} %get-tuple-element.43), custom_call_target="InvertDiagBlocksLowerTriangular" | custom-call | tf_op jit(solution)/shard_map/triangular_solve/custom-call.0 | solution.py:45
  82.0 11.7 %cholesky.156 = f32[128,128]{1,0:T(8,128)S(1)} custom-call(f32[128,128]{1,0:T(8,128)S(1)} %fusion.65), custom_call_target="Cholesky" | custom-call | tf_op jit(solution)/shard_map/jit(cholesky)/cholesky | solution.py:44
  95.1 9.8 %custom-call.16 = f32[1,128,128]{1,2,0:T(8,128)S(1)} custom-call(f32[1,128,128]{2,1,0:T(8,128)S(1)} %fusion.44), custom_call_target="InvertDiagBlocksLowerTriangular" | custom-call | tf_op jit(solution)/shard_map/triangular_solve/custom-call.0 | solution.py:45
  105.9 23.7 %cholesky.167 = f32[128,128]{1,0:T(8,128)S(1)} custom-call(f32[128,128]{1,0:T(8,128)S(1)} %fusion.63), custom_call_target="Cholesky" | custom-call | tf_op jit(solution)/shard_map/jit(cholesky)/cholesky | solution.py:44
  131.0 9.8 %custom-call.17 = f32[1,128,128]{1,2,0:T(8,128)S(1)} custom-call(f32[1,128,128]{2,1,0:T(8,128)S(1)} %fusion.45), custom_call_target="InvertDiagBlocksLowerTriangular" | custom-call | tf_op jit(solution)/shard_map/triangular_solve/custom-call.0 | solution.py:45
  151.0 97.4 %all-gather.4.cloned.1.call-done = f32[8,128,512]{2,1,0:T(8,128)} async-done(((f32[8,8,512]{2,1,0:T(8,128)}), f32[8,128,512]{2,1,0:T(8,128)}) %all-gather.4.cloned.1.call-update) | async-done | bytes 2097168 | tf_op jit(solution)/shard_map/all_gather | solution.py:108
  255.3 17.9 %fusion = f32[256,8,8,128]{3,1,2,0:T(8,128)S(1)} fusion(f32[256,8,8,128]{3,2,1,0:T(8,128)} %bitcast.243, f32[512,2048]{1,0:T(8,128)S(1)} %copy-done, f32[1024,512]{1,0:T(8,128)S(1)} %fusion.2), kind=kOutput, calls=%fused_computation.4 | convolution fusion | flops 6444548096 | bytes 23068672 | tf_op jit(solution)/shard_map/dot_general | solution.py:120
  280.0 16.2 %gather_fusion = f32[256,128,128]{2,1,0:T(8,128)} fusion(f32[16,128,8,128]{3,1,2,0:T(8,128)} %copy.137, s32[256]{0:T(256)S(1)} %reshape.466), kind=kCustom, calls=%fused_computation | custom fusion | bytes 33556480 | tf_op jit(solution)/shard_map/gather | solution.py:157
  307.0 11.7 %cholesky.178 = f32[128,128]{1,0:T(8,128)S(1)} custom-call(f32[128,128]{1,0:T(8,128)S(1)} %fusion.61), custom_call_target="Cholesky" | custom-call | tf_op jit(solution)/shard_map/jit(cholesky)/cholesky | solution.py:44
  320.1 9.8 %custom-call.18 = f32[1,128,128]{1,2,0:T(8,128)S(1)} custom-call(f32[1,128,128]{2,1,0:T(8,128)S(1)} %get-tuple-element.37), custom_call_target="InvertDiagBlocksLowerTriangular" | custom-call | tf_op jit(solution)/shard_map/triangular_solve/custom-call.0 | solution.py:45
  333.9 11.9 %cholesky.189 = f32[128,128]{1,0:T(8,128)S(1)} custom-call(f32[128,128]{1,0:T(8,128)S(1)} %fusion.59), custom_call_target="Cholesky" | custom-call | tf_op jit(solution)/shard_map/jit(cholesky)/cholesky | solution.py:44
  347.1 9.8 %custom-call.19 = f32[1,128,128]{1,2,0:T(8,128)S(1)} custom-call(f32[1,128,128]{2,1,0:T(8,128)S(1)} %get-tuple-element.35), custom_call_target="InvertDiagBlocksLowerTriangular" | custom-call | tf_op jit(solution)/shard_map/triangular_solve/custom-call.0 | solution.py:45
  360.1 11.7 %cholesky.200 = f32[128,128]{1,0:T(8,128)S(1)} custom-call(f32[128,128]{1,0:T(8,128)S(1)} %fusion.57), custom_call_target="Cholesky" | custom-call | tf_op jit(solution)/shard_map/jit(cholesky)/cholesky | solution.py:44
  373.7 9.8 %custom-call.20 = f32[1,128,128]{1,2,0:T(8,128)S(1)} custom-call(f32[1,128,128]{2,1,0:T(8,128)S(1)} %get-tuple-element.33), custom_call_target="InvertDiagBlocksLowerTriangular" | custom-call | tf_op jit(solution)/shard_map/triangular_solve/custom-call.0 | solution.py:45
  384.5 12.1 %cholesky.211 = f32[128,128]{1,0:T(8,128)S(1)} custom-call(f32[128,128]{1,0:T(8,128)S(1)} %fusion.55), custom_call_target="Cholesky" | custom-call | tf_op jit(solution)/shard_map/jit(cholesky)/cholesky | solution.py:44
  398.6 9.8 %custom-call.21 = f32[1,128,128]{1,2,0:T(8,128)S(1)} custom-call(f32[1,128,128]{2,1,0:T(8,128)S(1)} %get-tuple-element.31), custom_call_target="InvertDiagBlocksLowerTriangular" | custom-call | tf_op jit(solution)/shard_map/triangular_solve/custom-call.0 | solution.py:45
  415.7 11.3 %fusion.106 = f32[3072,512]{1,0:T(8,128)S(1)} fusion(f32[3072,512]{1,0:T(8,128)S(1)} %bitcast.246, f32[256,256]{1,0:T(8,128)S(1)} %select_maximum_fusion.7, f32[128,128]{1,0:T(8,128)S(1)} %copy.153, f32[128,128]{1,0:T(8,128)S(1)} %convolution_negate_fusion.2, f32[128,256]{1,0:T(8,128)S(1)} %concatenate.99, f32[256,256]{1,0:T(8,128)S(1)} %convolution_negate_fusion), kind=kOutput, calls=%fused_computation.238 | convolution fusion | flops 9665249280 | bytes 13369344 | tf_op jit(solution)/shard_map/dot_general | solution.py:164
  426.9 12.1 %fusion.118 = f32[3072,512]{1,0:T(8,128)} fusion(f32[3072,512]{1,0:T(8,128)S(1)} %fusion.106, f32[512,512]{1,0:T(8,128)S(1)} %fusion.105), kind=kOutput, calls=%fused_computation.245 | convolution fusion | flops 9663676416 | bytes 13631488 | tf_op jit(solution)/shard_map/dot_general | solution.py:168
  449.7 130.9 %all-to-all-done = f32[128,2,128,128]{3,2,1,0:T(8,128)} async-done(((f32[128,2,128,128]{3,2,1,0:T(8,128)}), f32[128,2,128,128]{3,2,1,0:T(8,128)}, u32[]{:S(2)}, u32[]{:S(2)}) %all-to-all-start) | async-done | bytes 16777248 | tf_op jit(solution)/shard_map/all_to_all | solution.py:169
  580.6 9.4 %gather_fusion.2 = f32[96,128,128]{2,1,0:T(8,128)} fusion(f32[256,128,128]{2,1,0:T(8,128)} %bitcast.28, s32[1024]{0:T(1024)S(1)} %pad_clamp_fusion), kind=kCustom, calls=%fused_computation.2 | custom fusion | bytes 12583296 | tf_op jit(solution)/shard_map/jit(_take)/gather | solution.py:188
  590.0 9.4 %gather_fusion.1 = f32[96,128,128]{2,1,0:T(8,128)} fusion(f32[256,128,128]{2,1,0:T(8,128)} %bitcast.28, s32[1024]{0:T(1024)S(1)} %pad_clamp_fusion.1), kind=kCustom, calls=%fused_computation.1 | custom fusion | bytes 12583296 | tf_op jit(solution)/shard_map/jit(_take)/gather | solution.py:187
  (201 shorter events, 116.6 us)
Async XLA Ops:
  7.2 241.2 %all-gather.4.cloned.1.call-start = ((), (), s32[]{:S(2)}) async-start(), calls=%async_computation.1 | async-start | bytes 2228224 | tf_op jit(solution)/shard_map/all_gather | solution.py:108
  8.1 12.5 %collective-permute-start.1 = (f32[8,8,512]{2,1,0:T(8,128)S(1)}, f32[8,8,512]{2,1,0:T(8,128)S(1)}, u32[]{:S(2)}, u32[]{:S(2)}) collective-permute-start(f32[8,8,512]{2,1,0:T(8,128)S(1)} %slice_bitcast_fusion), channel_id=1, source_target_pairs={{1,8},{2,16},{3,24},{4,32},{5,40},{6,48},{7,56},{8,1},{10,17},{11,... | collective-permute-start | bytes 393224 | tf_op jit(solution)/shard_map/ppermute | solution.py:106
  22.2 274.0 %all-gather.6.cloned.1.call-start = ((), (), s32[]{:S(2)}) async-start(), calls=%async_computation.2 | async-start | bytes 6684672 | tf_op jit(solution)/shard_map/all_gather | solution.py:98
  23.0 227.8 %collective-permute-start = (f32[16,128,512]{2,1,0:T(8,128)}, f32[16,128,512]{2,1,0:T(8,128)}, u32[]{:S(2)}, u32[]{:S(2)}) collective-permute-start(f32[16,128,512]{2,1,0:T(8,128)} %bitcast.239), channel_id=1, source_target_pairs={{1,8},{2,16},{3,24},{4,32},{5,40},{6,48},{7,56},{8,1},{10,17},{11,... | collective-permute-start | bytes 12582920 | tf_op jit(solution)/shard_map/ppermute | solution.py:94
  248.4 7.0 %copy-start = (f32[512,2048]{1,0:T(8,128)S(1)}, f32[512,2048]{1,0:T(8,128)}, u32[]{:S(2)}) copy-start(f32[512,2048]{1,0:T(8,128)} %fusion.3) | copy-start | bytes 12582916
  296.2 7.5 %copy-start.8 = (s32[2,128]{1,0:T(2,128)S(1)}, s32[2,128]{1,0:T(2,128)}, u32[]{:S(2)}) copy-start(s32[2,128]{1,0:T(2,128)} %param.14) | copy-start | bytes 3076
  296.2 10.3 %copy-start.2 = (f32[512,512]{1,0:T(8,128)S(1)}, f32[512,512]{1,0:T(8,128)}, u32[]{:S(2)}) copy-start(f32[512,512]{1,0:T(8,128)} %param.12) | copy-start | bytes 3145732
  296.2 284.4 %all-to-all-start = ((f32[128,2,128,128]{3,2,1,0:T(8,128)}), f32[128,2,128,128]{3,2,1,0:T(8,128)}, u32[]{:S(2)}, u32[]{:S(2)}) async-start(f32[128,2,128,128]{3,2,1,0:T(8,128)} %bitcast.235), calls=%async_computation | async-start | bytes 33554432 | tf_op jit(solution)/shard_map/all_to_all | solution.py:169
  306.9 108.8 %slice-start = ((s8[6291456]{0:T(1024)(128)(4,1)}), s8[2097152]{0:T(1024)(128)(4,1)S(1)}, s32[]{:S(2)}) async-start(s8[6291456]{0:T(1024)(128)(4,1)} %bitcast.244), calls=%async_computation.3 | async-start | bytes 4194304
  332.1 0.8 copy-start.1
  408.8 6.9 %slice-start.1 = ((s8[6291456]{0:T(1024)(128)(4,1)}), s8[4194304]{0:T(1024)(128)(4,1)S(1)}, s32[]{:S(2)}) async-start(s8[6291456]{0:T(1024)(128)(4,1)} %bitcast.244), calls=%async_computation.4 | async-start | bytes 8388608
  409.3 17.6 %copy-start.4 = (f32[256,256]{1,0:T(8,128)}, f32[256,256]{1,0:T(8,128)S(1)}, u32[]{:S(2)}) copy-start(f32[256,256]{1,0:T(8,128)S(1)} %select_maximum_fusion.7) | copy-start | bytes 786436
  439.0 7.8 %copy-start.6 = (f32[512,128]{1,0:T(8,128)S(1)}, f32[512,128]{1,0:T(8,128)}, u32[]{:S(2)}) copy-start(f32[512,128]{1,0:T(8,128)} %get-tuple-element.55) | copy-start | bytes 786436
  439.0 7.8 %copy-start.7 = (f32[128,128]{1,0:T(8,128)S(1)}, f32[128,128]{1,0:T(8,128)}, u32[]{:S(2)}) copy-start(f32[128,128]{1,0:T(8,128)} %get-tuple-element.32) | copy-start | bytes 196612
  439.0 8.9 %copy-start.3 = (f32[24,1,1,1,8,512]{5,4,3,2,1,0:T(8,128)S(1)}, f32[24,1,1,1,8,512]{5,4,3,2,1,0:T(8,128)}, u32[]{:S(2)}) copy-start(f32[24,1,1,1,8,512]{5,4,3,2,1,0:T(8,128)} %param.13) | copy-start | bytes 1179652
  439.0 8.9 %copy-start.5 = (f32[256,256]{1,0:T(8,128)S(1)}, f32[256,256]{1,0:T(8,128)}, u32[]{:S(2)}) copy-start(f32[256,256]{1,0:T(8,128)} %copy-done.4) | copy-start | bytes 786436
Sparse Core Ops, SparseCore 0:
  22.4 225.9 all-gather.3
  250.1 41.0 all-gather.5
